TPU v7x, 512 devices: a whole 4x8x8 slice. The times are simulated.
512 devices in a mesh: tiles: 128 (over z, y, core), rep: 4 (over x).
Axes of the slice: x: 4, y: 8, z: 8, core: 2. Of those that a mesh axis runs over, the one named last changes fastest.
Arguments:
- tile_data: float32 [1536, 64, 4096], P(('tiles', 'rep')), may hold values from -64 to 64
- tile_coords: int32 [1536, 3], P(('tiles', 'rep')), may hold values from 0 to 127, as said below
- tile_count: int32 [512], P(('tiles', 'rep')), may hold values from 1 to 3, 1024 in all
- weights: int32 [1536], P(('tiles', 'rep')), may hold values from 1 to 4
- owner_map: int32 [128], replicated, may hold values from 0 to 127, as said below
- factor_b: bfloat16 [8192, 256], P(('tiles', 'rep'))
- factor_c: bfloat16 [1024, 256], replicated
Outputs:
- updated: float32 [8192, 256], P(('tiles', 'rep'))
Inputs may be any that keep to these rules, and one draw needn't show every extreme that they name: `tile_coords`: columns 0 and 1 name row blocks below 128, column 2 a block below 16. Every slot of device d = t * 4 + e has owner_map[i_s] = t. Among the 3 slots of one device the positions owner_map[j_s] all differ. `owner_map`: A permutation of the 128 row blocks.
All inputs are finite; a program needn't handle non-finite values. No bound on the sum of `tile_count` on one device may be relied on, other than what follows from the above.
Results may differ from a plain program's by a relative error of at most 0.0095.
Values may be sent and summed in bfloat16 or wider, within the bound.
No kernel may reach another device: no remote copies, remote signals or barrier semaphores. Data moves between devices by JAX's collectives and lax.ppermute only.
A program may use at most 128 MiB of HBM per device.

v0:
```python
import jax
import jax.numpy as jnp
from jax import lax
from jax.sharding import PartitionSpec as P


def per_device(tile_data, tile_coords, tile_count, weights, owner_map, factor_b, factor_c):
    slot_total = tile_data.shape[0]
    tile_edge = tile_data.shape[1]
    rank_cols = factor_b.shape[1]
    is_live = jnp.arange(slot_total, dtype=jnp.int32) < tile_count[0]
    slot_scale = weights.astype(jnp.float32) * is_live.astype(jnp.float32)
    stored_second = jnp.take(owner_map, tile_coords[:, 1])
    block_offsets = jnp.arange(tile_edge, dtype=jnp.int32)
    initial = jnp.zeros((slot_total, tile_edge, rank_cols), jnp.bfloat16)
    owned = lax.all_gather(factor_b, "rep", axis=0, tiled=True)
    row_piece = lax.all_gather(owned, "tiles", axis=0, tiled=True)
    piece_rows = row_piece.shape[0]
    wanted = stored_second[:, None] * tile_edge + block_offsets[None, :]
    inside = (wanted >= 0) & (wanted < piece_rows)
    taken = jnp.take(row_piece, jnp.clip(wanted, 0, piece_rows - 1), axis=0)
    blocks = jnp.where(inside[:, :, None], taken, initial)
    summed = jnp.zeros((tile_edge, rank_cols), jnp.float32)
    for position in range(slot_total):
        c_block = lax.dynamic_slice_in_dim(
            factor_c, tile_coords[position, 2] * tile_edge, tile_edge, 0
        ).astype(jnp.float32)
        flat_tile = tile_data[position].reshape(tile_edge * tile_edge, tile_edge)
        inner_sum = jnp.dot(flat_tile, c_block, precision=lax.Precision.HIGHEST)
        inner_sum = inner_sum.reshape(tile_edge, tile_edge, rank_cols)
        partial_value = jnp.einsum("ijr,jr->ir", inner_sum, blocks[position].astype(jnp.float32))
        rounded = (partial_value * slot_scale[position]).astype(jnp.bfloat16)
        summed = summed + rounded.astype(jnp.float32)
    my_rows = lax.psum_scatter(summed, "rep", scatter_dimension=0, tiled=True)
    own_gram = jnp.dot(factor_b.T, factor_b, preferred_element_type=jnp.float32)
    gram_b = lax.psum(own_gram, ("tiles", "rep"))
    gram_c = jnp.dot(factor_c.T, factor_c, preferred_element_type=jnp.float32)
    normal_matrix = gram_b * gram_c
    lower_factor = jnp.linalg.cholesky(normal_matrix)
    return jax.scipy.linalg.cho_solve((lower_factor, True), my_rows.T).T


def solution(mesh):
    in_specs = (
        P(("tiles", "rep"), None, None),
        P(("tiles", "rep"), None),
        P(("tiles", "rep")),
        P(("tiles", "rep")),
        P(),
        P(("tiles", "rep"), None),
        P(),
    )
    out_specs = P(("tiles", "rep"), None)
    return jax.shard_map(
        per_device, mesh=mesh, in_specs=in_specs, out_specs=out_specs, check_vma=False
    )
```

profile of v0, /device:TPU:1, one launch (start us, length us, event | category | flops | bytes accessed | tf_op | source)
XLA Modules:
  0.0 374.4 jit_solution(15148988416922388078)
XLA Ops:
  7.4 1.7 fusion.28
  9.1 11.9 %all_gather.6 = bf16[64,256]{1,0:T(8,128)(2,1)} all-gather(bf16[16,256]{1,0:T(8,128)(2,1)} %param.12), channel_id=1, replica_groups=mesh['tiles'=128,'rep'=4] {'rep'}, dimensions={0}, use_global_device_ids=true | all-gather | bytes 40960 | tf_op jit(solution)/shard_map/all_gather | solution.py:16
  21.9 1.5 fusion.26
  25.5 1.3 gather_fusion
  26.9 3.7 fusion.25
  30.7 2.0 reshape_squeeze.9
  32.7 3.9 %convolution_bitcast_fusion.2 = f32[4096,256]{0,1:T(8,128)} fusion(f32[4096,64]{1,0:T(8,128)S(1)} %reshape_squeeze.9, bf16[1024,256]{1,0:T(8,128)(2,1)S(1)} %copy-done, s32[]{:T(128)S(6)} %select_n.56), kind=kOutput, calls=%fused_computation.6 | convolution fusion | flops 805306368 | bytes 6324228 | tf_op jit(solution)/shard_map/dot_general | solution.py:29
  36.6 5.6 %copy.50 = f32[4096,256]{1,0:T(8,128)} copy(f32[4096,256]{0,1:T(8,128)} %convolution_bitcast_fusion.2) | data formatting | bytes 8388608
  42.2 2.0 reshape_squeeze.11
  44.2 3.9 %convolution_bitcast_fusion = f32[4096,256]{0,1:T(8,128)} fusion(f32[4096,64]{1,0:T(8,128)S(1)} %reshape_squeeze.11, bf16[1024,256]{1,0:T(8,128)(2,1)S(1)} %copy-done, s32[]{:T(128)S(6)} %select_n.58), kind=kOutput, calls=%fused_computation.4 | convolution fusion | flops 805306368 | bytes 6324228 | tf_op jit(solution)/shard_map/dot_general | solution.py:29
  48.1 5.6 %copy.52 = f32[4096,256]{1,0:T(8,128)} copy(f32[4096,256]{0,1:T(8,128)} %convolution_bitcast_fusion) | data formatting | bytes 8388608
  53.8 2.0 reshape_squeeze.10
  55.8 3.9 %convolution_bitcast_fusion.1 = f32[4096,256]{0,1:T(8,128)} fusion(f32[4096,64]{1,0:T(8,128)S(1)} %reshape_squeeze.10, bf16[1024,256]{1,0:T(8,128)(2,1)S(1)} %copy-done, s32[]{:T(128)S(6)} %select_n.57), kind=kOutput, calls=%fused_computation.5 | convolution fusion | flops 805306368 | bytes 6324228 | tf_op jit(solution)/shard_map/dot_general | solution.py:29
  59.6 5.7 %copy.51 = f32[4096,256]{1,0:T(8,128)} copy(f32[4096,256]{0,1:T(8,128)} %convolution_bitcast_fusion.1) | data formatting | bytes 8388608
  66.8 221.5 %all-reduce.3.cloned.1.call-done = f32[256,256]{0,1:T(8,128)} async-done(((f32[256,256]{0,1:T(8,128)}), f32[256,256]{0,1:T(8,128)}) %all-reduce.3.cloned.1.call-update) | async-done | bytes 262160 | tf_op jit(solution)/shard_map/psum | solution.py:36
  289.7 11.7 %cholesky.50 = f32[128,128]{1,0:T(8,128)S(1)} custom-call(f32[128,128]{1,0:T(8,128)S(1)} %cholesky.118), custom_call_target="Cholesky" | custom-call | tf_op jit(solution)/shard_map/jit(cholesky)/cholesky | solution.py:39
  301.5 9.8 %custom-call.18 = f32[1,128,128]{1,2,0:T(8,128)S(1)} custom-call(f32[1,128,128]{2,1,0:T(8,128)S(1)} %get-tuple-element.32), custom_call_target="InvertDiagBlocksLowerTriangular" | custom-call | tf_op jit(solution)/shard_map/jit(cholesky)/cholesky | solution.py:39
  311.8 11.7 %cholesky.105 = f32[128,128]{1,0:T(8,128)S(1)} custom-call(f32[128,128]{1,0:T(8,128)S(1)} %convolution_subtract_fusion), custom_call_target="Cholesky" | custom-call | tf_op jit(solution)/shard_map/jit(cholesky)/cholesky | solution.py:39
  325.6 3.6 gather_fusion.1
  329.3 3.0 multiply_reduce_fusion.2
  332.5 4.9 %multiply_reduce_fusion = (f32[256,64]{0,1:T(8,128)S(1)}, f32[256,64]{0,1:T(8,128)S(1)}) fusion(f32[256,64]{0,1:T(8,128)S(1)} %get-tuple-element.26, f32[4096,256]{1,0:T(8,128)} %copy.52, f32[4096,256]{1,0:T(8,128)} %copy.51, f32[256,64]{0,1:T(8,128)S(1)} %get-tuple-element.27), kind=kLoop, calls=%fused_computation.7 | loop fusion | flops 4161536 | bytes 8650752
  337.6 1.9 add_bitcast_fusion
  340.3 3.8 %while.1 = (s32[]{:T(128)}, f32[256,256]{1,0:T(8,128)S(1)}, s32[2,2]{1,0:T(2,128)S(1)}, f32[2,128,128]{2,1,0:T(8,128)S(1)}, s32[]{:T(128)}) while((s32[]{:T(128)}, f32[256,256]{1,0:T(8,128)S(1)}, s32[2,2]{1,0:T(2,128)S(1)}, f32[2,128,128]{2,1,0:T(8,128)S(1)}, s32[]{:T(128)}) %tuple.33), condition=%wide.while_cond, body=%wide.while_body.sunk | while | flops 2 | bytes 131189 | solution.py:40
  344.1 19.7 %custom-call.19 = f32[2,128,128]{1,2,0:T(8,128)S(1)} custom-call(f32[2,128,128]{2,1,0:T(8,128)S(1)} %get-tuple-element.12), custom_call_target="InvertDiagBlocksLowerTriangular" | custom-call | tf_op jit(solution)/shard_map/jit(_cho_solve)/triangular_solve | solution.py:40
  (56 shorter events, 12.8 us)
Async XLA Ops:
  7.4 25.3 %copy-start = (bf16[1024,256]{1,0:T(8,128)(2,1)S(1)}, bf16[1024,256]{1,0:T(8,128)(2,1)}, u32[]{:S(2)}) copy-start(bf16[1024,256]{1,0:T(8,128)(2,1)} %param.13) | copy-start | bytes 1572868
  7.4 280.9 %all-reduce.3.cloned.1.call-start = ((), (), s32[]{:S(2)}) async-start(), calls=%async_computation.1 | async-start | bytes 524288 | tf_op jit(solution)/shard_map/psum | solution.py:36
  9.1 316.5 %all-gather.2.cloned.1.call-start = ((), (), s32[]{:S(2)}) async-start(), calls=%async_computation.2 | async-start | bytes 4227072 | tf_op jit(solution)/shard_map/all_gather | solution.py:17
  21.1 342.7 %reduce-scatter.4.cloned.1.call-start = ((), (), s32[]{:S(2)}) async-start(), calls=%async_computation.3 | async-start | bytes 81920 | tf_op jit(solution)/shard_map/reduce_scatter | solution.py:34
  59.6 6.4 %copy-start.1 = (s32[3]{0:T(128)S(1)}, s32[3]{0:T(128)}, u32[]{:S(2)}) copy-start(s32[3]{0:T(128)} %param.10) | copy-start | bytes 40
Sparse Core Ops, SparseCore 0:
  13.2 275.0 all-reduce.2
Sparse Core Ops, SparseCore 1:
  21.1 91.5 all-gather.1
  340.3 19.7 reduce-scatter.3
where the time goes:
time: 375 us; the launch traced here: 374 us
  waiting for transfers between devices  222 us (59%)
  other arithmetic  64.6 us (17%)
  local copies, waits for them, and re-layouts  39.5 us (11%)
  between operations  19 us (5%)
  matrix products  17.7 us (5%)
  blocking collectives  11.9 us (3%)
    psum x1, waiting for transfers between devices, per_device(): gram_b = lax.psum(own_gram, ('tiles', 'rep'))  221 us
    another operation x6, other arithmetic, per_device(): lower_factor = jnp.linalg.cholesky(normal_matrix)  34 us
    another operation x3, other arithmetic, per_device(): return jax.scipy.linalg.cho_solve((lower_factor, True), my_rows.T).T  19.7 us
    unnamed x9, local copies, waits for them, and re-layouts  17.7 us
    all_gather x1, blocking collectives, per_device(): owned = lax.all_gather(factor_b, 'rep', axis=0, tiled=True)  11.9 us
    dot_general x3, matrix products, per_device(): inner_sum = jnp.dot(flat_tile, c_block, precision=lax.Precision.HIGHEST)  11.7 us
    unnamed x4, other arithmetic  7.99 us
  transfers between devices with their start and end apart: 3, of which 1 were waited for; matrix products, arithmetic and copies ran while one was open for 27% of the time, Pallas kernels for 0%

commit v1 on v0

v1 whole, which is shorter than its diff:
```python
import jax
import jax.numpy as jnp
from jax import lax
from jax.sharding import PartitionSpec as P


def per_device(tile_data, tile_coords, tile_count, weights, owner_map, factor_b, factor_c):
    slot_total = tile_data.shape[0]
    tile_edge = tile_data.shape[1]
    rank_cols = factor_b.shape[1]
    is_live = jnp.arange(slot_total, dtype=jnp.int32) < tile_count[0]
    slot_scale = weights.astype(jnp.float32) * is_live.astype(jnp.float32)
    stored_second = jnp.take(owner_map, tile_coords[:, 1])
    owned = lax.all_gather(factor_b, "rep", axis=0, tiled=True)
    whole_b = lax.all_gather(owned, "tiles", axis=0, tiled=True)
    summed = jnp.zeros((tile_edge, rank_cols), jnp.float32)
    for position in range(slot_total):
        c_block = lax.dynamic_slice_in_dim(
            factor_c, tile_coords[position, 2] * tile_edge, tile_edge, 0
        ).astype(jnp.float32)
        b_block = lax.dynamic_slice_in_dim(
            whole_b, stored_second[position] * tile_edge, tile_edge, 0
        ).astype(jnp.float32)
        flat_tile = tile_data[position].reshape(tile_edge * tile_edge, tile_edge)
        inner_sum = jnp.dot(flat_tile, c_block, precision=lax.Precision.HIGHEST)
        inner_sum = inner_sum.reshape(tile_edge, tile_edge, rank_cols)
        partial_value = jnp.einsum("ijr,jr->ir", inner_sum, b_block)
        rounded = (partial_value * slot_scale[position]).astype(jnp.bfloat16)
        summed = summed + rounded.astype(jnp.float32)
    my_rows = lax.psum_scatter(summed, "rep", scatter_dimension=0, tiled=True)
    gram_b = jnp.dot(whole_b.T, whole_b, preferred_element_type=jnp.float32)
    gram_c = jnp.dot(factor_c.T, factor_c, preferred_element_type=jnp.float32)
    normal_matrix = gram_b * gram_c
    lower_factor = jnp.linalg.cholesky(normal_matrix)
    return jax.scipy.linalg.cho_solve((lower_factor, True), my_rows.T).T


def solution(mesh):
    in_specs = (
        P(("tiles", "rep"), None, None),
        P(("tiles", "rep"), None),
        P(("tiles", "rep")),
        P(("tiles", "rep")),
        P(),
        P(("tiles", "rep"), None),
        P(),
    )
    out_specs = P(("tiles", "rep"), None)
    return jax.shard_map(
        per_device, mesh=mesh, in_specs=in_specs, out_specs=out_specs, check_vma=False
    )
```

time: 375 us -> 198 us (0.53)
  waiting for transfers between devices: 222 us -> 42.6 us
  local copies, waits for them, and re-layouts: 39.5 us -> 35.6 us
    psum x1 -> x0, waiting for transfers between devices: 221 us -> none  [per_device(): gram_b = lax.psum(own_gram, ('tiles', 'rep'))]
    all_gather x1, waiting for transfers between devices: 0.03 us -> 42.6 us  [per_device(): whole_b = lax.all_gather(owned, 'tiles', axis=0, tiled=True)]
    unnamed x9 -> x8, local copies, waits for them, and re-layouts: 17.7 us -> 17.6 us
  transfers between devices with their start and end apart: 3 -> 2, of which waited for: 1 -> 1; matrix products, arithmetic and copies ran while one was open for 27% -> 35% of each run, Pallas kernels for 0% -> 0%
where the time goes in v1:
time: 198 us; the launch traced here: 197 us
  other arithmetic  66.7 us (34%)
  waiting for transfers between devices  42.6 us (22%)
  local copies, waits for them, and re-layouts  35.6 us (18%)
  matrix products  20.2 us (10%)
  between operations  19.4 us (10%)
  blocking collectives  12 us (6%)
    all_gather x1, waiting for transfers between devices, per_device(): whole_b = lax.all_gather(owned, 'tiles', axis=0, tiled=True)  42.6 us
    another operation x6, other arithmetic, per_device(): lower_factor = jnp.linalg.cholesky(normal_matrix)  34.1 us
    another operation x3, other arithmetic, per_device(): return jax.scipy.linalg.cho_solve((lower_factor, True), my_rows.T).T  19.7 us
    unnamed x8, local copies, waits for them, and re-layouts  17.6 us
    all_gather x1, blocking collectives, per_device(): owned = lax.all_gather(factor_b, 'rep', axis=0, tiled=True)  12 us
    dot_general x3, matrix products, per_device(): inner_sum = jnp.dot(flat_tile, c_block, precision=lax.Precision.HIGHEST)  11.7 us
    unnamed x4, other arithmetic  8.57 us
    another operation x3, local copies, waits for them, and re-layouts, per_device(): flat_tile = tile_data[position].reshape(tile_edge * tile_edge, tile_edge)  5.99 us
  transfers between devices with their start and end apart: 2, of which 1 were waited for; matrix products, arithmetic and copies ran while one was open for 35% of the time, Pallas kernels for 0%

profile of v1, /device:TPU:1, one launch (start us, length us, event | category | flops | bytes accessed | tf_op | source)
XLA Modules:
  0.0 196.7 jit_solution(10054851824223870427)
XLA Ops:
  6.5 12.0 %all_gather.6 = bf16[64,256]{1,0:T(8,128)(2,1)} all-gather(bf16[16,256]{1,0:T(8,128)(2,1)} %param.12), channel_id=1, replica_groups=mesh['tiles'=128,'rep'=4] {'rep'}, dimensions={0}, use_global_device_ids=true | all-gather | bytes 40960 | tf_op jit(solution)/shard_map/all_gather | solution.py:14
  19.5 1.3 gather_fusion
  24.3 1.5 fusion.20
  27.8 3.7 %fusion.19 = (f32[1,64,4096]{2,1,0:T(8,128)}, f32[1,64,4096]{2,1,0:T(8,128)}, f32[1,64,4096]{2,1,0:T(8,128)}) fusion(f32[3,64,4096]{2,1,0:T(8,128)} %param.7), kind=kLoop, calls=%fused_computation.60 | loop fusion | bytes 6291456 | tf_op jit(solution)/shard_map/slice | solution.py:24
  31.5 2.0 %reshape_squeeze.9 = f32[4096,64]{1,0:T(8,128)S(1)} reshape(f32[1,64,4096]{2,1,0:T(8,128)} %get-tuple-element.27) | data formatting | bytes 2097152 | tf_op jit(solution)/shard_map/reshape;squeeze | solution.py:24
  33.5 3.9 %convolution_bitcast_fusion.2 = f32[4096,256]{0,1:T(8,128)} fusion(f32[4096,64]{1,0:T(8,128)S(1)} %reshape_squeeze.9, bf16[1024,256]{1,0:T(8,128)(2,1)S(1)} %copy-done, s32[]{:T(128)S(6)} %select_n.37), kind=kOutput, calls=%fused_computation.5 | convolution fusion | flops 805306368 | bytes 6324228 | tf_op jit(solution)/shard_map/dot_general | solution.py:25
  37.4 5.6 %copy.47 = f32[4096,256]{1,0:T(8,128)} copy(f32[4096,256]{0,1:T(8,128)} %convolution_bitcast_fusion.2) | data formatting | bytes 8388608
  43.1 2.0 %reshape_squeeze.11 = f32[4096,64]{1,0:T(8,128)S(1)} reshape(f32[1,64,4096]{2,1,0:T(8,128)} %get-tuple-element.26) | data formatting | bytes 2097152 | tf_op jit(solution)/shard_map/reshape;squeeze | solution.py:24
  45.1 3.9 %convolution_bitcast_fusion = f32[4096,256]{0,1:T(8,128)} fusion(f32[4096,64]{1,0:T(8,128)S(1)} %reshape_squeeze.11, bf16[1024,256]{1,0:T(8,128)(2,1)S(1)} %copy-done, s32[]{:T(128)S(6)} %select_n.41), kind=kOutput, calls=%fused_computation.3 | convolution fusion | flops 805306368 | bytes 6324228 | tf_op jit(solution)/shard_map/dot_general | solution.py:25
  49.0 5.6 %copy.49 = f32[4096,256]{1,0:T(8,128)} copy(f32[4096,256]{0,1:T(8,128)} %convolution_bitcast_fusion) | data formatting | bytes 8388608
  54.6 2.0 %reshape_squeeze.10 = f32[4096,64]{1,0:T(8,128)S(1)} reshape(f32[1,64,4096]{2,1,0:T(8,128)} %get-tuple-element.28) | data formatting | bytes 2097152 | tf_op jit(solution)/shard_map/reshape;squeeze | solution.py:24
  56.6 3.9 %convolution_bitcast_fusion.1 = f32[4096,256]{0,1:T(8,128)} fusion(f32[4096,64]{1,0:T(8,128)S(1)} %reshape_squeeze.10, bf16[1024,256]{1,0:T(8,128)(2,1)S(1)} %copy-done, s32[]{:T(128)S(6)} %select_n.39), kind=kOutput, calls=%fused_computation.4 | convolution fusion | flops 805306368 | bytes 6324228 | tf_op jit(solution)/shard_map/dot_general | solution.py:25
  60.5 5.7 %copy.48 = f32[4096,256]{1,0:T(8,128)} copy(f32[4096,256]{0,1:T(8,128)} %convolution_bitcast_fusion.1) | data formatting | bytes 8388608
  67.5 42.6 %all-gather.2.cloned.1.call-done = bf16[8192,256]{1,0:T(8,128)(2,1)} async-done(((bf16[64,256]{1,0:T(8,128)(2,1)}), bf16[8192,256]{1,0:T(8,128)(2,1)}) %all-gather.2.cloned.1.call-update) | async-done | bytes 4194320 | tf_op jit(solution)/shard_map/all_gather | solution.py:15
  110.0 5.2 %fusion.23 = f32[256,256]{0,1:T(8,128)S(1)} fusion(bf16[8192,256]{1,0:T(8,128)(2,1)} %all-gather.2.cloned.1.call-done), kind=kOutput, calls=%fused_computation.64 | convolution fusion | flops 1073741824 | bytes 4456448 | tf_op jit(solution)/shard_map/dot_general | solution.py:31
  115.8 11.7 %cholesky.50 = f32[128,128]{1,0:T(8,128)S(1)} custom-call(f32[128,128]{1,0:T(8,128)S(1)} %cholesky.118), custom_call_target="Cholesky" | custom-call | tf_op jit(solution)/shard_map/jit(cholesky)/cholesky | solution.py:34
  127.6 9.8 %custom-call.18 = f32[1,128,128]{1,2,0:T(8,128)S(1)} custom-call(f32[1,128,128]{2,1,0:T(8,128)S(1)} %get-tuple-element.32), custom_call_target="InvertDiagBlocksLowerTriangular" | custom-call | tf_op jit(solution)/shard_map/jit(cholesky)/cholesky | solution.py:34
  137.9 11.8 %cholesky.105 = f32[128,128]{1,0:T(8,128)S(1)} custom-call(f32[128,128]{1,0:T(8,128)S(1)} %convolution_subtract_fusion), custom_call_target="Cholesky" | custom-call | tf_op jit(solution)/shard_map/jit(cholesky)/cholesky | solution.py:34
  150.5 2.8 %multiply_reduce_fusion.2 = f32[256,64]{0,1:T(8,128)S(1)} fusion(f32[256,64]{0,1:T(8,128)S(1)} %get-tuple-element.25, f32[4096,256]{1,0:T(8,128)} %copy.47), kind=kLoop, calls=%fused_computation.8 | loop fusion | flops 2080768 | bytes 4325376
  153.5 4.9 %multiply_reduce_fusion = (f32[256,64]{0,1:T(8,128)S(1)}, f32[256,64]{0,1:T(8,128)S(1)}) fusion(f32[256,64]{0,1:T(8,128)S(1)} %get-tuple-element.23, f32[4096,256]{1,0:T(8,128)} %copy.49, f32[4096,256]{1,0:T(8,128)} %copy.48, f32[256,64]{0,1:T(8,128)S(1)} %get-tuple-element.24), kind=kLoop, calls=%fused_computation.6 | loop fusion | flops 4161536 | bytes 8650752
  158.6 1.9 add_bitcast_fusion
  163.2 3.8 %while.1 = (s32[]{:T(128)}, f32[256,256]{1,0:T(8,128)S(1)}, s32[2,2]{1,0:T(2,128)S(1)}, f32[2,128,128]{2,1,0:T(8,128)S(1)}, s32[]{:T(128)}) while((s32[]{:T(128)}, f32[256,256]{1,0:T(8,128)S(1)}, s32[2,2]{1,0:T(2,128)S(1)}, f32[2,128,128]{2,1,0:T(8,128)S(1)}, s32[]{:T(128)}) %tuple.34), condition=%wide.while_cond, body=%wide.while_body.sunk | while | flops 2 | bytes 131189 | solution.py:35
  165.7 1.3 bitcast_dynamic-update-slice_fusion.2
  167.0 19.7 %custom-call.19 = f32[2,128,128]{1,2,0:T(8,128)S(1)} custom-call(f32[2,128,128]{2,1,0:T(8,128)S(1)} %get-tuple-element.12), custom_call_target="InvertDiagBlocksLowerTriangular" | custom-call | tf_op jit(solution)/shard_map/jit(_cho_solve)/triangular_solve | solution.py:35
  (47 shorter events, 12.5 us)
Async XLA Ops:
  6.5 27.0 %copy-start = (bf16[1024,256]{1,0:T(8,128)(2,1)S(1)}, bf16[1024,256]{1,0:T(8,128)(2,1)}, u32[]{:S(2)}) copy-start(bf16[1024,256]{1,0:T(8,128)(2,1)} %param.13) | copy-start | bytes 1572868
  6.5 103.5 %all-gather.2.cloned.1.call-start = ((), (), s32[]{:S(2)}) async-start(), calls=%async_computation.1 | async-start | bytes 4227072 | tf_op jit(solution)/shard_map/all_gather | solution.py:15
  18.6 168.1 %reduce-scatter.4.cloned.1.call-start = ((), (), s32[]{:S(2)}) async-start(), calls=%async_computation.2 | async-start | bytes 81920 | tf_op jit(solution)/shard_map/reduce_scatter | solution.py:30
  60.5 6.3 %copy-start.1 = (s32[3]{0:T(128)S(1)}, s32[3]{0:T(128)}, u32[]{:S(2)}) copy-start(s32[3]{0:T(128)} %param.10) | copy-start | bytes 40
Sparse Core Ops, SparseCore 0:
  18.7 91.2 all-gather.1
  161.3 19.9 reduce-scatter.3

commit v2 on v1

--- a/solution.py
+++ b/solution.py
@@ -27,12 +27,20 @@
         partial_value = jnp.einsum("ijr,jr->ir", inner_sum, b_block)
         rounded = (partial_value * slot_scale[position]).astype(jnp.bfloat16)
         summed = summed + rounded.astype(jnp.float32)
+    summed, whole_b = lax.optimization_barrier((summed, whole_b))
     my_rows = lax.psum_scatter(summed, "rep", scatter_dimension=0, tiled=True)
     gram_b = jnp.dot(whole_b.T, whole_b, preferred_element_type=jnp.float32)
     gram_c = jnp.dot(factor_c.T, factor_c, preferred_element_type=jnp.float32)
     normal_matrix = gram_b * gram_c
     lower_factor = jnp.linalg.cholesky(normal_matrix)
-    return jax.scipy.linalg.cho_solve((lower_factor, True), my_rows.T).T
+    identity = jnp.eye(rank_cols, dtype=jnp.float32)
+    lower_inverse = lax.linalg.triangular_solve(
+        lower_factor, identity, left_side=True, lower=True
+    )
+    normal_inverse = jnp.dot(
+        lower_inverse.T, lower_inverse, precision=lax.Precision.HIGHEST
+    )
+    return jnp.dot(my_rows, normal_inverse, precision=lax.Precision.HIGHEST)
 
 
 def solution(mesh):

time: 198 us -> 199 us (level)
    dot_general x0 -> x2, matrix products: none -> 2.15 us  [the longest x1 1.55 us: per_device(): return jnp.dot(my_rows, normal_inverse, precision=lax.Precision.HIGHEST)]
    another operation x6 -> x7, other arithmetic: 34.1 us -> 34.9 us  [per_device(): lower_factor = jnp.linalg.cholesky(normal_matrix)]
  transfers between devices with their start and end apart: 2 -> 2, of which waited for: 1 -> 1; matrix products, arithmetic and copies ran while one was open for 35% -> 56% of each run, Pallas kernels for 0% -> 0%
where the time goes in v2:
time: 199 us; the launch traced here: 198 us
  other arithmetic  66.9 us (34%)
  waiting for transfers between devices  42.7 us (21%)
  local copies, waits for them, and re-layouts  35.9 us (18%)
  matrix products  20.7 us (10%)
  between operations  19.6 us (10%)
  blocking collectives  12 us (6%)
    all_gather x1, waiting for transfers between devices, per_device(): whole_b = lax.all_gather(owned, 'tiles', axis=0, tiled=True)  42.6 us
    another operation x7, other arithmetic, per_device(): lower_factor = jnp.linalg.cholesky(normal_matrix)  34.9 us
    another operation x3, other arithmetic, per_device(): lax.linalg.triangular_solve(lower_factor, identity, left_side=True, lower...  19.7 us
    unnamed x8, local copies, waits for them, and re-layouts  17.6 us
    all_gather x1, blocking collectives, per_device(): owned = lax.all_gather(factor_b, 'rep', axis=0, tiled=True)  12 us
    dot_general x3, matrix products, per_device(): inner_sum = jnp.dot(flat_tile, c_block, precision=lax.Precision.HIGHEST)  11.7 us
    unnamed x4, other arithmetic  8.56 us
    another operation x3, local copies, waits for them, and re-layouts, per_device(): flat_tile = tile_data[position].reshape(tile_edge * tile_edge, tile_edge)  5.99 us
  transfers between devices with their start and end apart: 2, of which 1 were waited for; matrix products, arithmetic and copies ran while one was open for 56% of the time, Pallas kernels for 0%

profile of v2, /device:TPU:1, one launch (start us, length us, event | category | flops | bytes accessed | tf_op | source)
XLA Modules:
  0.0 197.8 jit_solution(16335417801402918147)
XLA Ops:
  6.5 12.0 %all_gather.6 = bf16[64,256]{1,0:T(8,128)(2,1)} all-gather(bf16[16,256]{1,0:T(8,128)(2,1)} %param.12), channel_id=1, replica_groups=mesh['tiles'=128,'rep'=4] {'rep'}, dimensions={0}, use_global_device_ids=true | all-gather | bytes 40960 | tf_op jit(solution)/shard_map/all_gather | solution.py:14
  24.2 1.5 fusion.22
  27.7 3.7 %fusion.21 = (f32[1,64,4096]{2,1,0:T(8,128)}, f32[1,64,4096]{2,1,0:T(8,128)}, f32[1,64,4096]{2,1,0:T(8,128)}) fusion(f32[3,64,4096]{2,1,0:T(8,128)} %param.7), kind=kLoop, calls=%fused_computation.61 | loop fusion | bytes 6291456 | tf_op jit(solution)/shard_map/slice | solution.py:24
  31.4 2.0 %reshape_squeeze.9 = f32[4096,64]{1,0:T(8,128)S(1)} reshape(f32[1,64,4096]{2,1,0:T(8,128)} %get-tuple-element.31) | data formatting | bytes 2097152 | tf_op jit(solution)/shard_map/reshape;squeeze | solution.py:24
  33.4 3.9 %convolution_bitcast_fusion.2 = f32[4096,256]{0,1:T(8,128)} fusion(f32[4096,64]{1,0:T(8,128)S(1)} %reshape_squeeze.9, bf16[1024,256]{1,0:T(8,128)(2,1)S(1)} %copy-done, s32[]{:T(128)S(6)} %select_n.36), kind=kOutput, calls=%fused_computation.5 | convolution fusion | flops 805306368 | bytes 6324228 | tf_op jit(solution)/shard_map/dot_general | solution.py:25
  37.3 5.6 %copy.46 = f32[4096,256]{1,0:T(8,128)} copy(f32[4096,256]{0,1:T(8,128)} %convolution_bitcast_fusion.2) | data formatting | bytes 8388608
  43.0 2.0 %reshape_squeeze.11 = f32[4096,64]{1,0:T(8,128)S(1)} reshape(f32[1,64,4096]{2,1,0:T(8,128)} %get-tuple-element.30) | data formatting | bytes 2097152 | tf_op jit(solution)/shard_map/reshape;squeeze | solution.py:24
  45.0 3.9 %convolution_bitcast_fusion = f32[4096,256]{0,1:T(8,128)} fusion(f32[4096,64]{1,0:T(8,128)S(1)} %reshape_squeeze.11, bf16[1024,256]{1,0:T(8,128)(2,1)S(1)} %copy-done, s32[]{:T(128)S(6)} %select_n.40), kind=kOutput, calls=%fused_computation.3 | convolution fusion | flops 805306368 | bytes 6324228 | tf_op jit(solution)/shard_map/dot_general | solution.py:25
  48.9 5.6 %copy.48 = f32[4096,256]{1,0:T(8,128)} copy(f32[4096,256]{0,1:T(8,128)} %convolution_bitcast_fusion) | data formatting | bytes 8388608
  54.5 2.0 %reshape_squeeze.10 = f32[4096,64]{1,0:T(8,128)S(1)} reshape(f32[1,64,4096]{2,1,0:T(8,128)} %get-tuple-element.32) | data formatting | bytes 2097152 | tf_op jit(solution)/shard_map/reshape;squeeze | solution.py:24
  56.5 3.9 %convolution_bitcast_fusion.1 = f32[4096,256]{0,1:T(8,128)} fusion(f32[4096,64]{1,0:T(8,128)S(1)} %reshape_squeeze.10, bf16[1024,256]{1,0:T(8,128)(2,1)S(1)} %copy-done, s32[]{:T(128)S(6)} %select_n.38), kind=kOutput, calls=%fused_computation.4 | convolution fusion | flops 805306368 | bytes 6324228 | tf_op jit(solution)/shard_map/dot_general | solution.py:25
  60.3 5.7 %copy.47 = f32[4096,256]{1,0:T(8,128)} copy(f32[4096,256]{0,1:T(8,128)} %convolution_bitcast_fusion.1) | data formatting | bytes 8388608
  67.4 42.6 %all-gather.2.cloned.1.call-done = bf16[8192,256]{1,0:T(8,128)(2,1)} async-done(((bf16[64,256]{1,0:T(8,128)(2,1)}), bf16[8192,256]{1,0:T(8,128)(2,1)}) %all-gather.2.cloned.1.call-update) | async-done | bytes 4194320 | tf_op jit(solution)/shard_map/all_gather | solution.py:15
  110.8 2.8 %multiply_reduce_fusion.2 = f32[256,64]{0,1:T(8,128)S(1)} fusion(f32[256,64]{0,1:T(8,128)S(1)} %get-tuple-element.29, f32[4096,256]{1,0:T(8,128)} %copy.46), kind=kLoop, calls=%fused_computation.8 | loop fusion | flops 2080768 | bytes 4325376
  113.8 4.9 %multiply_reduce_fusion = (f32[256,64]{0,1:T(8,128)S(1)}, f32[256,64]{0,1:T(8,128)S(1)}) fusion(f32[256,64]{0,1:T(8,128)S(1)} %get-tuple-element.27, f32[4096,256]{1,0:T(8,128)} %copy.48, f32[4096,256]{1,0:T(8,128)} %copy.47, f32[256,64]{0,1:T(8,128)S(1)} %get-tuple-element.28), kind=kLoop, calls=%fused_computation.6 | loop fusion | flops 4161536 | bytes 8650752
  118.9 1.9 add_bitcast_fusion
  121.6 5.2 %fusion.25 = f32[256,256]{0,1:T(8,128)S(1)} fusion(bf16[8192,256]{1,0:T(8,128)(2,1)} %all-gather.2.cloned.1.call-done), kind=kOutput, calls=%fused_computation.65 | convolution fusion | flops 1073741824 | bytes 4456448 | tf_op jit(solution)/shard_map/dot_general | solution.py:32
  127.3 11.7 %cholesky.50 = f32[128,128]{1,0:T(8,128)S(1)} custom-call(f32[128,128]{1,0:T(8,128)S(1)} %cholesky.118), custom_call_target="Cholesky" | custom-call | tf_op jit(solution)/shard_map/jit(cholesky)/cholesky | solution.py:35
  139.1 9.8 %custom-call.14 = f32[1,128,128]{1,2,0:T(8,128)S(1)} custom-call(f32[1,128,128]{2,1,0:T(8,128)S(1)} %get-tuple-element.36), custom_call_target="InvertDiagBlocksLowerTriangular" | custom-call | tf_op jit(solution)/shard_map/jit(cholesky)/cholesky | solution.py:35
  149.4 11.9 %cholesky.105 = f32[128,128]{1,0:T(8,128)S(1)} custom-call(f32[128,128]{1,0:T(8,128)S(1)} %convolution_subtract_fusion.1), custom_call_target="Cholesky" | custom-call | tf_op jit(solution)/shard_map/jit(cholesky)/cholesky | solution.py:35
  164.2 4.1 %while.1 = (s32[]{:T(128)}, f32[256,256]{1,0:T(8,128)S(1)}, s32[2,2]{1,0:T(2,128)S(1)}, f32[2,128,128]{2,1,0:T(8,128)S(1)}, s32[]{:T(128)}) while((s32[]{:T(128)}, f32[256,256]{1,0:T(8,128)S(1)}, s32[2,2]{1,0:T(2,128)S(1)}, f32[2,128,128]{2,1,0:T(8,128)S(1)}, s32[]{:T(128)}) %tuple.35), condition=%wide.while_cond, body=%wide.while_body.sunk | while | flops 2 | bytes 131189 | solution.py:37
  164.8 1.4 bitcast_dynamic-update-slice_fusion.2
  168.3 19.7 %custom-call.15 = f32[2,128,128]{1,2,0:T(8,128)S(1)} custom-call(f32[2,128,128]{2,1,0:T(8,128)S(1)} %get-tuple-element.16), custom_call_target="InvertDiagBlocksLowerTriangular" | custom-call | tf_op jit(solution)/shard_map/triangular_solve | solution.py:37
  189.4 1.6 fusion.26
  (47 shorter events, 12.9 us)
Async XLA Ops:
  6.5 26.9 %copy-start = (bf16[1024,256]{1,0:T(8,128)(2,1)S(1)}, bf16[1024,256]{1,0:T(8,128)(2,1)}, u32[]{:S(2)}) copy-start(bf16[1024,256]{1,0:T(8,128)(2,1)} %param.13) | copy-start | bytes 1572868
  6.5 103.5 %all-gather.2.cloned.1.call-start = ((), (), s32[]{:S(2)}) async-start(), calls=%async_computation.1 | async-start | bytes 4227072 | tf_op jit(solution)/shard_map/all_gather | solution.py:15
  18.6 170.9 %reduce-scatter.4.cloned.1.call-start = ((), (), s32[]{:S(2)}) async-start(), calls=%async_computation.2 | async-start | bytes 81920
  60.3 6.3 %copy-start.1 = (s32[3]{0:T(128)S(1)}, s32[3]{0:T(128)}, u32[]{:S(2)}) copy-start(s32[3]{0:T(128)} %param.10) | copy-start | bytes 40
Sparse Core Ops, SparseCore 0:
  18.7 91.2 all-gather.1
  121.7 19.9 reduce-scatter.3

commit v3 on v1

--- a/solution.py
+++ b/solution.py
@@ -27,12 +27,49 @@
         partial_value = jnp.einsum("ijr,jr->ir", inner_sum, b_block)
         rounded = (partial_value * slot_scale[position]).astype(jnp.bfloat16)
         summed = summed + rounded.astype(jnp.float32)
+    summed, whole_b = lax.optimization_barrier((summed, whole_b))
     my_rows = lax.psum_scatter(summed, "rep", scatter_dimension=0, tiled=True)
     gram_b = jnp.dot(whole_b.T, whole_b, preferred_element_type=jnp.float32)
     gram_c = jnp.dot(factor_c.T, factor_c, preferred_element_type=jnp.float32)
     normal_matrix = gram_b * gram_c
-    lower_factor = jnp.linalg.cholesky(normal_matrix)
-    return jax.scipy.linalg.cho_solve((lower_factor, True), my_rows.T).T
+    normal_inverse = spd_inverse(normal_matrix)
+    return jnp.dot(my_rows, normal_inverse, precision=lax.Precision.HIGHEST)
+
+
+def mm(left, right):
+    return jnp.dot(left, right, precision=lax.Precision.HIGHEST)
+
+
+def lower_inverse(lower):
+    size = lower.shape[0]
+    diagonal = jnp.diagonal(lower)
+    identity = jnp.eye(size, dtype=lower.dtype)
+    strict = identity - lower / diagonal[:, None]
+    product = identity + strict
+    power = strict
+    reach = 2
+    while reach < size:
+        power = mm(power, power)
+        product = product + mm(product, power)
+        reach *= 2
+    return product / diagonal[None, :]
+
+
+def spd_inverse(matrix):
+    half = matrix.shape[0] // 2
+    top = matrix[:half, :half]
+    side = matrix[half:, :half]
+    bottom = matrix[half:, half:]
+    top_inverse = lower_inverse(lax.linalg.cholesky(top))
+    side_factor = mm(side, top_inverse.T)
+    schur = bottom - mm(side_factor, side_factor.T)
+    bottom_inverse = lower_inverse(lax.linalg.cholesky(schur))
+    corner = -mm(bottom_inverse, mm(side_factor, top_inverse))
+    zeros = jnp.zeros((half, matrix.shape[0] - half), matrix.dtype)
+    inverse = jnp.concatenate(
+        [jnp.concatenate([top_inverse, zeros], 1), jnp.concatenate([corner, bottom_inverse], 1)], 0
+    )
+    return mm(inverse.T, inverse)
 
 
 def solution(mesh):

time: 198 us -> 191 us (0.965)
  other arithmetic: 66.7 us -> 38.4 us
  waiting for transfers between devices: 42.6 us -> 60 us
  matrix products: 20.2 us -> 25.4 us
    another operation x9 -> x6, other arithmetic: 53.8 us -> 24.8 us  [the longest x3 12.4 us: spd_inverse(): top_inverse = lower_inverse(lax.linalg.cholesky(top))]
    unnamed x2 -> x3, waiting for transfers between devices: 0.03 us -> 17.4 us
    dot_general x0 -> x30, matrix products: none -> 8.17 us  [the longest x29 6.62 us: mm(): return jnp.dot(left, right, precision=lax.Precision.HIGHEST)]
    another operation x9 -> x0, local copies, waits for them, and re-layouts: 3.83 us -> none
    another operation x8 -> x0, matrix products: 3 us -> none  [the longest x6 2.53 us: per_device(): return jax.scipy.linalg.cho_solve((lower_factor, True), my_rows.T).T]
    gather x0 -> x2, local copies, waits for them, and re-layouts: none -> 2.71 us  [lower_inverse(): diagonal = jnp.diagonal(lower)]
    unnamed x4 -> x3, other arithmetic: 8.57 us -> 8.56 us
  transfers between devices with their start and end apart: 2 -> 2, of which waited for: 1 -> 2; matrix products, arithmetic and copies ran while one was open for 35% -> 25% of each run, Pallas kernels for 0% -> 0%
where the time goes in v3:
time: 191 us; the launch traced here: 189 us
  waiting for transfers between devices  60 us (31%)
  other arithmetic  38.4 us (20%)
  local copies, waits for them, and re-layouts  34.6 us (18%)
  matrix products  25.4 us (13%)
  between operations  18.4 us (10%)
  blocking collectives  12 us (6%)
    all_gather x1, waiting for transfers between devices, per_device(): whole_b = lax.all_gather(owned, 'tiles', axis=0, tiled=True)  42.7 us
    unnamed x8, local copies, waits for them, and re-layouts  17.6 us
    unnamed x3, waiting for transfers between devices  17.4 us
    another operation x3, other arithmetic, spd_inverse(): top_inverse = lower_inverse(lax.linalg.cholesky(top))  12.4 us
    another operation x3, other arithmetic, spd_inverse(): bottom_inverse = lower_inverse(lax.linalg.cholesky(schur))  12.4 us
    all_gather x1, blocking collectives, per_device(): owned = lax.all_gather(factor_b, 'rep', axis=0, tiled=True)  12 us
    dot_general x3, matrix products, per_device(): inner_sum = jnp.dot(flat_tile, c_block, precision=lax.Precision.HIGHEST)  11.7 us
    unnamed x3, other arithmetic  8.56 us
  transfers between devices with their start and end apart: 2, of which 2 were waited for; matrix products, arithmetic and copies ran while one was open for 25% of the time, Pallas kernels for 0%

profile of v3, /device:TPU:1, one launch (start us, length us, event | category | flops | bytes accessed | tf_op | source)
XLA Modules:
  0.0 188.9 jit_solution(7040868909790658833)
XLA Ops:
  6.5 12.0 %all_gather.6 = bf16[64,256]{1,0:T(8,128)(2,1)} all-gather(bf16[16,256]{1,0:T(8,128)(2,1)} %param.13), channel_id=1, replica_groups=mesh['tiles'=128,'rep'=4] {'rep'}, dimensions={0}, use_global_device_ids=true | all-gather | bytes 40960 | tf_op jit(solution)/shard_map/all_gather | solution.py:14
  19.5 1.3 gather_fusion
  24.2 1.5 fusion.25
  27.7 3.7 %fusion.24 = (f32[1,64,4096]{2,1,0:T(8,128)}, f32[1,64,4096]{2,1,0:T(8,128)}, f32[1,64,4096]{2,1,0:T(8,128)}) fusion(f32[3,64,4096]{2,1,0:T(8,128)} %param.8), kind=kLoop, calls=%fused_computation.78 | loop fusion | bytes 6291456 | tf_op jit(solution)/shard_map/slice | solution.py:24
  31.4 2.0 %reshape_squeeze.9 = f32[4096,64]{1,0:T(8,128)S(1)} reshape(f32[1,64,4096]{2,1,0:T(8,128)} %get-tuple-element.14) | data formatting | bytes 2097152 | tf_op jit(solution)/shard_map/reshape;squeeze | solution.py:24
  33.4 3.9 %convolution_bitcast_fusion.2 = f32[4096,256]{0,1:T(8,128)} fusion(f32[4096,64]{1,0:T(8,128)S(1)} %reshape_squeeze.9, bf16[1024,256]{1,0:T(8,128)(2,1)S(1)} %copy-done, s32[]{:T(128)S(6)} %select_n.44), kind=kOutput, calls=%fused_computation.5 | convolution fusion | flops 805306368 | bytes 6324228 | tf_op jit(solution)/shard_map/dot_general | solution.py:25
  37.3 5.6 %copy.82 = f32[4096,256]{1,0:T(8,128)} copy(f32[4096,256]{0,1:T(8,128)} %convolution_bitcast_fusion.2) | data formatting | bytes 8388608
  42.9 2.0 %reshape_squeeze.11 = f32[4096,64]{1,0:T(8,128)S(1)} reshape(f32[1,64,4096]{2,1,0:T(8,128)} %get-tuple-element.13) | data formatting | bytes 2097152 | tf_op jit(solution)/shard_map/reshape;squeeze | solution.py:24
  45.0 3.9 %convolution_bitcast_fusion = f32[4096,256]{0,1:T(8,128)} fusion(f32[4096,64]{1,0:T(8,128)S(1)} %reshape_squeeze.11, bf16[1024,256]{1,0:T(8,128)(2,1)S(1)} %copy-done, s32[]{:T(128)S(6)} %select_n.48), kind=kOutput, calls=%fused_computation.3 | convolution fusion | flops 805306368 | bytes 6324228 | tf_op jit(solution)/shard_map/dot_general | solution.py:25
  48.9 5.6 %copy.84 = f32[4096,256]{1,0:T(8,128)} copy(f32[4096,256]{0,1:T(8,128)} %convolution_bitcast_fusion) | data formatting | bytes 8388608
  54.5 2.0 %reshape_squeeze.10 = f32[4096,64]{1,0:T(8,128)S(1)} reshape(f32[1,64,4096]{2,1,0:T(8,128)} %get-tuple-element.15) | data formatting | bytes 2097152 | tf_op jit(solution)/shard_map/reshape;squeeze | solution.py:24
  56.5 3.9 %convolution_bitcast_fusion.1 = f32[4096,256]{0,1:T(8,128)} fusion(f32[4096,64]{1,0:T(8,128)S(1)} %reshape_squeeze.10, bf16[1024,256]{1,0:T(8,128)(2,1)S(1)} %copy-done, s32[]{:T(128)S(6)} %select_n.46), kind=kOutput, calls=%fused_computation.4 | convolution fusion | flops 805306368 | bytes 6324228 | tf_op jit(solution)/shard_map/dot_general | solution.py:25
  60.3 5.7 %copy.83 = f32[4096,256]{1,0:T(8,128)} copy(f32[4096,256]{0,1:T(8,128)} %convolution_bitcast_fusion.1) | data formatting | bytes 8388608
  67.4 42.7 %all-gather.2.cloned.1.call-done = bf16[8192,256]{1,0:T(8,128)(2,1)} async-done(((bf16[64,256]{1,0:T(8,128)(2,1)}), bf16[8192,256]{1,0:T(8,128)(2,1)}) %all-gather.2.cloned.1.call-update) | async-done | bytes 4194320 | tf_op jit(solution)/shard_map/all_gather | solution.py:15
  110.8 2.8 %multiply_reduce_fusion.2 = f32[256,64]{0,1:T(8,128)S(1)} fusion(f32[256,64]{0,1:T(8,128)S(1)} %get-tuple-element.12, f32[4096,256]{1,0:T(8,128)} %copy.82), kind=kLoop, calls=%fused_computation.8 | loop fusion | flops 2080768 | bytes 4325376
  113.8 4.9 %multiply_reduce_fusion = (f32[256,64]{0,1:T(8,128)S(1)}, f32[256,64]{0,1:T(8,128)S(1)}) fusion(f32[256,64]{0,1:T(8,128)S(1)} %get-tuple-element.10, f32[4096,256]{1,0:T(8,128)} %copy.84, f32[4096,256]{1,0:T(8,128)} %copy.83, f32[256,64]{0,1:T(8,128)S(1)} %get-tuple-element.11), kind=kLoop, calls=%fused_computation.6 | loop fusion | flops 4161536 | bytes 8650752
  118.9 1.9 %add_bitcast_fusion = f32[64,256]{0,1:T(8,128)S(1)} fusion(f32[256,64]{1,0:T(8,128)S(1)} %copy.57, f32[256,64]{1,0:T(8,128)S(1)} %copy.64, f32[256,64]{1,0:T(8,128)S(1)} %copy.71, f32[]{:T(128)} %bitcast.27, f32[]{:T(128)} %bitcast.20, f32[]{:T(128)} %bitcast.13), kind=kLoop, calls=%fused_computation.39 | loop fusion | flops 180224 | bytes 262156 | tf_op jit(solution)/shard_map/add | solution.py:29
  120.8 5.2 %fusion.28 = f32[256,256]{0,1:T(8,128)S(1)} fusion(bf16[8192,256]{1,0:T(8,128)(2,1)} %all-gather.2.cloned.1.call-done), kind=kOutput, calls=%fused_computation.82 | convolution fusion | flops 1073741824 | bytes 4456448 | tf_op jit(solution)/shard_map/dot_general | solution.py:32
  126.5 11.7 %custom-call.8 = f32[128,128]{1,0:T(8,128)S(1)} custom-call(f32[128,128]{1,0:T(8,128)S(1)} %fusion.11), custom_call_target="Cholesky" | custom-call | tf_op jit(solution)/shard_map/cholesky/custom-call.1 | solution.py:63
  139.6 1.5 gather_fusion.1
  144.5 11.7 %custom-call.9 = f32[128,128]{1,0:T(8,128)S(1)} custom-call(f32[128,128]{1,0:T(8,128)S(1)} %broadcast_multiply_fusion), custom_call_target="Cholesky" | custom-call | tf_op jit(solution)/shard_map/cholesky/custom-call.1 | solution.py:66
  157.6 1.2 gather_fusion.2
  163.2 17.3 %reduce-scatter.4.cloned.1.call-done = f32[16,256]{1,0:T(8,128)} async-done(((f32[64,256]{1,0:T(8,128)}), f32[16,256]{1,0:T(8,128)}) %reduce-scatter.4.cloned.1.call-update) | async-done | bytes 16400
  180.5 1.6 fusion.40
  (64 shorter events, 14.9 us)
Async XLA Ops:
  6.5 26.9 %copy-start = (bf16[1024,256]{1,0:T(8,128)(2,1)S(1)}, bf16[1024,256]{1,0:T(8,128)(2,1)}, u32[]{:S(2)}) copy-start(bf16[1024,256]{1,0:T(8,128)(2,1)} %param.14) | copy-start | bytes 1572868
  6.5 103.5 %all-gather.2.cloned.1.call-start = ((), (), s32[]{:S(2)}) async-start(), calls=%async_computation.1 | async-start | bytes 4227072 | tf_op jit(solution)/shard_map/all_gather | solution.py:15
  18.6 161.9 %reduce-scatter.4.cloned.1.call-start = ((), (), s32[]{:S(2)}) async-start(), calls=%async_computation.2 | async-start | bytes 81920
  60.3 6.3 %copy-start.1 = (s32[3]{0:T(128)S(1)}, s32[3]{0:T(128)}, u32[]{:S(2)}) copy-start(s32[3]{0:T(128)} %param.11) | copy-start | bytes 40
Sparse Core Ops, SparseCore 0:
  18.7 91.2 all-gather.1
  160.7 19.7 reduce-scatter.3

commit v4 on v3

--- a/solution.py
+++ b/solution.py
@@ -11,7 +11,14 @@
     is_live = jnp.arange(slot_total, dtype=jnp.int32) < tile_count[0]
     slot_scale = weights.astype(jnp.float32) * is_live.astype(jnp.float32)
     stored_second = jnp.take(owner_map, tile_coords[:, 1])
-    owned = lax.all_gather(factor_b, "rep", axis=0, tiled=True)
+    replicas = lax.psum(1, "rep")
+    mine = lax.axis_index("rep")
+    by_shift = [factor_b] + [
+        lax.ppermute(factor_b, "rep", [(e, (e + k) % replicas) for e in range(replicas)])
+        for k in range(1, replicas)
+    ]
+    order = (mine - jnp.arange(replicas)) % replicas
+    owned = jnp.take(jnp.stack(by_shift), order, axis=0).reshape(-1, rank_cols)
     whole_b = lax.all_gather(owned, "tiles", axis=0, tiled=True)
     summed = jnp.zeros((tile_edge, rank_cols), jnp.float32)
     for position in range(slot_total):
@@ -28,11 +35,17 @@
         rounded = (partial_value * slot_scale[position]).astype(jnp.bfloat16)
         summed = summed + rounded.astype(jnp.float32)
     summed, whole_b = lax.optimization_barrier((summed, whole_b))
-    my_rows = lax.psum_scatter(summed, "rep", scatter_dimension=0, tiled=True)
+    share = tile_edge // replicas
+    my_rows = lax.dynamic_slice_in_dim(summed, mine * share, share, 0)
+    for k in range(1, replicas):
+        outgoing = lax.dynamic_slice_in_dim(summed, ((mine + k) % replicas) * share, share, 0)
+        my_rows = my_rows + lax.ppermute(
+            outgoing, "rep", [(e, (e + k) % replicas) for e in range(replicas)]
+        )
     gram_b = jnp.dot(whole_b.T, whole_b, preferred_element_type=jnp.float32)
     gram_c = jnp.dot(factor_c.T, factor_c, preferred_element_type=jnp.float32)
     normal_matrix = gram_b * gram_c
-    normal_inverse = spd_inverse(normal_matrix)
+    normal_inverse, my_rows = spd_inverse(normal_matrix, my_rows)
     return jnp.dot(my_rows, normal_inverse, precision=lax.Precision.HIGHEST)
 
 
@@ -55,7 +68,7 @@
     return product / diagonal[None, :]
 
 
-def spd_inverse(matrix):
+def spd_inverse(matrix, carried):
     half = matrix.shape[0] // 2
     top = matrix[:half, :half]
     side = matrix[half:, :half]
@@ -63,13 +76,14 @@
     top_inverse = lower_inverse(lax.linalg.cholesky(top))
     side_factor = mm(side, top_inverse.T)
     schur = bottom - mm(side_factor, side_factor.T)
+    schur, carried = lax.optimization_barrier((schur, carried))
     bottom_inverse = lower_inverse(lax.linalg.cholesky(schur))
     corner = -mm(bottom_inverse, mm(side_factor, top_inverse))
     zeros = jnp.zeros((half, matrix.shape[0] - half), matrix.dtype)
     inverse = jnp.concatenate(
         [jnp.concatenate([top_inverse, zeros], 1), jnp.concatenate([corner, bottom_inverse], 1)], 0
     )
-    return mm(inverse.T, inverse)
+    return mm(inverse.T, inverse), carried
 
 
 def solution(mesh):

time: 191 us -> 189 us (0.990)
  starting transfers between devices: 0.04 us -> 19.8 us
  blocking collectives: 12 us -> 0 us
  waiting for transfers between devices: 60 us -> 50.2 us
    ppermute x0 -> x6, starting transfers between devices: none -> 19.8 us  [the longest x3 10.3 us: per_device(): lax.ppermute(factor_b, 'rep', [(e, (e + k) % replicas) for e in range(rep...]
    unnamed x3 -> x1, waiting for transfers between devices: 17.4 us -> 0.02 us
    all_gather x1 -> x0, blocking collectives: 12 us -> none  [per_device(): owned = lax.all_gather(factor_b, 'rep', axis=0, tiled=True)]
    ppermute x0 -> x6, waiting for transfers between devices: none -> 8.84 us  [the longest x3 5.76 us: per_device(): lax.ppermute(outgoing, 'rep', [(e, (e + k) % replicas) for e in range(rep...]
    unnamed x8 -> x7, local copies, waits for them, and re-layouts: 17.6 us -> 16.9 us
  transfers between devices with their start and end apart: 2 -> 7, of which waited for: 2 -> 5; matrix products, arithmetic and copies ran while one was open for 25% -> 24% of each run, Pallas kernels for 0% -> 0%
where the time goes in v4:
time: 189 us; the launch traced here: 188 us
  waiting for transfers between devices  50.2 us (27%)
  other arithmetic  39.9 us (21%)
  local copies, waits for them, and re-layouts  34.5 us (18%)
  matrix products  24.8 us (13%)
  starting transfers between devices  19.8 us (10%)
  between operations  18.6 us (10%)
    all_gather x1, waiting for transfers between devices, per_device(): whole_b = lax.all_gather(owned, 'tiles', axis=0, tiled=True)  41.4 us
    unnamed x7, local copies, waits for them, and re-layouts  16.9 us
    another operation x3, other arithmetic, spd_inverse(): top_inverse = lower_inverse(lax.linalg.cholesky(top))  12.4 us
    another operation x3, other arithmetic, spd_inverse(): bottom_inverse = lower_inverse(lax.linalg.cholesky(schur))  12.4 us
    dot_general x3, matrix products, per_device(): inner_sum = jnp.dot(flat_tile, c_block, precision=lax.Precision.HIGHEST)  11.7 us
    ppermute x3, starting transfers between devices, per_device(): lax.ppermute(factor_b, 'rep', [(e, (e + k) % replicas) for e in range(rep...  10.3 us
    ppermute x3, starting transfers between devices, per_device(): lax.ppermute(outgoing, 'rep', [(e, (e + k) % replicas) for e in range(rep...  9.5 us
    unnamed x3, other arithmetic  8.56 us
  transfers between devices with their start and end apart: 7, of which 5 were waited for; matrix products, arithmetic and copies ran while one was open for 24% of the time, Pallas kernels for 0%

profile of v4, /device:TPU:1, one launch (start us, length us, event | category | flops | bytes accessed | tf_op | source)
XLA Modules:
  0.0 187.8 jit_solution(11314126703124636446)
XLA Ops:
  6.5 5.3 %collective-permute-start.2 = (bf16[16,256]{1,0:T(8,128)(2,1)}, bf16[16,256]{1,0:T(8,128)(2,1)S(1)}, u32[]{:S(2)}, u32[]{:S(2)}) collective-permute-start(bf16[16,256]{1,0:T(8,128)(2,1)} %param.13), channel_id=1, source_target_pairs={{0,3},{1,0},{2,1},{3,2},{4,7},{5,4},{6,5},{7,6},{8,11},{9,8},{10,9... | collective-permute-start | bytes 24584 | tf_op jit(solution)/shard_map/ppermute | solution.py:17
  11.9 2.4 %collective-permute-start.1 = (bf16[16,256]{1,0:T(8,128)(2,1)}, bf16[16,256]{1,0:T(8,128)(2,1)S(1)}, u32[]{:S(2)}, u32[]{:S(2)}) collective-permute-start(bf16[16,256]{1,0:T(8,128)(2,1)} %param.13), channel_id=1, source_target_pairs={{0,2},{1,3},{2,0},{3,1},{4,6},{5,7},{6,4},{7,5},{8,10},{9,11},{10,... | collective-permute-start | bytes 24584 | tf_op jit(solution)/shard_map/ppermute | solution.py:17
  14.3 2.5 %collective-permute-start = (bf16[16,256]{1,0:T(8,128)(2,1)}, bf16[16,256]{1,0:T(8,128)(2,1)S(1)}, u32[]{:S(2)}, u32[]{:S(2)}) collective-permute-start(bf16[16,256]{1,0:T(8,128)(2,1)} %param.13), channel_id=1, source_target_pairs={{0,1},{1,2},{2,3},{3,0},{4,5},{5,6},{6,7},{7,4},{8,9},{9,10},{10,1... | collective-permute-start | bytes 24584 | tf_op jit(solution)/shard_map/ppermute | solution.py:17
  18.0 2.1 %collective-permute-done = bf16[16,256]{1,0:T(8,128)(2,1)S(1)} collective-permute-done((bf16[16,256]{1,0:T(8,128)(2,1)}, bf16[16,256]{1,0:T(8,128)(2,1)S(1)}, u32[]{:S(2)}, u32[]{:S(2)}) %collective-permute-start) | collective-permute-done | bytes 8224 | tf_op jit(solution)/shard_map/ppermute | solution.py:17
  31.2 3.7 %fusion.27 = (f32[1,64,4096]{2,1,0:T(8,128)}, f32[1,64,4096]{2,1,0:T(8,128)}, f32[1,64,4096]{2,1,0:T(8,128)}) fusion(f32[3,64,4096]{2,1,0:T(8,128)} %param.8), kind=kLoop, calls=%fused_computation.98 | loop fusion | bytes 6291456 | tf_op jit(solution)/shard_map/slice | solution.py:31
  34.9 2.0 %reshape_squeeze.9 = f32[4096,64]{1,0:T(8,128)S(1)} reshape(f32[1,64,4096]{2,1,0:T(8,128)} %get-tuple-element.18) | data formatting | bytes 2097152 | tf_op jit(solution)/shard_map/reshape;squeeze | solution.py:31
  36.9 3.9 %convolution_bitcast_fusion.2 = f32[4096,256]{0,1:T(8,128)} fusion(f32[4096,64]{1,0:T(8,128)S(1)} %reshape_squeeze.9, bf16[1024,256]{1,0:T(8,128)(2,1)S(1)} %copy-done, s32[]{:T(128)S(6)} %select_n.114), kind=kOutput, calls=%fused_computation.6 | convolution fusion | flops 805306368 | bytes 6324228 | tf_op jit(solution)/shard_map/dot_general | solution.py:32
  40.8 5.6 %copy.65 = f32[4096,256]{1,0:T(8,128)} copy(f32[4096,256]{0,1:T(8,128)} %convolution_bitcast_fusion.2) | data formatting | bytes 8388608
  46.5 2.0 %reshape_squeeze.11 = f32[4096,64]{1,0:T(8,128)S(1)} reshape(f32[1,64,4096]{2,1,0:T(8,128)} %get-tuple-element.17) | data formatting | bytes 2097152 | tf_op jit(solution)/shard_map/reshape;squeeze | solution.py:31
  48.5 3.9 %convolution_bitcast_fusion = f32[4096,256]{0,1:T(8,128)} fusion(f32[4096,64]{1,0:T(8,128)S(1)} %reshape_squeeze.11, bf16[1024,256]{1,0:T(8,128)(2,1)S(1)} %copy-done, s32[]{:T(128)S(6)} %select_n.118), kind=kOutput, calls=%fused_computation.4 | convolution fusion | flops 805306368 | bytes 6324228 | tf_op jit(solution)/shard_map/dot_general | solution.py:32
  52.4 5.6 %copy.67 = f32[4096,256]{1,0:T(8,128)} copy(f32[4096,256]{0,1:T(8,128)} %convolution_bitcast_fusion) | data formatting | bytes 8388608
  60.0 3.9 %convolution_bitcast_fusion.1 = f32[4096,256]{0,1:T(8,128)} fusion(f32[4096,64]{1,0:T(8,128)S(1)} %reshape_squeeze.10, bf16[1024,256]{1,0:T(8,128)(2,1)S(1)} %copy-done, s32[]{:T(128)S(6)} %select_n.116), kind=kOutput, calls=%fused_computation.5 | convolution fusion | flops 805306368 | bytes 6324228 | tf_op jit(solution)/shard_map/dot_general | solution.py:32
  63.9 5.6 %copy.66 = f32[4096,256]{1,0:T(8,128)} copy(f32[4096,256]{0,1:T(8,128)} %convolution_bitcast_fusion.1) | data formatting | bytes 8388608
  70.9 41.4 %all-gather.2.cloned.1.call-done = bf16[8192,256]{1,0:T(8,128)(2,1)} async-done(((bf16[64,256]{1,0:T(8,128)(2,1)}), bf16[8192,256]{1,0:T(8,128)(2,1)}) %all-gather.2.cloned.1.call-update) | async-done | bytes 4194320 | tf_op jit(solution)/shard_map/all_gather | solution.py:22
  113.1 2.8 %multiply_reduce_fusion.2 = f32[256,64]{0,1:T(8,128)S(1)} fusion(f32[256,64]{0,1:T(8,128)S(1)} %get-tuple-element.16, f32[4096,256]{1,0:T(8,128)} %copy.65), kind=kLoop, calls=%fused_computation.9 | loop fusion | flops 2080768 | bytes 4325376
  116.0 4.9 %multiply_reduce_fusion = (f32[256,64]{0,1:T(8,128)S(1)}, f32[256,64]{0,1:T(8,128)S(1)}) fusion(f32[256,64]{0,1:T(8,128)S(1)} %get-tuple-element.14, f32[4096,256]{1,0:T(8,128)} %copy.67, f32[4096,256]{1,0:T(8,128)} %copy.66, f32[256,64]{0,1:T(8,128)S(1)} %get-tuple-element.15), kind=kLoop, calls=%fused_computation.7 | loop fusion | flops 4161536 | bytes 8650752
  123.1 5.2 %fusion.31 = f32[256,256]{0,1:T(8,128)S(1)} fusion(bf16[8192,256]{1,0:T(8,128)(2,1)} %all-gather.2.cloned.1.call-done), kind=kOutput, calls=%fused_computation.102 | convolution fusion | flops 1073741824 | bytes 4456448 | tf_op jit(solution)/shard_map/dot_general | solution.py:45
  128.7 11.7 %custom-call.8 = f32[128,128]{1,0:T(8,128)S(1)} custom-call(f32[128,128]{1,0:T(8,128)S(1)} %fusion.11), custom_call_target="Cholesky" | custom-call | tf_op jit(solution)/shard_map/cholesky/custom-call.1 | solution.py:76
  146.5 4.3 %collective-permute-start.5 = (f32[16,256]{0,1:T(8,128)S(1)}, f32[16,256]{0,1:T(8,128)S(1)}, u32[]{:S(2)}, u32[]{:S(2)}) collective-permute-start(f32[16,256]{0,1:T(8,128)S(1)} %get-tuple-element.21), channel_id=1, source_target_pairs={{0,3},{1,0},{2,1},{3,2},{4,7},{5,4},{6,5},{7,6},{8,11},{9,8},{10,9... | collective-permute-start | bytes 49160 | tf_op jit(solution)/shard_map/ppermute | solution.py:42
  150.8 2.5 %collective-permute-start.4 = (f32[16,256]{0,1:T(8,128)S(1)}, f32[16,256]{0,1:T(8,128)S(1)}, u32[]{:S(2)}, u32[]{:S(2)}) collective-permute-start(f32[16,256]{0,1:T(8,128)S(1)} %get-tuple-element.22), channel_id=1, source_target_pairs={{0,2},{1,3},{2,0},{3,1},{4,6},{5,7},{6,4},{7,5},{8,10},{9,11},{10,... | collective-permute-start | bytes 49160 | tf_op jit(solution)/shard_map/ppermute | solution.py:42
  153.3 2.7 %collective-permute-start.3 = (f32[16,256]{0,1:T(8,128)S(1)}, f32[16,256]{0,1:T(8,128)S(1)}, u32[]{:S(2)}, u32[]{:S(2)}) collective-permute-start(f32[16,256]{0,1:T(8,128)S(1)} %get-tuple-element.20), channel_id=1, source_target_pairs={{0,1},{1,2},{2,3},{3,0},{4,5},{5,6},{6,7},{7,4},{8,9},{9,10},{10,1... | collective-permute-start | bytes 49160 | tf_op jit(solution)/shard_map/ppermute | solution.py:42
  156.2 2.5 %collective-permute-done.4 = f32[16,256]{0,1:T(8,128)S(1)} collective-permute-done((f32[16,256]{0,1:T(8,128)S(1)}, f32[16,256]{0,1:T(8,128)S(1)}, u32[]{:S(2)}, u32[]{:S(2)}) %collective-permute-start.4) | collective-permute-done | bytes 16416 | tf_op jit(solution)/shard_map/ppermute | solution.py:42
  158.7 3.3 %collective-permute-done.3 = f32[16,256]{0,1:T(8,128)S(1)} collective-permute-done((f32[16,256]{0,1:T(8,128)S(1)}, f32[16,256]{0,1:T(8,128)S(1)}, u32[]{:S(2)}, u32[]{:S(2)}) %collective-permute-start.3) | collective-permute-done | bytes 16416 | tf_op jit(solution)/shard_map/ppermute | solution.py:42
  162.3 11.7 %custom-call.9 = f32[128,128]{1,0:T(8,128)S(1)} custom-call(f32[128,128]{1,0:T(8,128)S(1)} %broadcast_multiply_fusion), custom_call_target="Cholesky" | custom-call | tf_op jit(solution)/shard_map/cholesky/custom-call.1 | solution.py:80
  (81 shorter events, 27.6 us)
Async XLA Ops:
  6.5 30.4 %copy-start = (bf16[1024,256]{1,0:T(8,128)(2,1)S(1)}, bf16[1024,256]{1,0:T(8,128)(2,1)}, u32[]{:S(2)}) copy-start(bf16[1024,256]{1,0:T(8,128)(2,1)} %param.14) | copy-start | bytes 1572868
  6.5 105.7 %all-gather.2.cloned.1.call-start = ((), (), s32[]{:S(2)}) async-start(), calls=%async_computation | async-start | bytes 4227072 | tf_op jit(solution)/shard_map/all_gather | solution.py:22
  6.5 10.5 %collective-permute-start.2 = (bf16[16,256]{1,0:T(8,128)(2,1)}, bf16[16,256]{1,0:T(8,128)(2,1)S(1)}, u32[]{:S(2)}, u32[]{:S(2)}) collective-permute-start(bf16[16,256]{1,0:T(8,128)(2,1)} %param.13), channel_id=1, source_target_pairs={{0,3},{1,0},{2,1},{3,2},{4,7},{5,4},{6,5},{7,6},{8,11},{9,8},{10,9... | collective-permute-start | bytes 24584 | tf_op jit(solution)/shard_map/ppermute | solution.py:17
  11.9 6.1 %collective-permute-start.1 = (bf16[16,256]{1,0:T(8,128)(2,1)}, bf16[16,256]{1,0:T(8,128)(2,1)S(1)}, u32[]{:S(2)}, u32[]{:S(2)}) collective-permute-start(bf16[16,256]{1,0:T(8,128)(2,1)} %param.13), channel_id=1, source_target_pairs={{0,2},{1,3},{2,0},{3,1},{4,6},{5,7},{6,4},{7,5},{8,10},{9,11},{10,... | collective-permute-start | bytes 24584 | tf_op jit(solution)/shard_map/ppermute | solution.py:17
  14.3 5.8 %collective-permute-start = (bf16[16,256]{1,0:T(8,128)(2,1)}, bf16[16,256]{1,0:T(8,128)(2,1)S(1)}, u32[]{:S(2)}, u32[]{:S(2)}) collective-permute-start(bf16[16,256]{1,0:T(8,128)(2,1)} %param.13), channel_id=1, source_target_pairs={{0,1},{1,2},{2,3},{3,0},{4,5},{5,6},{6,7},{7,4},{8,9},{9,10},{10,1... | collective-permute-start | bytes 24584 | tf_op jit(solution)/shard_map/ppermute | solution.py:17
  63.9 6.4 %copy-start.1 = (s32[3]{0:T(128)S(1)}, s32[3]{0:T(128)}, u32[]{:S(2)}) copy-start(s32[3]{0:T(128)} %param.11) | copy-start | bytes 40
  146.5 9.7 %collective-permute-start.5 = (f32[16,256]{0,1:T(8,128)S(1)}, f32[16,256]{0,1:T(8,128)S(1)}, u32[]{:S(2)}, u32[]{:S(2)}) collective-permute-start(f32[16,256]{0,1:T(8,128)S(1)} %get-tuple-element.21), channel_id=1, source_target_pairs={{0,3},{1,0},{2,1},{3,2},{4,7},{5,4},{6,5},{7,6},{8,11},{9,8},{10,9... | collective-permute-start | bytes 49160 | tf_op jit(solution)/shard_map/ppermute | solution.py:42
  150.8 7.9 %collective-permute-start.4 = (f32[16,256]{0,1:T(8,128)S(1)}, f32[16,256]{0,1:T(8,128)S(1)}, u32[]{:S(2)}, u32[]{:S(2)}) collective-permute-start(f32[16,256]{0,1:T(8,128)S(1)} %get-tuple-element.22), channel_id=1, source_target_pairs={{0,2},{1,3},{2,0},{3,1},{4,6},{5,7},{6,4},{7,5},{8,10},{9,11},{10,... | collective-permute-start | bytes 49160 | tf_op jit(solution)/shard_map/ppermute | solution.py:42
  153.3 8.7 %collective-permute-start.3 = (f32[16,256]{0,1:T(8,128)S(1)}, f32[16,256]{0,1:T(8,128)S(1)}, u32[]{:S(2)}, u32[]{:S(2)}) collective-permute-start(f32[16,256]{0,1:T(8,128)S(1)} %get-tuple-element.20), channel_id=1, source_target_pairs={{0,1},{1,2},{2,3},{3,0},{4,5},{5,6},{6,7},{7,4},{8,9},{9,10},{10,1... | collective-permute-start | bytes 49160 | tf_op jit(solution)/shard_map/ppermute | solution.py:42
Sparse Core Ops, SparseCore 0:
  22.2 89.9 all-gather.1

commit v5 on v4

--- a/solution.py
+++ b/solution.py
@@ -19,14 +19,23 @@
     ]
     order = (mine - jnp.arange(replicas)) % replicas
     owned = jnp.take(jnp.stack(by_shift), order, axis=0).reshape(-1, rank_cols)
-    whole_b = lax.all_gather(owned, "tiles", axis=0, tiled=True)
+    holders = lax.psum(1, "tiles")
+    me = lax.axis_index("tiles")
+    levels = holders.bit_length() - 1
+    gathered = owned[None]
+    for bit in reversed(range(levels)):
+        partner = [(t, t ^ (1 << bit)) for t in range(holders)]
+        gathered = jnp.concatenate([gathered, lax.ppermute(gathered, "tiles", partner)], 0)
+    whole_b = gathered.reshape(-1, rank_cols)
+    apart = stored_second ^ me
+    place = sum(((apart >> (levels - 1 - k)) & 1) << k for k in range(levels))
     summed = jnp.zeros((tile_edge, rank_cols), jnp.float32)
     for position in range(slot_total):
         c_block = lax.dynamic_slice_in_dim(
             factor_c, tile_coords[position, 2] * tile_edge, tile_edge, 0
         ).astype(jnp.float32)
         b_block = lax.dynamic_slice_in_dim(
-            whole_b, stored_second[position] * tile_edge, tile_edge, 0
+            whole_b, place[position] * tile_edge, tile_edge, 0
         ).astype(jnp.float32)
         flat_tile = tile_data[position].reshape(tile_edge * tile_edge, tile_edge)
         inner_sum = jnp.dot(flat_tile, c_block, precision=lax.Precision.HIGHEST)

time: 189 us -> 228 us (1.21)
  starting transfers between devices: 19.8 us -> 58.5 us
  between operations: 18.6 us -> 4.98 us
  waiting for transfers between devices: 50.2 us -> 60.1 us
  local copies, waits for them, and re-layouts: 34.5 us -> 41.3 us
  other arithmetic: 39.9 us -> 37 us
    ppermute x0 -> x7, waiting for transfers between devices: none -> 52.5 us  [per_device(): lax.ppermute(gathered, 'tiles', partner)]
    all_gather x1 -> x0, waiting for transfers between devices: 41.4 us -> none  [per_device(): whole_b = lax.all_gather(owned, 'tiles', axis=0, tiled=True)]
    ppermute x0 -> x7, starting transfers between devices: none -> 40.1 us  [per_device(): lax.ppermute(gathered, 'tiles', partner)]
    unnamed x7 -> x23, local copies, waits for them, and re-layouts: 16.9 us -> 22.5 us
    concatenate x0 -> x2, local copies, waits for them, and re-layouts: none -> 4.64 us  [per_device(): jnp.concatenate([gathered, lax.ppermute(gathered, 'tiles', partner)], 0)]
    unnamed x3 -> x4, other arithmetic: 8.56 us -> 7.08 us
  transfers between devices with their start and end apart: 7 -> 13, of which waited for: 5 -> 10; matrix products, arithmetic and copies ran while one was open for 24% -> 19% of each run, Pallas kernels for 0% -> 0%
where the time goes in v5:
time: 228 us; the launch traced here: 227 us
  waiting for transfers between devices  60.1 us (26%)
  starting transfers between devices  58.5 us (26%)
  local copies, waits for them, and re-layouts  41.3 us (18%)
  other arithmetic  37 us (16%)
  matrix products  24.8 us (11%)
  between operations  4.98 us (2%)
    ppermute x7, waiting for transfers between devices, per_device(): lax.ppermute(gathered, 'tiles', partner)  52.5 us
    ppermute x7, starting transfers between devices, per_device(): lax.ppermute(gathered, 'tiles', partner)  40.1 us
    unnamed x23, local copies, waits for them, and re-layouts  22.5 us
    another operation x3, other arithmetic, spd_inverse(): top_inverse = lower_inverse(lax.linalg.cholesky(top))  12.4 us
    another operation x3, other arithmetic, spd_inverse(): bottom_inverse = lower_inverse(lax.linalg.cholesky(schur))  12.4 us
    dot_general x3, matrix products, per_device(): inner_sum = jnp.dot(flat_tile, c_block, precision=lax.Precision.HIGHEST)  11.7 us
    ppermute x3, starting transfers between devices, per_device(): lax.ppermute(factor_b, 'rep', [(e, (e + k) % replicas) for e in range(rep...  10.3 us
    ppermute x3, starting transfers between devices, per_device(): lax.ppermute(outgoing, 'rep', [(e, (e + k) % replicas) for e in range(rep...  8.05 us
  transfers between devices with their start and end apart: 13, of which 10 were waited for; matrix products, arithmetic and copies ran while one was open for 19% of the time, Pallas kernels for 0%

profile of v5, /device:TPU:1, one launch (start us, length us, event | category | flops | bytes accessed | tf_op | source)
XLA Modules:
  0.0 226.6 jit_solution(8222968480210627176)
XLA Ops:
  0.0 5.3 %collective-permute-start.2 = (bf16[16,256]{1,0:T(8,128)(2,1)}, bf16[16,256]{1,0:T(8,128)(2,1)S(1)}, u32[]{:S(2)}, u32[]{:S(2)}) collective-permute-start(bf16[16,256]{1,0:T(8,128)(2,1)} %param.13), channel_id=1, source_target_pairs={{0,3},{1,0},{2,1},{3,2},{4,7},{5,4},{6,5},{7,6},{8,11},{9,8},{10,9... | collective-permute-start | bytes 24584 | tf_op jit(solution)/shard_map/ppermute | solution.py:17
  7.8 2.5 %collective-permute-start = (bf16[16,256]{1,0:T(8,128)(2,1)}, bf16[16,256]{1,0:T(8,128)(2,1)S(1)}, u32[]{:S(2)}, u32[]{:S(2)}) collective-permute-start(bf16[16,256]{1,0:T(8,128)(2,1)} %param.13), channel_id=1, source_target_pairs={{0,1},{1,2},{2,3},{3,0},{4,5},{5,6},{6,7},{7,4},{8,9},{9,10},{10,1... | collective-permute-start | bytes 24584 | tf_op jit(solution)/shard_map/ppermute | solution.py:17
  15.6 10.8 %collective-permute-start.3 = (bf16[1,64,256]{2,1,0:T(8,128)(2,1)S(1)}, bf16[1,64,256]{2,1,0:T(8,128)(2,1)S(1)}, u32[]{:S(2)}, u32[]{:S(2)}) collective-permute-start(bf16[1,64,256]{2,1,0:T(8,128)(2,1)S(1)} %get-tuple-element.15), channel_id=1, source_target_pairs={{0,256},{4,260},{8,264},{12,268},{16,272},{20,276},{24,280},{28,28... | collective-permute-start | bytes 98312 | tf_op jit(solution)/shard_map/ppermute | solution.py:28
  27.7 4.4 %collective-permute-start.4 = (bf16[2,64,256]{2,1,0:T(8,128)(2,1)S(1)}, bf16[2,64,256]{2,1,0:T(8,128)(2,1)S(1)}, u32[]{:S(2)}, u32[]{:S(2)}) collective-permute-start(bf16[2,64,256]{2,1,0:T(8,128)(2,1)S(1)} %pad_maximum_fusion.2), channel_id=1, source_target_pairs={{0,128},{4,132},{8,136},{12,140},{16,144},{20,148},{24,152},{28,15... | collective-permute-start | bytes 196616 | tf_op jit(solution)/shard_map/ppermute | solution.py:28
  32.1 2.7 %collective-permute-done.4 = bf16[2,64,256]{2,1,0:T(8,128)(2,1)S(1)} collective-permute-done((bf16[2,64,256]{2,1,0:T(8,128)(2,1)S(1)}, bf16[2,64,256]{2,1,0:T(8,128)(2,1)S(1)}, u32[]{:S(2)}, u32[]{:S(2)}) %collective-permute-start.4) | collective-permute-done | bytes 65568 | tf_op jit(solution)/shard_map/ppermute | solution.py:28
  36.7 3.8 %collective-permute-done.5 = bf16[4,64,256]{2,1,0:T(8,128)(2,1)S(1)} collective-permute-done((bf16[4,64,256]{2,1,0:T(8,128)(2,1)S(1)}, bf16[4,64,256]{2,1,0:T(8,128)(2,1)S(1)}, u32[]{:S(2)}, u32[]{:S(2)}) %collective-permute-start.5) | collective-permute-done | bytes 131104 | tf_op jit(solution)/shard_map/ppermute | solution.py:28
  40.5 7.5 %collective-permute-start.6 = (bf16[8,64,256]{2,1,0:T(8,128)(2,1)S(1)}, bf16[8,64,256]{2,1,0:T(8,128)(2,1)S(1)}, u32[]{:S(2)}, u32[]{:S(2)}) collective-permute-start(bf16[8,64,256]{2,1,0:T(8,128)(2,1)S(1)} %pad_maximum_fusion), channel_id=1, source_target_pairs={{0,32},{4,36},{8,40},{12,44},{16,48},{20,52},{24,56},{28,60},{32,0... | collective-permute-start | bytes 786440 | tf_op jit(solution)/shard_map/ppermute | solution.py:28
  52.6 10.4 %collective-permute-start.7 = (bf16[16,64,256]{2,1,0:T(8,128)(2,1)S(1)}, bf16[16,64,256]{2,1,0:T(8,128)(2,1)S(1)}, u32[]{:S(2)}, u32[]{:S(2)}) collective-permute-start(bf16[16,64,256]{2,1,0:T(8,128)(2,1)S(1)} %get-tuple-element.30), channel_id=1, source_target_pairs={{0,16},{4,20},{8,24},{12,28},{16,0},{20,4},{24,8},{28,12},{32,48},... | collective-permute-start | bytes 1572872 | tf_op jit(solution)/shard_map/ppermute | solution.py:28
  64.0 20.6 %collective-permute-done.7 = bf16[16,64,256]{2,1,0:T(8,128)(2,1)S(1)} collective-permute-done((bf16[16,64,256]{2,1,0:T(8,128)(2,1)S(1)}, bf16[16,64,256]{2,1,0:T(8,128)(2,1)S(1)}, u32[]{:S(2)}, u32[]{:S(2)}) %collective-permute-start.7) | collective-permute-done | bytes 524320 | tf_op jit(solution)/shard_map/ppermute | solution.py:28
  89.4 22.3 %collective-permute-done.8 = bf16[32,64,256]{2,1,0:T(8,128)(2,1)S(1)} collective-permute-done((bf16[32,64,256]{2,1,0:T(8,128)(2,1)S(1)}, bf16[32,64,256]{2,1,0:T(8,128)(2,1)S(1)}, u32[]{:S(2)}, u32[]{:S(2)}) %collective-permute-start.8) | collective-permute-done | bytes 1048608 | tf_op jit(solution)/shard_map/ppermute | solution.py:28
  114.8 3.2 %collective-permute-start.9 = (bf16[64,64,256]{2,1,0:T(8,128)(2,1)}, bf16[64,64,256]{2,1,0:T(8,128)(2,1)}, u32[]{:S(2)}, u32[]{:S(2)}) collective-permute-start(bf16[64,64,256]{2,1,0:T(8,128)(2,1)} %get-tuple-element.22), channel_id=1, source_target_pairs={{0,4},{4,0},{8,12},{12,8},{16,20},{20,16},{24,28},{28,24},{32,36},... | collective-permute-start | bytes 6291464 | tf_op jit(solution)/shard_map/ppermute | solution.py:28
  125.5 3.9 %convolution_bitcast_fusion.2 = f32[4096,256]{0,1:T(8,128)} fusion(f32[4096,64]{1,0:T(8,128)S(1)} %reshape_squeeze.9, bf16[1024,256]{1,0:T(8,128)(2,1)S(1)} %copy-done, s32[]{:T(128)S(6)} %select_n.120), kind=kOutput, calls=%fused_computation.6 | convolution fusion | flops 805306368 | bytes 6324228 | tf_op jit(solution)/shard_map/dot_general | solution.py:41
  129.4 5.6 %copy.65 = f32[4096,256]{1,0:T(8,128)} copy(f32[4096,256]{0,1:T(8,128)} %convolution_bitcast_fusion.2) | data formatting | bytes 8388608
  137.1 3.9 %convolution_bitcast_fusion = f32[4096,256]{0,1:T(8,128)} fusion(f32[4096,64]{1,0:T(8,128)S(1)} %reshape_squeeze.11, bf16[1024,256]{1,0:T(8,128)(2,1)S(1)} %copy-done, s32[]{:T(128)S(6)} %select_n.124), kind=kOutput, calls=%fused_computation.4 | convolution fusion | flops 805306368 | bytes 6324228 | tf_op jit(solution)/shard_map/dot_general | solution.py:41
  140.9 5.6 %copy.67 = f32[4096,256]{1,0:T(8,128)} copy(f32[4096,256]{0,1:T(8,128)} %convolution_bitcast_fusion) | data formatting | bytes 8388608
  148.6 3.9 %convolution_bitcast_fusion.1 = f32[4096,256]{0,1:T(8,128)} fusion(f32[4096,64]{1,0:T(8,128)S(1)} %reshape_squeeze.10, bf16[1024,256]{1,0:T(8,128)(2,1)S(1)} %copy-done, s32[]{:T(128)S(6)} %select_n.122), kind=kOutput, calls=%fused_computation.5 | convolution fusion | flops 805306368 | bytes 6324228 | tf_op jit(solution)/shard_map/dot_general | solution.py:41
  152.4 5.6 %copy.66 = f32[4096,256]{1,0:T(8,128)} copy(f32[4096,256]{0,1:T(8,128)} %convolution_bitcast_fusion.1) | data formatting | bytes 8388608
  159.4 3.5 %constant_dynamic-update-slice_fusion.18 = bf16[128,64,256]{2,1,0:T(8,128)(2,1)} fusion(bf16[128,64,256]{2,1,0:T(8,128)(2,1)} %copy-done.5, bf16[64,64,256]{2,1,0:T(8,128)(2,1)} %collective-permute-done.9), kind=kLoop, calls=%fused_computation.77 | loop fusion | bytes 4194304 | tf_op jit(solution)/shard_map/concatenate | solution.py:28
  164.4 4.9 %multiply_reduce_fusion = (f32[256,64]{0,1:T(8,128)S(1)}, f32[256,64]{0,1:T(8,128)S(1)}) fusion(f32[256,64]{0,1:T(8,128)S(1)} %get-tuple-element.16, f32[4096,256]{1,0:T(8,128)} %copy.67, f32[4096,256]{1,0:T(8,128)} %copy.66, f32[256,64]{0,1:T(8,128)S(1)} %get-tuple-element.17), kind=kLoop, calls=%fused_computation.7 | loop fusion | flops 4161536 | bytes 8650752
  171.4 5.2 %fusion.31 = f32[256,256]{0,1:T(8,128)S(1)} fusion(bf16[8192,256]{1,0:T(8,128)(2,1)} %bitcast.122), kind=kOutput, calls=%fused_computation.131 | convolution fusion | flops 1073741824 | bytes 4456448 | tf_op jit(solution)/shard_map/dot_general | solution.py:54
  177.1 11.7 %custom-call.8 = f32[128,128]{1,0:T(8,128)S(1)} custom-call(f32[128,128]{1,0:T(8,128)S(1)} %fusion.11), custom_call_target="Cholesky" | custom-call | tf_op jit(solution)/shard_map/cholesky/custom-call.1 | solution.py:85
  196.7 3.1 %collective-permute-start.11 = (f32[16,256]{0,1:T(8,128)S(1)}, f32[16,256]{0,1:T(8,128)S(1)}, u32[]{:S(2)}, u32[]{:S(2)}) collective-permute-start(f32[16,256]{0,1:T(8,128)S(1)} %get-tuple-element.33), channel_id=1, source_target_pairs={{0,2},{1,3},{2,0},{3,1},{4,6},{5,7},{6,4},{7,5},{8,10},{9,11},{10,... | collective-permute-start | bytes 49160 | tf_op jit(solution)/shard_map/ppermute | solution.py:51
  199.9 3.0 %collective-permute-start.10 = (f32[16,256]{0,1:T(8,128)S(1)}, f32[16,256]{0,1:T(8,128)S(1)}, u32[]{:S(2)}, u32[]{:S(2)}) collective-permute-start(f32[16,256]{0,1:T(8,128)S(1)} %get-tuple-element.31), channel_id=1, source_target_pairs={{0,1},{1,2},{2,3},{3,0},{4,5},{5,6},{6,7},{7,4},{8,9},{9,10},{10,1... | collective-permute-start | bytes 49160 | tf_op jit(solution)/shard_map/ppermute | solution.py:51
  207.9 11.7 %custom-call.9 = f32[128,128]{1,0:T(8,128)S(1)} custom-call(f32[128,128]{1,0:T(8,128)S(1)} %broadcast_multiply_fusion), custom_call_target="Cholesky" | custom-call | tf_op jit(solution)/shard_map/cholesky/custom-call.1 | solution.py:89
  (113 shorter events, 56.5 us)
Async XLA Ops:
  0.0 125.5 %copy-start = (bf16[1024,256]{1,0:T(8,128)(2,1)S(1)}, bf16[1024,256]{1,0:T(8,128)(2,1)}, u32[]{:S(2)}) copy-start(bf16[1024,256]{1,0:T(8,128)(2,1)} %param.14) | copy-start | bytes 1572868
  0.0 87.4 %copy-start.4 = (s32[3,3]{1,0:T(4,128)S(1)}, s32[3,3]{1,0:T(4,128)}, u32[]{:S(2)}) copy-start(s32[3,3]{1,0:T(4,128)} %param.9) | copy-start | bytes 112
  0.0 10.5 %collective-permute-start.2 = (bf16[16,256]{1,0:T(8,128)(2,1)}, bf16[16,256]{1,0:T(8,128)(2,1)S(1)}, u32[]{:S(2)}, u32[]{:S(2)}) collective-permute-start(bf16[16,256]{1,0:T(8,128)(2,1)} %param.13), channel_id=1, source_target_pairs={{0,3},{1,0},{2,1},{3,2},{4,7},{5,4},{6,5},{7,6},{8,11},{9,8},{10,9... | collective-permute-start | bytes 24584 | tf_op jit(solution)/shard_map/ppermute | solution.py:17
  5.4 6.1 %collective-permute-start.1 = (bf16[16,256]{1,0:T(8,128)(2,1)}, bf16[16,256]{1,0:T(8,128)(2,1)S(1)}, u32[]{:S(2)}, u32[]{:S(2)}) collective-permute-start(bf16[16,256]{1,0:T(8,128)(2,1)} %param.13), channel_id=1, source_target_pairs={{0,2},{1,3},{2,0},{3,1},{4,6},{5,7},{6,4},{7,5},{8,10},{9,11},{10,... | collective-permute-start | bytes 24584 | tf_op jit(solution)/shard_map/ppermute | solution.py:17
  7.8 5.8 %collective-permute-start = (bf16[16,256]{1,0:T(8,128)(2,1)}, bf16[16,256]{1,0:T(8,128)(2,1)S(1)}, u32[]{:S(2)}, u32[]{:S(2)}) collective-permute-start(bf16[16,256]{1,0:T(8,128)(2,1)} %param.13), channel_id=1, source_target_pairs={{0,1},{1,2},{2,3},{3,0},{4,5},{5,6},{6,7},{7,4},{8,9},{9,10},{10,1... | collective-permute-start | bytes 24584 | tf_op jit(solution)/shard_map/ppermute | solution.py:17
  14.9 72.8 %copy-start.3 = (f32[3,64,4096]{2,1,0:T(8,128)S(1)}, f32[3,64,4096]{2,1,0:T(8,128)}, u32[]{:S(2)}) copy-start(f32[3,64,4096]{2,1,0:T(8,128)} %param.8) | copy-start | bytes 9437188
  15.6 12.1 %collective-permute-start.3 = (bf16[1,64,256]{2,1,0:T(8,128)(2,1)S(1)}, bf16[1,64,256]{2,1,0:T(8,128)(2,1)S(1)}, u32[]{:S(2)}, u32[]{:S(2)}) collective-permute-start(bf16[1,64,256]{2,1,0:T(8,128)(2,1)S(1)} %get-tuple-element.15), channel_id=1, source_target_pairs={{0,256},{4,260},{8,264},{12,268},{16,272},{20,276},{24,280},{28,28... | collective-permute-start | bytes 98312 | tf_op jit(solution)/shard_map/ppermute | solution.py:28
  27.7 7.1 %collective-permute-start.4 = (bf16[2,64,256]{2,1,0:T(8,128)(2,1)S(1)}, bf16[2,64,256]{2,1,0:T(8,128)(2,1)S(1)}, u32[]{:S(2)}, u32[]{:S(2)}) collective-permute-start(bf16[2,64,256]{2,1,0:T(8,128)(2,1)S(1)} %pad_maximum_fusion.2), channel_id=1, source_target_pairs={{0,128},{4,132},{8,136},{12,140},{16,144},{20,148},{24,152},{28,15... | collective-permute-start | bytes 196616 | tf_op jit(solution)/shard_map/ppermute | solution.py:28
  34.8 5.7 %collective-permute-start.5 = (bf16[4,64,256]{2,1,0:T(8,128)(2,1)S(1)}, bf16[4,64,256]{2,1,0:T(8,128)(2,1)S(1)}, u32[]{:S(2)}, u32[]{:S(2)}) collective-permute-start(bf16[4,64,256]{2,1,0:T(8,128)(2,1)S(1)} %pad_maximum_fusion.1), channel_id=1, source_target_pairs={{0,64},{4,68},{8,72},{12,76},{16,80},{20,84},{24,88},{28,92},{32,9... | collective-permute-start | bytes 393224 | tf_op jit(solution)/shard_map/ppermute | solution.py:28
  40.5 11.3 %collective-permute-start.6 = (bf16[8,64,256]{2,1,0:T(8,128)(2,1)S(1)}, bf16[8,64,256]{2,1,0:T(8,128)(2,1)S(1)}, u32[]{:S(2)}, u32[]{:S(2)}) collective-permute-start(bf16[8,64,256]{2,1,0:T(8,128)(2,1)S(1)} %pad_maximum_fusion), channel_id=1, source_target_pairs={{0,32},{4,36},{8,40},{12,44},{16,48},{20,52},{24,56},{28,60},{32,0... | collective-permute-start | bytes 786440 | tf_op jit(solution)/shard_map/ppermute | solution.py:28
  52.6 31.9 %collective-permute-start.7 = (bf16[16,64,256]{2,1,0:T(8,128)(2,1)S(1)}, bf16[16,64,256]{2,1,0:T(8,128)(2,1)S(1)}, u32[]{:S(2)}, u32[]{:S(2)}) collective-permute-start(bf16[16,64,256]{2,1,0:T(8,128)(2,1)S(1)} %get-tuple-element.30), channel_id=1, source_target_pairs={{0,16},{4,20},{8,24},{12,28},{16,0},{20,4},{24,8},{28,12},{32,48},... | collective-permute-start | bytes 1572872 | tf_op jit(solution)/shard_map/ppermute | solution.py:28
  85.5 26.1 %collective-permute-start.8 = (bf16[32,64,256]{2,1,0:T(8,128)(2,1)S(1)}, bf16[32,64,256]{2,1,0:T(8,128)(2,1)S(1)}, u32[]{:S(2)}, u32[]{:S(2)}) collective-permute-start(bf16[32,64,256]{2,1,0:T(8,128)(2,1)S(1)} %get-tuple-element.26), channel_id=1, source_target_pairs={{0,8},{4,12},{8,0},{12,4},{16,24},{20,28},{24,16},{28,20},{32,40},... | collective-permute-start | bytes 3145736 | tf_op jit(solution)/shard_map/ppermute | solution.py:28
  87.6 30.4 %copy-start.1 = (s32[128]{0:T(128)S(1)}, s32[128]{0:T(128)}, u32[]{:S(2)}) copy-start(s32[128]{0:T(128)} %param.12) | copy-start | bytes 1540
  112.8 1.9 copy-start.5
  114.8 44.6 %collective-permute-start.9 = (bf16[64,64,256]{2,1,0:T(8,128)(2,1)}, bf16[64,64,256]{2,1,0:T(8,128)(2,1)}, u32[]{:S(2)}, u32[]{:S(2)}) collective-permute-start(bf16[64,64,256]{2,1,0:T(8,128)(2,1)} %get-tuple-element.22), channel_id=1, source_target_pairs={{0,4},{4,0},{8,12},{12,8},{16,20},{20,16},{24,28},{28,24},{32,36},... | collective-permute-start | bytes 6291464 | tf_op jit(solution)/shard_map/ppermute | solution.py:28
  152.4 6.3 %copy-start.6 = (s32[3]{0:T(128)S(1)}, s32[3]{0:T(128)}, u32[]{:S(2)}) copy-start(s32[3]{0:T(128)} %param.11) | copy-start | bytes 40
  158.7 4.9 %copy-start.2 = (f32[4096,256]{1,0:T(8,128)S(1)}, f32[4096,256]{1,0:T(8,128)}, u32[]{:S(2)}) copy-start(f32[4096,256]{1,0:T(8,128)} %copy.65) | copy-start | bytes 12582916
  194.8 8.3 %collective-permute-start.12 = (f32[16,256]{0,1:T(8,128)S(1)}, f32[16,256]{0,1:T(8,128)S(1)}, u32[]{:S(2)}, u32[]{:S(2)}) collective-permute-start(f32[16,256]{0,1:T(8,128)S(1)} %get-tuple-element.32), channel_id=1, source_target_pairs={{0,3},{1,0},{2,1},{3,2},{4,7},{5,4},{6,5},{7,6},{8,11},{9,8},{10,9... | collective-permute-start | bytes 49160 | tf_op jit(solution)/shard_map/ppermute | solution.py:51
  196.7 8.5 %collective-permute-start.11 = (f32[16,256]{0,1:T(8,128)S(1)}, f32[16,256]{0,1:T(8,128)S(1)}, u32[]{:S(2)}, u32[]{:S(2)}) collective-permute-start(f32[16,256]{0,1:T(8,128)S(1)} %get-tuple-element.33), channel_id=1, source_target_pairs={{0,2},{1,3},{2,0},{3,1},{4,6},{5,7},{6,4},{7,5},{8,10},{9,11},{10,... | collective-permute-start | bytes 49160 | tf_op jit(solution)/shard_map/ppermute | solution.py:51
  199.9 7.7 %collective-permute-start.10 = (f32[16,256]{0,1:T(8,128)S(1)}, f32[16,256]{0,1:T(8,128)S(1)}, u32[]{:S(2)}, u32[]{:S(2)}) collective-permute-start(f32[16,256]{0,1:T(8,128)S(1)} %get-tuple-element.31), channel_id=1, source_target_pairs={{0,1},{1,2},{2,3},{3,0},{4,5},{5,6},{6,7},{7,4},{8,9},{9,10},{10,1... | collective-permute-start | bytes 49160 | tf_op jit(solution)/shard_map/ppermute | solution.py:51

commit v6 on v3

--- a/solution.py
+++ b/solution.py
@@ -11,7 +11,9 @@
     is_live = jnp.arange(slot_total, dtype=jnp.int32) < tile_count[0]
     slot_scale = weights.astype(jnp.float32) * is_live.astype(jnp.float32)
     stored_second = jnp.take(owner_map, tile_coords[:, 1])
-    owned = lax.all_gather(factor_b, "rep", axis=0, tiled=True)
+    replicas = lax.psum(1, "rep")
+    copies = jnp.broadcast_to(factor_b[None], (replicas,) + factor_b.shape)
+    owned = lax.all_to_all(copies, "rep", 0, 0).reshape(-1, rank_cols)
     whole_b = lax.all_gather(owned, "tiles", axis=0, tiled=True)
     summed = jnp.zeros((tile_edge, rank_cols), jnp.float32)
     for position in range(slot_total):
@@ -28,11 +30,12 @@
         rounded = (partial_value * slot_scale[position]).astype(jnp.bfloat16)
         summed = summed + rounded.astype(jnp.float32)
     summed, whole_b = lax.optimization_barrier((summed, whole_b))
-    my_rows = lax.psum_scatter(summed, "rep", scatter_dimension=0, tiled=True)
+    pieces = summed.reshape(replicas, tile_edge // replicas, rank_cols)
+    my_rows = lax.all_to_all(pieces, "rep", 0, 0).sum(0)
     gram_b = jnp.dot(whole_b.T, whole_b, preferred_element_type=jnp.float32)
     gram_c = jnp.dot(factor_c.T, factor_c, preferred_element_type=jnp.float32)
     normal_matrix = gram_b * gram_c
-    normal_inverse = spd_inverse(normal_matrix)
+    normal_inverse, my_rows = spd_inverse(normal_matrix, my_rows)
     return jnp.dot(my_rows, normal_inverse, precision=lax.Precision.HIGHEST)
 
 
@@ -55,7 +58,7 @@
     return product / diagonal[None, :]
 
 
-def spd_inverse(matrix):
+def spd_inverse(matrix, carried):
     half = matrix.shape[0] // 2
     top = matrix[:half, :half]
     side = matrix[half:, :half]
@@ -63,13 +66,14 @@
     top_inverse = lower_inverse(lax.linalg.cholesky(top))
     side_factor = mm(side, top_inverse.T)
     schur = bottom - mm(side_factor, side_factor.T)
+    schur, carried = lax.optimization_barrier((schur, carried))
     bottom_inverse = lower_inverse(lax.linalg.cholesky(schur))
     corner = -mm(bottom_inverse, mm(side_factor, top_inverse))
     zeros = jnp.zeros((half, matrix.shape[0] - half), matrix.dtype)
     inverse = jnp.concatenate(
         [jnp.concatenate([top_inverse, zeros], 1), jnp.concatenate([corner, bottom_inverse], 1)], 0
     )
-    return mm(inverse.T, inverse)
+    return mm(inverse.T, inverse), carried
 
 
 def solution(mesh):

time: 191 us -> 171 us (0.90)
  waiting for transfers between devices: 60 us -> 45.1 us
  matrix products: 25.4 us -> 21.3 us
  starting transfers between devices: 0.04 us -> 3.98 us
  blocking collectives: 12 us -> 9.04 us
    unnamed x3 -> x1, waiting for transfers between devices: 17.4 us -> 0.02 us
    all_gather x1 -> x0, blocking collectives: 12 us -> none  [per_device(): owned = lax.all_gather(factor_b, 'rep', axis=0, tiled=True)]
    all_to_all x0 -> x1, blocking collectives: none -> 9.04 us  [per_device(): owned = lax.all_to_all(copies, 'rep', 0, 0).reshape(-1, rank_cols)]
    unnamed x3 -> x1, other arithmetic: 8.56 us -> 0.95 us
    dot_general x0 -> x2, other arithmetic: none -> 6.91 us  [per_device(): partial_value = jnp.einsum('ijr,jr->ir', inner_sum, b_block)]
    all_to_all x0 -> x1, waiting for transfers between devices: none -> 4.27 us  [per_device(): my_rows = lax.all_to_all(pieces, 'rep', 0, 0).sum(0)]
    all_to_all x0 -> x1, starting transfers between devices: none -> 3.98 us  [per_device(): my_rows = lax.all_to_all(pieces, 'rep', 0, 0).sum(0)]
    dot_general x1, matrix products: 5.2 us -> 1.84 us  [per_device(): gram_b = jnp.dot(whole_b.T, whole_b, preferred_element_type=jnp.float32)]
  transfers between devices with their start and end apart: 2 -> 2, of which waited for: 2 -> 2; matrix products, arithmetic and copies ran while one was open for 25% -> 26% of each run, Pallas kernels for 0% -> 0%
where the time goes in v6:
time: 171 us; the launch traced here: 170 us
  waiting for transfers between devices  45.1 us (26%)
  other arithmetic  38.3 us (22%)
  local copies, waits for them, and re-layouts  34.1 us (20%)
  matrix products  21.3 us (12%)
  between operations  18.4 us (11%)
  blocking collectives  9.04 us (5%)
  starting transfers between devices  3.98 us (2%)
    all_gather x1, waiting for transfers between devices, per_device(): whole_b = lax.all_gather(owned, 'tiles', axis=0, tiled=True)  40.8 us
    unnamed x11, local copies, waits for them, and re-layouts  16.9 us
    another operation x3, other arithmetic, spd_inverse(): top_inverse = lower_inverse(lax.linalg.cholesky(top))  12.4 us
    another operation x3, other arithmetic, spd_inverse(): bottom_inverse = lower_inverse(lax.linalg.cholesky(schur))  12.4 us
    dot_general x3, matrix products, per_device(): inner_sum = jnp.dot(flat_tile, c_block, precision=lax.Precision.HIGHEST)  11.7 us
    all_to_all x1, blocking collectives, per_device(): owned = lax.all_to_all(copies, 'rep', 0, 0).reshape(-1, rank_cols)  9.04 us
    dot_general x2, other arithmetic, per_device(): partial_value = jnp.einsum('ijr,jr->ir', inner_sum, b_block)  6.91 us
    dot_general x29, matrix products, mm(): return jnp.dot(left, right, precision=lax.Precision.HIGHEST)  6.62 us
  transfers between devices with their start and end apart: 2, of which 2 were waited for; matrix products, arithmetic and copies ran while one was open for 26% of the time, Pallas kernels for 0%

profile of v6, /device:TPU:1, one launch (start us, length us, event | category | flops | bytes accessed | tf_op | source)
XLA Modules:
  0.0 170.3 jit_solution(16010142907541364856)
XLA Ops:
  7.3 9.0 %all_to_all.10 = bf16[4,16,256]{2,1,0:T(8,128)(2,1)} all-to-all(bf16[4,16,256]{2,1,0:T(8,128)(2,1)S(1)} %broadcast_in_dim.10), channel_id=1, replica_groups=mesh['tiles'=128,'rep'=4] {'rep'}, dimensions={0} | all-to-all | bytes 65536 | tf_op jit(solution)/shard_map/all_to_all | solution.py:16
  17.2 1.3 gather_fusion
  21.9 1.5 fusion.25
  25.4 3.7 %fusion.24 = (f32[1,64,4096]{2,1,0:T(8,128)}, f32[1,64,4096]{2,1,0:T(8,128)}, f32[1,64,4096]{2,1,0:T(8,128)}) fusion(f32[3,64,4096]{2,1,0:T(8,128)} %param.8), kind=kLoop, calls=%fused_computation.78 | loop fusion | bytes 6291456 | tf_op jit(solution)/shard_map/slice | solution.py:26
  29.1 2.0 %reshape_squeeze.9 = f32[4096,64]{1,0:T(8,128)S(1)} reshape(f32[1,64,4096]{2,1,0:T(8,128)} %get-tuple-element.18) | data formatting | bytes 2097152 | tf_op jit(solution)/shard_map/reshape;squeeze | solution.py:26
  31.1 3.9 %convolution_bitcast_fusion.2 = f32[4096,256]{0,1:T(8,128)} fusion(f32[4096,64]{1,0:T(8,128)S(1)} %reshape_squeeze.9, bf16[1024,256]{1,0:T(8,128)(2,1)S(1)} %copy-done, s32[]{:T(128)S(6)} %select_n.44), kind=kOutput, calls=%fused_computation.5 | convolution fusion | flops 805306368 | bytes 6324228 | tf_op jit(solution)/shard_map/dot_general | solution.py:27
  35.1 5.6 %copy.62 = f32[4096,256]{1,0:T(8,128)} copy(f32[4096,256]{0,1:T(8,128)} %convolution_bitcast_fusion.2) | data formatting | bytes 8388608
  40.7 2.0 %reshape_squeeze.11 = f32[4096,64]{1,0:T(8,128)S(1)} reshape(f32[1,64,4096]{2,1,0:T(8,128)} %get-tuple-element.17) | data formatting | bytes 2097152 | tf_op jit(solution)/shard_map/reshape;squeeze | solution.py:26
  42.7 3.9 %convolution_bitcast_fusion = f32[4096,256]{0,1:T(8,128)} fusion(f32[4096,64]{1,0:T(8,128)S(1)} %reshape_squeeze.11, bf16[1024,256]{1,0:T(8,128)(2,1)S(1)} %copy-done, s32[]{:T(128)S(6)} %select_n.48), kind=kOutput, calls=%fused_computation.3 | convolution fusion | flops 805306368 | bytes 6324228 | tf_op jit(solution)/shard_map/dot_general | solution.py:27
  46.6 5.6 %copy.64 = f32[4096,256]{1,0:T(8,128)} copy(f32[4096,256]{0,1:T(8,128)} %convolution_bitcast_fusion) | data formatting | bytes 8388608
  52.2 2.0 %reshape_squeeze.10 = f32[4096,64]{1,0:T(8,128)S(1)} reshape(f32[1,64,4096]{2,1,0:T(8,128)} %get-tuple-element.19) | data formatting | bytes 2097152 | tf_op jit(solution)/shard_map/reshape;squeeze | solution.py:26
  54.2 3.9 %convolution_bitcast_fusion.1 = f32[4096,256]{0,1:T(8,128)} fusion(f32[4096,64]{1,0:T(8,128)S(1)} %reshape_squeeze.10, bf16[1024,256]{1,0:T(8,128)(2,1)S(1)} %copy-done, s32[]{:T(128)S(6)} %select_n.46), kind=kOutput, calls=%fused_computation.4 | convolution fusion | flops 805306368 | bytes 6324228 | tf_op jit(solution)/shard_map/dot_general | solution.py:27
  58.1 5.6 %copy.63 = f32[4096,256]{1,0:T(8,128)} copy(f32[4096,256]{0,1:T(8,128)} %convolution_bitcast_fusion.1) | data formatting | bytes 8388608
  65.1 40.8 %all-gather.2.cloned.1.call-done = bf16[8192,256]{1,0:T(8,128)(2,1)} async-done(((bf16[64,256]{1,0:T(8,128)(2,1)}), bf16[8192,256]{1,0:T(8,128)(2,1)}) %all-gather.2.cloned.1.call-update) | async-done | bytes 4194320 | tf_op jit(solution)/shard_map/all_gather | solution.py:17
  106.8 3.1 %multiply_reduce_fusion.2 = f32[256,64]{0,1:T(8,128)S(1)} fusion(f32[256,64]{0,1:T(8,128)S(1)} %get-tuple-element.16, f32[4096,256]{1,0:T(8,128)} %copy.62), kind=kLoop, calls=%fused_computation.8 | loop fusion | flops 2080768 | bytes 4325376 | tf_op jit(solution)/shard_map/ijr,jr->ir/dot_general | solution.py:29
  109.9 3.9 %multiply_reduce_fusion = (f32[256,64]{0,1:T(8,128)S(1)}, f32[256,64]{0,1:T(8,128)S(1)}) fusion(f32[256,64]{0,1:T(8,128)S(1)} %get-tuple-element.14, f32[4096,256]{1,0:T(8,128)S(1)} %copy-done.1, f32[4096,256]{1,0:T(8,128)} %copy.63, f32[256,64]{0,1:T(8,128)S(1)} %get-tuple-element.15), kind=kLoop, calls=%fused_computation.6 | loop fusion | flops 4161536 | bytes 8650752 | tf_op jit(solution)/shard_map/ijr,jr->ir/dot_general | solution.py:29
  113.8 2.5 %add_bitcast_fusion = f32[64,256]{1,0:T(8,128)} fusion(f32[256,64]{0,1:T(8,128)S(1)} %multiply_reduce_fusion.2, f32[256,64]{0,1:T(8,128)S(1)} %get-tuple-element.30, f32[256,64]{0,1:T(8,128)S(1)} %get-tuple-element.29, f32[]{:T(128)} %bitcast.28, f32[]{:T(128)} %bitcast.21, f32[]{:T(128)} %bitcast.14), kind=kLoop, calls=%fused_computation.48 | loop fusion | flops 180224 | bytes 262156 | tf_op jit(solution)/shard_map/add | solution.py:31
  116.3 1.8 %fusion.28 = f32[256,256]{0,1:T(8,128)S(1)} fusion(bf16[8192,256]{1,0:T(8,128)(2,1)S(1)} %copy-done.2), kind=kOutput, calls=%fused_computation.82 | convolution fusion | flops 1073741824 | bytes 4456448 | tf_op jit(solution)/shard_map/dot_general | solution.py:35
  118.6 11.7 %custom-call.8 = f32[128,128]{1,0:T(8,128)S(1)} custom-call(f32[128,128]{1,0:T(8,128)S(1)} %fusion.11), custom_call_target="Cholesky" | custom-call | tf_op jit(solution)/shard_map/cholesky/custom-call.1 | solution.py:66
  131.7 1.2 gather_fusion.1
  136.2 4.0 %all-to-all-start.1 = ((f32[4,16,256]{2,1,0:T(8,128)}), f32[4,16,256]{2,1,0:T(8,128)S(1)}, u32[]{:S(2)}, u32[]{:S(2)}) async-start(f32[4,16,256]{2,1,0:T(8,128)} %bitcast.32), calls=%async_computation.1 | async-start | bytes 131072 | tf_op jit(solution)/shard_map/all_to_all | solution.py:34
  140.4 4.3 %all-to-all-done.1 = f32[4,16,256]{2,1,0:T(8,128)S(1)} async-done(((f32[4,16,256]{2,1,0:T(8,128)}), f32[4,16,256]{2,1,0:T(8,128)S(1)}, u32[]{:S(2)}, u32[]{:S(2)}) %all-to-all-start.1) | async-done | bytes 65568 | tf_op jit(solution)/shard_map/all_to_all | solution.py:34
  144.9 11.7 %custom-call.9 = f32[128,128]{1,0:T(8,128)S(1)} custom-call(f32[128,128]{1,0:T(8,128)S(1)} %broadcast_multiply_fusion), custom_call_target="Cholesky" | custom-call | tf_op jit(solution)/shard_map/cholesky/custom-call.1 | solution.py:70
  157.9 1.2 gather_fusion.2
  (65 shorter events, 15.6 us)
Async XLA Ops:
  6.5 24.6 %copy-start = (bf16[1024,256]{1,0:T(8,128)(2,1)S(1)}, bf16[1024,256]{1,0:T(8,128)(2,1)}, u32[]{:S(2)}) copy-start(bf16[1024,256]{1,0:T(8,128)(2,1)} %param.14) | copy-start | bytes 1572868
  6.5 99.3 %all-gather.2.cloned.1.call-start = ((), (), s32[]{:S(2)}) async-start(), calls=%async_computation.2 | async-start | bytes 4227072 | tf_op jit(solution)/shard_map/all_gather | solution.py:17
  58.1 6.3 %copy-start.3 = (s32[3]{0:T(128)S(1)}, s32[3]{0:T(128)}, u32[]{:S(2)}) copy-start(s32[3]{0:T(128)} %param.11) | copy-start | bytes 40
  105.9 4.0 %copy-start.1 = (f32[4096,256]{1,0:T(8,128)S(1)}, f32[4096,256]{1,0:T(8,128)}, u32[]{:S(2)}) copy-start(f32[4096,256]{1,0:T(8,128)} %copy.64) | copy-start | bytes 12582916
  109.9 6.4 %copy-start.2 = (bf16[8192,256]{1,0:T(8,128)(2,1)S(1)}, bf16[8192,256]{1,0:T(8,128)(2,1)}, u32[]{:S(2)}) copy-start(bf16[8192,256]{1,0:T(8,128)(2,1)} %all-gather.2.cloned.1.call-done) | copy-start | bytes 12582916
  136.2 8.5 %all-to-all-start.1 = ((f32[4,16,256]{2,1,0:T(8,128)}), f32[4,16,256]{2,1,0:T(8,128)S(1)}, u32[]{:S(2)}, u32[]{:S(2)}) async-start(f32[4,16,256]{2,1,0:T(8,128)} %bitcast.32), calls=%async_computation.1 | async-start | bytes 131072 | tf_op jit(solution)/shard_map/all_to_all | solution.py:34
Sparse Core Ops, SparseCore 0:
  16.5 89.3 all-gather.1

commit v7 on v6

--- a/solution.py
+++ b/solution.py
@@ -1,6 +1,8 @@
 import jax
 import jax.numpy as jnp
 from jax import lax
+from jax.experimental import pallas as pl
+from jax.experimental.pallas import tpu as pltpu
 from jax.sharding import PartitionSpec as P
 
 
@@ -15,20 +17,19 @@
     copies = jnp.broadcast_to(factor_b[None], (replicas,) + factor_b.shape)
     owned = lax.all_to_all(copies, "rep", 0, 0).reshape(-1, rank_cols)
     whole_b = lax.all_gather(owned, "tiles", axis=0, tiled=True)
-    summed = jnp.zeros((tile_edge, rank_cols), jnp.float32)
+    inners = []
+    b_blocks = []
     for position in range(slot_total):
         c_block = lax.dynamic_slice_in_dim(
             factor_c, tile_coords[position, 2] * tile_edge, tile_edge, 0
         ).astype(jnp.float32)
-        b_block = lax.dynamic_slice_in_dim(
-            whole_b, stored_second[position] * tile_edge, tile_edge, 0
-        ).astype(jnp.float32)
+        b_blocks.append(
+            lax.dynamic_slice_in_dim(whole_b, stored_second[position] * tile_edge, tile_edge, 0)
+        )
         flat_tile = tile_data[position].reshape(tile_edge * tile_edge, tile_edge)
         inner_sum = jnp.dot(flat_tile, c_block, precision=lax.Precision.HIGHEST)
-        inner_sum = inner_sum.reshape(tile_edge, tile_edge, rank_cols)
-        partial_value = jnp.einsum("ijr,jr->ir", inner_sum, b_block)
-        rounded = (partial_value * slot_scale[position]).astype(jnp.bfloat16)
-        summed = summed + rounded.astype(jnp.float32)
+        inners.append(inner_sum.reshape(tile_edge, tile_edge, rank_cols))
+    summed = weighted_sum(slot_scale, jnp.stack(b_blocks), inners)
     summed, whole_b = lax.optimization_barrier((summed, whole_b))
     pieces = summed.reshape(replicas, tile_edge // replicas, rank_cols)
     my_rows = lax.all_to_all(pieces, "rep", 0, 0).sum(0)
@@ -39,14 +40,41 @@
     return jnp.dot(my_rows, normal_inverse, precision=lax.Precision.HIGHEST)
 
 
+def weigh_kernel(scale_ref, b_ref, *refs):
+    inner_refs, out_ref = refs[:-1], refs[-1]
+    total = jnp.zeros(out_ref.shape, jnp.float32)
+    for slot, inner_ref in enumerate(inner_refs):
+        second = b_ref[slot].astype(jnp.float32)
+        partial_value = jnp.sum(inner_ref[...] * second[None], axis=1)
+        rounded = (partial_value * scale_ref[slot]).astype(jnp.bfloat16)
+        total = total + rounded.astype(jnp.float32)
+    out_ref[...] = total
+
+
+def weighted_sum(slot_scale, b_blocks, inners, rows=8):
+    edge, second, rank_cols = inners[0].shape
+    inner_spec = pl.BlockSpec((rows, second, rank_cols), lambda i: (i, 0, 0))
+    return pl.pallas_call(
+        weigh_kernel,
+        grid=(edge // rows,),
+        in_specs=[
+            pl.BlockSpec(memory_space=pltpu.SMEM),
+            pl.BlockSpec(b_blocks.shape, lambda i: (0, 0, 0)),
+        ]
+        + [inner_spec] * len(inners),
+        out_specs=pl.BlockSpec((rows, rank_cols), lambda i: (i, 0)),
+        out_shape=jax.ShapeDtypeStruct((edge, rank_cols), jnp.float32),
+    )(slot_scale, b_blocks, *inners)
+
+
 def mm(left, right):
     return jnp.dot(left, right, precision=lax.Precision.HIGHEST)
 
 
 def lower_inverse(lower):
     size = lower.shape[0]
-    diagonal = jnp.diagonal(lower)
     identity = jnp.eye(size, dtype=lower.dtype)
+    diagonal = jnp.sum(lower * identity, axis=1)
     strict = identity - lower / diagonal[:, None]
     product = identity + strict
     power = strict

time: 171 us -> 174 us (1.018)
  other arithmetic: 38.3 us -> 29.2 us
  Pallas kernels: 0 us -> 7.94 us
  matrix products: 21.3 us -> 27.3 us
  local copies, waits for them, and re-layouts: 34.1 us -> 31.8 us
    unnamed x11 -> x4, local copies, waits for them, and re-layouts: 16.9 us -> 0.01 us
    dot_general x0 -> x3, local copies, waits for them, and re-layouts: none -> 16.8 us  [per_device(): inner_sum = jnp.dot(flat_tile, c_block, precision=lax.Precision.HIGHEST)]
    pallas_call x0 -> x1, Pallas kernels: none -> 7.94 us  [weighted_sum(): pl.pallas_call(weigh_kernel, grid=(edge // rows,), in_specs=[pl.BlockSpec...]
    dot_general x2 -> x0, other arithmetic: 6.91 us -> none  [per_device(): partial_value = jnp.einsum('ijr,jr->ir', inner_sum, b_block)]
    dot_general x1, matrix products: 1.84 us -> 5.2 us  [per_device(): gram_b = jnp.dot(whole_b.T, whole_b, preferred_element_type=jnp.float32)]
    dot_general x29, matrix products: 6.62 us -> 9.21 us  [mm(): return jnp.dot(left, right, precision=lax.Precision.HIGHEST)]
    add x1 -> x0, other arithmetic: 2.54 us -> none  [per_device(): summed = summed + rounded.astype(jnp.float32)]
    gather x2 -> x0, local copies, waits for them, and re-layouts: 2.49 us -> none  [lower_inverse(): diagonal = jnp.diagonal(lower)]
where the time goes in v7:
time: 174 us; the launch traced here: 173 us
  waiting for transfers between devices  45.3 us (26%)
  local copies, waits for them, and re-layouts  31.8 us (18%)
  other arithmetic  29.2 us (17%)
  matrix products  27.3 us (16%)
  between operations  18.3 us (11%)
  blocking collectives  9.04 us (5%)
  Pallas kernels  7.94 us (5%)
  starting transfers between devices  3.98 us (2%)
    all_gather x1, waiting for transfers between devices, per_device(): whole_b = lax.all_gather(owned, 'tiles', axis=0, tiled=True)  41 us
    dot_general x3, local copies, waits for them, and re-layouts, per_device(): inner_sum = jnp.dot(flat_tile, c_block, precision=lax.Precision.HIGHEST)  16.8 us
    another operation x3, other arithmetic, spd_inverse(): bottom_inverse = lower_inverse(lax.linalg.cholesky(schur))  12.4 us
    another operation x3, other arithmetic, spd_inverse(): top_inverse = lower_inverse(lax.linalg.cholesky(top))  12.4 us
    dot_general x3, matrix products, per_device(): inner_sum = jnp.dot(flat_tile, c_block, precision=lax.Precision.HIGHEST)  11.7 us
    dot_general x29, matrix products, mm(): return jnp.dot(left, right, precision=lax.Precision.HIGHEST)  9.21 us
    all_to_all x1, blocking collectives, per_device(): owned = lax.all_to_all(copies, 'rep', 0, 0).reshape(-1, rank_cols)  9.04 us
    pallas_call x1, Pallas kernels, weighted_sum(): pl.pallas_call(weigh_kernel, grid=(edge // rows,), in_specs=[pl.BlockSpec...  7.94 us
  transfers between devices with their start and end apart: 2, of which 2 were waited for; matrix products, arithmetic and copies ran while one was open for 26% of the time, Pallas kernels for 0%

profile of v7, /device:TPU:1, one launch (start us, length us, event | category | flops | bytes accessed | tf_op | source)
XLA Modules:
  0.0 172.8 jit_solution(15992384057240751063)
XLA Ops:
  7.3 9.0 %all_to_all.10 = bf16[4,16,256]{2,1,0:T(8,128)(2,1)} all-to-all(bf16[4,16,256]{2,1,0:T(8,128)(2,1)S(1)} %broadcast_in_dim.4), channel_id=1, replica_groups=mesh['tiles'=128,'rep'=4] {'rep'}, dimensions={0} | all-to-all | bytes 65536 | tf_op jit(solution)/shard_map/all_to_all | solution.py:18
  17.2 1.3 gather_fusion
  21.9 1.5 fusion.25
  25.3 3.7 %fusion.24 = (f32[1,64,4096]{2,1,0:T(8,128)}, f32[1,64,4096]{2,1,0:T(8,128)}, f32[1,64,4096]{2,1,0:T(8,128)}) fusion(f32[3,64,4096]{2,1,0:T(8,128)} %param.8), kind=kLoop, calls=%fused_computation.71 | loop fusion | bytes 6291456 | tf_op jit(solution)/shard_map/slice | solution.py:29
  29.1 2.0 %reshape_squeeze.9 = f32[4096,64]{1,0:T(8,128)S(1)} reshape(f32[1,64,4096]{2,1,0:T(8,128)} %get-tuple-element.18) | data formatting | bytes 2097152 | tf_op jit(solution)/shard_map/reshape;squeeze | solution.py:29
  31.1 3.9 %convolution_bitcast_fusion.2 = f32[4096,256]{0,1:T(8,128)} fusion(f32[4096,64]{1,0:T(8,128)S(1)} %reshape_squeeze.9, bf16[1024,256]{1,0:T(8,128)(2,1)S(1)} %copy-done, s32[]{:T(128)S(6)} %select_n.40), kind=kOutput, calls=%fused_computation.3 | convolution fusion | flops 805306368 | bytes 6324228 | tf_op jit(solution)/shard_map/dot_general | solution.py:30
  35.0 5.6 %copy.23 = f32[4096,256]{1,0:T(8,128)} copy(f32[4096,256]{0,1:T(8,128)} %convolution_bitcast_fusion.2) | data formatting | bytes 8388608 | tf_op jit(solution)/shard_map/dot_general | solution.py:30
  40.6 2.0 %reshape_squeeze.10 = f32[4096,64]{1,0:T(8,128)S(1)} reshape(f32[1,64,4096]{2,1,0:T(8,128)} %get-tuple-element.19) | data formatting | bytes 2097152 | tf_op jit(solution)/shard_map/reshape;squeeze | solution.py:29
  42.6 3.9 %convolution_bitcast_fusion.1 = f32[4096,256]{0,1:T(8,128)} fusion(f32[4096,64]{1,0:T(8,128)S(1)} %reshape_squeeze.10, bf16[1024,256]{1,0:T(8,128)(2,1)S(1)} %copy-done, s32[]{:T(128)S(6)} %select_n.41), kind=kOutput, calls=%fused_computation.2 | convolution fusion | flops 805306368 | bytes 6324228 | tf_op jit(solution)/shard_map/dot_general | solution.py:30
  46.5 5.6 %copy.24 = f32[4096,256]{1,0:T(8,128)} copy(f32[4096,256]{0,1:T(8,128)} %convolution_bitcast_fusion.1) | data formatting | bytes 8388608 | tf_op jit(solution)/shard_map/dot_general | solution.py:30
  52.1 2.0 %reshape_squeeze.11 = f32[4096,64]{1,0:T(8,128)S(1)} reshape(f32[1,64,4096]{2,1,0:T(8,128)} %get-tuple-element.17) | data formatting | bytes 2097152 | tf_op jit(solution)/shard_map/reshape;squeeze | solution.py:29
  54.1 3.9 %convolution_bitcast_fusion = f32[4096,256]{0,1:T(8,128)} fusion(f32[4096,64]{1,0:T(8,128)S(1)} %reshape_squeeze.11, bf16[1024,256]{1,0:T(8,128)(2,1)S(1)} %copy-done, s32[]{:T(128)S(6)} %select_n.42), kind=kOutput, calls=%fused_computation.1 | convolution fusion | flops 805306368 | bytes 6324228 | tf_op jit(solution)/shard_map/dot_general | solution.py:30
  58.0 5.6 %copy.25 = f32[4096,256]{1,0:T(8,128)} copy(f32[4096,256]{0,1:T(8,128)} %convolution_bitcast_fusion) | data formatting | bytes 8388608 | tf_op jit(solution)/shard_map/dot_general | solution.py:30
  64.9 41.0 %all-gather.2.cloned.1.call-done = bf16[8192,256]{1,0:T(8,128)(2,1)} async-done(((bf16[64,256]{1,0:T(8,128)(2,1)}), bf16[8192,256]{1,0:T(8,128)(2,1)}) %all-gather.2.cloned.1.call-update) | async-done | bytes 4194320 | tf_op jit(solution)/shard_map/all_gather | solution.py:19
  107.3 7.9 %shard_map.73 = f32[64,256]{1,0:T(8,128)} custom-call(f32[3]{0:T(128)} %compare_select_fusion.1.scale_ref, bf16[3,64,256]{2,1,0:T(8,128)(2,1)} %pad_maximum_fusion.b_ref, f32[64,64,256]{2,1,0:T(8,128)} %bitcast.89, f32[64,64,256]{2,1,0:T(8,128)} %bitcast.90, f32[64,64,256]{2,1,0:T(8,128)} %bitcast.91), custom_call_target="tpu_custom_call" | custom-call | tf_op jit(solution)/shard_map/pallas_call | solution.py:57
  115.3 5.2 %fusion.27 = f32[256,256]{0,1:T(8,128)S(1)} fusion(bf16[8192,256]{1,0:T(8,128)(2,1)} %all-gather.2.cloned.1.call-done), kind=kOutput, calls=%fused_computation.74 | convolution fusion | flops 1073741824 | bytes 4456448 | tf_op jit(solution)/shard_map/dot_general | solution.py:36
  120.9 11.7 %custom-call.4 = f32[128,128]{1,0:T(8,128)S(1)} custom-call(f32[128,128]{1,0:T(8,128)S(1)} %fusion.11), custom_call_target="Cholesky" | custom-call | tf_op jit(solution)/shard_map/cholesky/custom-call.1 | solution.py:94
  134.1 0.9 fusion.22
  135.0 0.9 convolution_add_fusion.11
  138.6 4.0 %all-to-all-start.1 = ((f32[4,16,256]{2,1,0:T(8,128)}), f32[4,16,256]{2,1,0:T(8,128)S(1)}, u32[]{:S(2)}, u32[]{:S(2)}) async-start(f32[4,16,256]{2,1,0:T(8,128)} %bitcast.18), calls=%async_computation.1 | async-start | bytes 131072 | tf_op jit(solution)/shard_map/all_to_all | solution.py:35
  142.8 4.3 %all-to-all-done.1 = f32[4,16,256]{2,1,0:T(8,128)S(1)} async-done(((f32[4,16,256]{2,1,0:T(8,128)}), f32[4,16,256]{2,1,0:T(8,128)S(1)}, u32[]{:S(2)}, u32[]{:S(2)}) %all-to-all-start.1) | async-done | bytes 65568 | tf_op jit(solution)/shard_map/all_to_all | solution.py:35
  147.3 11.7 %custom-call.5 = f32[128,128]{1,0:T(8,128)S(1)} custom-call(f32[128,128]{1,0:T(8,128)S(1)} %broadcast_multiply_fusion), custom_call_target="Cholesky" | custom-call | tf_op jit(solution)/shard_map/cholesky/custom-call.1 | solution.py:98
  160.4 0.9 fusion.23
  161.4 0.9 convolution_add_fusion.5
  (56 shorter events, 15.0 us)
Async XLA Ops:
  6.5 24.6 %copy-start = (bf16[1024,256]{1,0:T(8,128)(2,1)S(1)}, bf16[1024,256]{1,0:T(8,128)(2,1)}, u32[]{:S(2)}) copy-start(bf16[1024,256]{1,0:T(8,128)(2,1)} %param.14) | copy-start | bytes 1572868
  6.5 99.3 %all-gather.2.cloned.1.call-start = ((), (), s32[]{:S(2)}) async-start(), calls=%async_computation.2 | async-start | bytes 4227072 | tf_op jit(solution)/shard_map/all_gather | solution.py:19
  58.0 6.3 %copy-start.1 = (s32[3]{0:T(128)S(1)}, s32[3]{0:T(128)}, u32[]{:S(2)}) copy-start(s32[3]{0:T(128)} %param.11) | copy-start | bytes 40
  138.6 8.5 %all-to-all-start.1 = ((f32[4,16,256]{2,1,0:T(8,128)}), f32[4,16,256]{2,1,0:T(8,128)S(1)}, u32[]{:S(2)}, u32[]{:S(2)}) async-start(f32[4,16,256]{2,1,0:T(8,128)} %bitcast.18), calls=%async_computation.1 | async-start | bytes 131072 | tf_op jit(solution)/shard_map/all_to_all | solution.py:35
Sparse Core Ops, SparseCore 0:
  16.5 89.3 all-gather.1

commit v8 on v7

--- a/solution.py
+++ b/solution.py
@@ -29,19 +29,30 @@
         flat_tile = tile_data[position].reshape(tile_edge * tile_edge, tile_edge)
         inner_sum = jnp.dot(flat_tile, c_block, precision=lax.Precision.HIGHEST)
         inners.append(inner_sum.reshape(tile_edge, tile_edge, rank_cols))
-    summed = weighted_sum(slot_scale, jnp.stack(b_blocks), inners)
-    summed, whole_b = lax.optimization_barrier((summed, whole_b))
+    summed, gram_b = weighted_sum(slot_scale, jnp.stack(b_blocks), whole_b, inners)
     pieces = summed.reshape(replicas, tile_edge // replicas, rank_cols)
     my_rows = lax.all_to_all(pieces, "rep", 0, 0).sum(0)
-    gram_b = jnp.dot(whole_b.T, whole_b, preferred_element_type=jnp.float32)
     gram_c = jnp.dot(factor_c.T, factor_c, preferred_element_type=jnp.float32)
     normal_matrix = gram_b * gram_c
     normal_inverse, my_rows = spd_inverse(normal_matrix, my_rows)
     return jnp.dot(my_rows, normal_inverse, precision=lax.Precision.HIGHEST)
 
 
-def weigh_kernel(scale_ref, b_ref, *refs):
-    inner_refs, out_ref = refs[:-1], refs[-1]
+def weigh_kernel(scale_ref, b_ref, whole_ref, *refs):
+    inner_refs, out_ref, gram_ref = refs[:-2], refs[-2], refs[-1]
+    chunk = whole_ref[...]
+    gram_part = lax.dot_general(
+        chunk, chunk, (((0,), (0,)), ((), ())), preferred_element_type=jnp.float32
+    )
+
+    @pl.when(pl.program_id(0) == 0)
+    def _():
+        gram_ref[...] = gram_part
+
+    @pl.when(pl.program_id(0) > 0)
+    def _():
+        gram_ref[...] = gram_ref[...] + gram_part
+
     total = jnp.zeros(out_ref.shape, jnp.float32)
     for slot, inner_ref in enumerate(inner_refs):
         second = b_ref[slot].astype(jnp.float32)
@@ -51,20 +62,29 @@
     out_ref[...] = total
 
 
-def weighted_sum(slot_scale, b_blocks, inners, rows=8):
+def weighted_sum(slot_scale, b_blocks, whole_b, inners, rows=8):
     edge, second, rank_cols = inners[0].shape
+    steps = edge // rows
     inner_spec = pl.BlockSpec((rows, second, rank_cols), lambda i: (i, 0, 0))
+    whole_rows = whole_b.shape[0] // steps
     return pl.pallas_call(
         weigh_kernel,
-        grid=(edge // rows,),
+        grid=(steps,),
         in_specs=[
             pl.BlockSpec(memory_space=pltpu.SMEM),
             pl.BlockSpec(b_blocks.shape, lambda i: (0, 0, 0)),
+            pl.BlockSpec((whole_rows, rank_cols), lambda i: (i, 0)),
         ]
         + [inner_spec] * len(inners),
-        out_specs=pl.BlockSpec((rows, rank_cols), lambda i: (i, 0)),
-        out_shape=jax.ShapeDtypeStruct((edge, rank_cols), jnp.float32),
-    )(slot_scale, b_blocks, *inners)
+        out_specs=[
+            pl.BlockSpec((rows, rank_cols), lambda i: (i, 0)),
+            pl.BlockSpec((rank_cols, rank_cols), lambda i: (0, 0)),
+        ],
+        out_shape=[
+            jax.ShapeDtypeStruct((edge, rank_cols), jnp.float32),
+            jax.ShapeDtypeStruct((rank_cols, rank_cols), jnp.float32),
+        ],
+    )(slot_scale, b_blocks, whole_b, *inners)
 
 
 def mm(left, right):

time: 174 us -> 172 us (0.989)
  matrix products: 27.3 us -> 22.1 us
  Pallas kernels: 7.94 us -> 10.2 us
    dot_general x1 -> x0, matrix products: 5.2 us -> none  [per_device(): gram_b = jnp.dot(whole_b.T, whole_b, preferred_element_type=jnp.float32)]
    pallas_call x1, Pallas kernels: 7.94 us -> 10.2 us  [weighted_sum(): pl.pallas_call(weigh_kernel, grid=(steps,), in_specs=[pl.BlockSpec(memory...]
where the time goes in v8:
time: 172 us; the launch traced here: 171 us
  waiting for transfers between devices  45.3 us (26%)
  local copies, waits for them, and re-layouts  32.8 us (19%)
  other arithmetic  29.2 us (17%)
  matrix products  22.1 us (13%)
  between operations  18.3 us (11%)
  Pallas kernels  10.2 us (6%)
  blocking collectives  9.04 us (5%)
  starting transfers between devices  3.97 us (2%)
    all_gather x1, waiting for transfers between devices, per_device(): whole_b = lax.all_gather(owned, 'tiles', axis=0, tiled=True)  41 us
    dot_general x3, local copies, waits for them, and re-layouts, per_device(): inner_sum = jnp.dot(flat_tile, c_block, precision=lax.Precision.HIGHEST)  16.8 us
    another operation x3, other arithmetic, spd_inverse(): top_inverse = lower_inverse(lax.linalg.cholesky(top))  12.4 us
    another operation x3, other arithmetic, spd_inverse(): bottom_inverse = lower_inverse(lax.linalg.cholesky(schur))  12.4 us
    dot_general x3, matrix products, per_device(): inner_sum = jnp.dot(flat_tile, c_block, precision=lax.Precision.HIGHEST)  11.7 us
    pallas_call x1, Pallas kernels, weighted_sum(): pl.pallas_call(weigh_kernel, grid=(steps,), in_specs=[pl.BlockSpec(memory...  10.2 us
    dot_general x29, matrix products, mm(): return jnp.dot(left, right, precision=lax.Precision.HIGHEST)  9.21 us
    all_to_all x1, blocking collectives, per_device(): owned = lax.all_to_all(copies, 'rep', 0, 0).reshape(-1, rank_cols)  9.04 us
  transfers between devices with their start and end apart: 2, of which 2 were waited for; matrix products, arithmetic and copies ran while one was open for 26% of the time, Pallas kernels for 0%

profile of v8, /device:TPU:1, one launch (start us, length us, event | category | flops | bytes accessed | tf_op | source)
XLA Modules:
  0.0 171.0 jit_solution(8300917449710545046)
XLA Ops:
  7.3 9.0 %all_to_all.10 = bf16[4,16,256]{2,1,0:T(8,128)(2,1)} all-to-all(bf16[4,16,256]{2,1,0:T(8,128)(2,1)S(1)} %broadcast_in_dim.4), channel_id=1, replica_groups=mesh['tiles'=128,'rep'=4] {'rep'}, dimensions={0} | all-to-all | bytes 65536 | tf_op jit(solution)/shard_map/all_to_all | solution.py:18
  17.2 1.3 gather_fusion
  21.9 1.5 fusion.25
  25.3 3.7 %fusion.24 = (f32[1,64,4096]{2,1,0:T(8,128)}, f32[1,64,4096]{2,1,0:T(8,128)}, f32[1,64,4096]{2,1,0:T(8,128)}) fusion(f32[3,64,4096]{2,1,0:T(8,128)} %param.8), kind=kLoop, calls=%fused_computation.71 | loop fusion | bytes 6291456 | tf_op jit(solution)/shard_map/slice | solution.py:29
  29.1 2.0 %reshape_squeeze.9 = f32[4096,64]{1,0:T(8,128)S(1)} reshape(f32[1,64,4096]{2,1,0:T(8,128)} %get-tuple-element.18) | data formatting | bytes 2097152 | tf_op jit(solution)/shard_map/reshape;squeeze | solution.py:29
  31.1 3.9 %convolution_bitcast_fusion.2 = f32[4096,256]{0,1:T(8,128)} fusion(f32[4096,64]{1,0:T(8,128)S(1)} %reshape_squeeze.9, bf16[1024,256]{1,0:T(8,128)(2,1)S(1)} %copy-done, s32[]{:T(128)S(6)} %select_n.40), kind=kOutput, calls=%fused_computation.3 | convolution fusion | flops 805306368 | bytes 6324228 | tf_op jit(solution)/shard_map/dot_general | solution.py:30
  35.0 5.6 %copy.23 = f32[4096,256]{1,0:T(8,128)} copy(f32[4096,256]{0,1:T(8,128)} %convolution_bitcast_fusion.2) | data formatting | bytes 8388608 | tf_op jit(solution)/shard_map/dot_general | solution.py:30
  40.6 2.0 %reshape_squeeze.10 = f32[4096,64]{1,0:T(8,128)S(1)} reshape(f32[1,64,4096]{2,1,0:T(8,128)} %get-tuple-element.19) | data formatting | bytes 2097152 | tf_op jit(solution)/shard_map/reshape;squeeze | solution.py:29
  42.6 3.9 %convolution_bitcast_fusion.1 = f32[4096,256]{0,1:T(8,128)} fusion(f32[4096,64]{1,0:T(8,128)S(1)} %reshape_squeeze.10, bf16[1024,256]{1,0:T(8,128)(2,1)S(1)} %copy-done, s32[]{:T(128)S(6)} %select_n.41), kind=kOutput, calls=%fused_computation.2 | convolution fusion | flops 805306368 | bytes 6324228 | tf_op jit(solution)/shard_map/dot_general | solution.py:30
  46.5 5.6 %copy.24 = f32[4096,256]{1,0:T(8,128)} copy(f32[4096,256]{0,1:T(8,128)} %convolution_bitcast_fusion.1) | data formatting | bytes 8388608 | tf_op jit(solution)/shard_map/dot_general | solution.py:30
  52.1 2.0 %reshape_squeeze.11 = f32[4096,64]{1,0:T(8,128)S(1)} reshape(f32[1,64,4096]{2,1,0:T(8,128)} %get-tuple-element.17) | data formatting | bytes 2097152 | tf_op jit(solution)/shard_map/reshape;squeeze | solution.py:29
  54.1 3.9 %convolution_bitcast_fusion = f32[4096,256]{0,1:T(8,128)} fusion(f32[4096,64]{1,0:T(8,128)S(1)} %reshape_squeeze.11, bf16[1024,256]{1,0:T(8,128)(2,1)S(1)} %copy-done, s32[]{:T(128)S(6)} %select_n.42), kind=kOutput, calls=%fused_computation.1 | convolution fusion | flops 805306368 | bytes 6324228 | tf_op jit(solution)/shard_map/dot_general | solution.py:30
  58.0 5.6 %copy.25 = f32[4096,256]{1,0:T(8,128)} copy(f32[4096,256]{0,1:T(8,128)} %convolution_bitcast_fusion) | data formatting | bytes 8388608 | tf_op jit(solution)/shard_map/dot_general | solution.py:30
  64.8 41.0 %all-gather.2.cloned.1.call-done.whole_ref = bf16[8192,256]{1,0:T(8,128)(2,1)} async-done(((bf16[64,256]{1,0:T(8,128)(2,1)}), bf16[8192,256]{1,0:T(8,128)(2,1)}) %all-gather.2.cloned.1.call-update) | async-done | bytes 4194320 | tf_op jit(solution)/shard_map/all_gather | solution.py:19
  107.3 10.2 %shard_map.73 = (f32[64,256]{1,0:T(8,128)}, f32[256,256]{1,0:T(8,128)}) custom-call(f32[3]{0:T(128)} %compare_select_fusion.1.scale_ref, bf16[3,64,256]{2,1,0:T(8,128)(2,1)} %pad_maximum_fusion.b_ref, bf16[8192,256]{1,0:T(8,128)(2,1)} %all-gather.2.cloned.1.call-done.whole_ref, f32[64,64,256]{2,1,0:T(8,128)} %bitcast.87, f32[64,64,256]{2,1,0:T(8,128)} %bitcast.88, ...), custom_call_target="tpu_custom_call" | custom-call | tf_op jit(solution)/shard_map/pallas_call | solution.py:70
  117.5 1.1 copy.26
  119.1 11.7 %custom-call.4 = f32[128,128]{1,0:T(8,128)S(1)} custom-call(f32[128,128]{1,0:T(8,128)S(1)} %fusion.11), custom_call_target="Cholesky" | custom-call | tf_op jit(solution)/shard_map/cholesky/custom-call.1 | solution.py:114
  132.2 0.9 fusion.22
  133.2 0.9 convolution_add_fusion.11
  136.8 4.0 %all-to-all-start.1 = ((f32[4,16,256]{2,1,0:T(8,128)}), f32[4,16,256]{2,1,0:T(8,128)S(1)}, u32[]{:S(2)}, u32[]{:S(2)}) async-start(f32[4,16,256]{2,1,0:T(8,128)} %bitcast.18), calls=%async_computation.1 | async-start | bytes 131072 | tf_op jit(solution)/shard_map/all_to_all | solution.py:34
  141.0 4.3 %all-to-all-done.1 = f32[4,16,256]{2,1,0:T(8,128)S(1)} async-done(((f32[4,16,256]{2,1,0:T(8,128)}), f32[4,16,256]{2,1,0:T(8,128)S(1)}, u32[]{:S(2)}, u32[]{:S(2)}) %all-to-all-start.1) | async-done | bytes 65568 | tf_op jit(solution)/shard_map/all_to_all | solution.py:34
  145.5 11.7 %custom-call.5 = f32[128,128]{1,0:T(8,128)S(1)} custom-call(f32[128,128]{1,0:T(8,128)S(1)} %broadcast_multiply_fusion), custom_call_target="Cholesky" | custom-call | tf_op jit(solution)/shard_map/cholesky/custom-call.1 | solution.py:118
  158.6 0.9 fusion.23
  159.5 0.9 convolution_add_fusion.5
  (56 shorter events, 15.0 us)
Async XLA Ops:
  6.5 24.6 %copy-start = (bf16[1024,256]{1,0:T(8,128)(2,1)S(1)}, bf16[1024,256]{1,0:T(8,128)(2,1)}, u32[]{:S(2)}) copy-start(bf16[1024,256]{1,0:T(8,128)(2,1)} %param.14) | copy-start | bytes 1572868
  6.5 99.3 %all-gather.2.cloned.1.call-start = ((), (), s32[]{:S(2)}) async-start(), calls=%async_computation.2 | async-start | bytes 4227072 | tf_op jit(solution)/shard_map/all_gather | solution.py:19
  58.0 6.3 %copy-start.1 = (s32[3]{0:T(128)S(1)}, s32[3]{0:T(128)}, u32[]{:S(2)}) copy-start(s32[3]{0:T(128)} %param.11) | copy-start | bytes 40
  136.8 8.4 %all-to-all-start.1 = ((f32[4,16,256]{2,1,0:T(8,128)}), f32[4,16,256]{2,1,0:T(8,128)S(1)}, u32[]{:S(2)}, u32[]{:S(2)}) async-start(f32[4,16,256]{2,1,0:T(8,128)} %bitcast.18), calls=%async_computation.1 | async-start | bytes 131072 | tf_op jit(solution)/shard_map/all_to_all | solution.py:34
Sparse Core Ops, SparseCore 0:
  16.5 89.3 all-gather.1

commit v9 on v8

--- a/solution.py
+++ b/solution.py
@@ -62,7 +62,7 @@
     out_ref[...] = total
 
 
-def weighted_sum(slot_scale, b_blocks, whole_b, inners, rows=8):
+def weighted_sum(slot_scale, b_blocks, whole_b, inners, rows=32):
     edge, second, rank_cols = inners[0].shape
     steps = edge // rows
     inner_spec = pl.BlockSpec((rows, second, rank_cols), lambda i: (i, 0, 0))

time: 172 us -> 170 us (0.988)
  Pallas kernels: 10.2 us -> 8.01 us
    pallas_call x1, Pallas kernels: 10.2 us -> 8.01 us  [weighted_sum(): pl.pallas_call(weigh_kernel, grid=(steps,), in_specs=[pl.BlockSpec(memory...]
where the time goes in v9:
time: 170 us; the launch traced here: 169 us
  waiting for transfers between devices  45.3 us (27%)
  local copies, waits for them, and re-layouts  32.8 us (19%)
  other arithmetic  29.2 us (17%)
  matrix products  22.1 us (13%)
  between operations  18.3 us (11%)
  blocking collectives  9.04 us (5%)
  Pallas kernels  8.01 us (5%)
  starting transfers between devices  3.99 us (2%)
    all_gather x1, waiting for transfers between devices, per_device(): whole_b = lax.all_gather(owned, 'tiles', axis=0, tiled=True)  41 us
    dot_general x3, local copies, waits for them, and re-layouts, per_device(): inner_sum = jnp.dot(flat_tile, c_block, precision=lax.Precision.HIGHEST)  16.8 us
    another operation x3, other arithmetic, spd_inverse(): top_inverse = lower_inverse(lax.linalg.cholesky(top))  12.4 us
    another operation x3, other arithmetic, spd_inverse(): bottom_inverse = lower_inverse(lax.linalg.cholesky(schur))  12.4 us
    dot_general x3, matrix products, per_device(): inner_sum = jnp.dot(flat_tile, c_block, precision=lax.Precision.HIGHEST)  11.7 us
    dot_general x29, matrix products, mm(): return jnp.dot(left, right, precision=lax.Precision.HIGHEST)  9.21 us
    all_to_all x1, blocking collectives, per_device(): owned = lax.all_to_all(copies, 'rep', 0, 0).reshape(-1, rank_cols)  9.04 us
    pallas_call x1, Pallas kernels, weighted_sum(): pl.pallas_call(weigh_kernel, grid=(steps,), in_specs=[pl.BlockSpec(memory...  8.01 us
  transfers between devices with their start and end apart: 2, of which 2 were waited for; matrix products, arithmetic and copies ran while one was open for 26% of the time, Pallas kernels for 0%

profile of v9, /device:TPU:1, one launch (start us, length us, event | category | flops | bytes accessed | tf_op | source)
XLA Modules:
  0.0 168.8 jit_solution(3178940777138724405)
XLA Ops:
  7.3 9.0 %all_to_all.10 = bf16[4,16,256]{2,1,0:T(8,128)(2,1)} all-to-all(bf16[4,16,256]{2,1,0:T(8,128)(2,1)S(1)} %broadcast_in_dim.4), channel_id=1, replica_groups=mesh['tiles'=128,'rep'=4] {'rep'}, dimensions={0} | all-to-all | bytes 65536 | tf_op jit(solution)/shard_map/all_to_all | solution.py:18
  17.2 1.3 gather_fusion
  21.9 1.5 fusion.25
  25.3 3.7 %fusion.24 = (f32[1,64,4096]{2,1,0:T(8,128)}, f32[1,64,4096]{2,1,0:T(8,128)}, f32[1,64,4096]{2,1,0:T(8,128)}) fusion(f32[3,64,4096]{2,1,0:T(8,128)} %param.8), kind=kLoop, calls=%fused_computation.71 | loop fusion | bytes 6291456 | tf_op jit(solution)/shard_map/slice | solution.py:29
  29.1 2.0 %reshape_squeeze.9 = f32[4096,64]{1,0:T(8,128)S(1)} reshape(f32[1,64,4096]{2,1,0:T(8,128)} %get-tuple-element.18) | data formatting | bytes 2097152 | tf_op jit(solution)/shard_map/reshape;squeeze | solution.py:29
  31.1 3.9 %convolution_bitcast_fusion.2 = f32[4096,256]{0,1:T(8,128)} fusion(f32[4096,64]{1,0:T(8,128)S(1)} %reshape_squeeze.9, bf16[1024,256]{1,0:T(8,128)(2,1)S(1)} %copy-done, s32[]{:T(128)S(6)} %select_n.40), kind=kOutput, calls=%fused_computation.3 | convolution fusion | flops 805306368 | bytes 6324228 | tf_op jit(solution)/shard_map/dot_general | solution.py:30
  35.0 5.6 %copy.23 = f32[4096,256]{1,0:T(8,128)} copy(f32[4096,256]{0,1:T(8,128)} %convolution_bitcast_fusion.2) | data formatting | bytes 8388608 | tf_op jit(solution)/shard_map/dot_general | solution.py:30
  40.6 2.0 %reshape_squeeze.10 = f32[4096,64]{1,0:T(8,128)S(1)} reshape(f32[1,64,4096]{2,1,0:T(8,128)} %get-tuple-element.19) | data formatting | bytes 2097152 | tf_op jit(solution)/shard_map/reshape;squeeze | solution.py:29
  42.6 3.9 %convolution_bitcast_fusion.1 = f32[4096,256]{0,1:T(8,128)} fusion(f32[4096,64]{1,0:T(8,128)S(1)} %reshape_squeeze.10, bf16[1024,256]{1,0:T(8,128)(2,1)S(1)} %copy-done, s32[]{:T(128)S(6)} %select_n.41), kind=kOutput, calls=%fused_computation.2 | convolution fusion | flops 805306368 | bytes 6324228 | tf_op jit(solution)/shard_map/dot_general | solution.py:30
  46.5 5.6 %copy.24 = f32[4096,256]{1,0:T(8,128)} copy(f32[4096,256]{0,1:T(8,128)} %convolution_bitcast_fusion.1) | data formatting | bytes 8388608 | tf_op jit(solution)/shard_map/dot_general | solution.py:30
  52.1 2.0 %reshape_squeeze.11 = f32[4096,64]{1,0:T(8,128)S(1)} reshape(f32[1,64,4096]{2,1,0:T(8,128)} %get-tuple-element.17) | data formatting | bytes 2097152 | tf_op jit(solution)/shard_map/reshape;squeeze | solution.py:29
  54.1 3.9 %convolution_bitcast_fusion = f32[4096,256]{0,1:T(8,128)} fusion(f32[4096,64]{1,0:T(8,128)S(1)} %reshape_squeeze.11, bf16[1024,256]{1,0:T(8,128)(2,1)S(1)} %copy-done, s32[]{:T(128)S(6)} %select_n.42), kind=kOutput, calls=%fused_computation.1 | convolution fusion | flops 805306368 | bytes 6324228 | tf_op jit(solution)/shard_map/dot_general | solution.py:30
  58.0 5.6 %copy.25 = f32[4096,256]{1,0:T(8,128)} copy(f32[4096,256]{0,1:T(8,128)} %convolution_bitcast_fusion) | data formatting | bytes 8388608 | tf_op jit(solution)/shard_map/dot_general | solution.py:30
  64.8 41.0 %all-gather.2.cloned.1.call-done.whole_ref = bf16[8192,256]{1,0:T(8,128)(2,1)} async-done(((bf16[64,256]{1,0:T(8,128)(2,1)}), bf16[8192,256]{1,0:T(8,128)(2,1)}) %all-gather.2.cloned.1.call-update) | async-done | bytes 4194320 | tf_op jit(solution)/shard_map/all_gather | solution.py:19
  107.3 8.0 %shard_map.73 = (f32[64,256]{1,0:T(8,128)}, f32[256,256]{1,0:T(8,128)}) custom-call(f32[3]{0:T(128)} %compare_select_fusion.1.scale_ref, bf16[3,64,256]{2,1,0:T(8,128)(2,1)} %pad_maximum_fusion.b_ref, bf16[8192,256]{1,0:T(8,128)(2,1)} %all-gather.2.cloned.1.call-done.whole_ref, f32[64,64,256]{2,1,0:T(8,128)} %bitcast.87, f32[64,64,256]{2,1,0:T(8,128)} %bitcast.88, ...), custom_call_target="tpu_custom_call" | custom-call | tf_op jit(solution)/shard_map/pallas_call | solution.py:70
  115.3 1.1 copy.26
  116.9 11.7 %custom-call.4 = f32[128,128]{1,0:T(8,128)S(1)} custom-call(f32[128,128]{1,0:T(8,128)S(1)} %fusion.11), custom_call_target="Cholesky" | custom-call | tf_op jit(solution)/shard_map/cholesky/custom-call.1 | solution.py:114
  130.0 0.9 fusion.22
  131.0 0.9 convolution_add_fusion.11
  134.6 4.0 %all-to-all-start.1 = ((f32[4,16,256]{2,1,0:T(8,128)}), f32[4,16,256]{2,1,0:T(8,128)S(1)}, u32[]{:S(2)}, u32[]{:S(2)}) async-start(f32[4,16,256]{2,1,0:T(8,128)} %bitcast.18), calls=%async_computation.1 | async-start | bytes 131072 | tf_op jit(solution)/shard_map/all_to_all | solution.py:34
  138.8 4.3 %all-to-all-done.1 = f32[4,16,256]{2,1,0:T(8,128)S(1)} async-done(((f32[4,16,256]{2,1,0:T(8,128)}), f32[4,16,256]{2,1,0:T(8,128)S(1)}, u32[]{:S(2)}, u32[]{:S(2)}) %all-to-all-start.1) | async-done | bytes 65568 | tf_op jit(solution)/shard_map/all_to_all | solution.py:34
  143.3 11.7 %custom-call.5 = f32[128,128]{1,0:T(8,128)S(1)} custom-call(f32[128,128]{1,0:T(8,128)S(1)} %broadcast_multiply_fusion), custom_call_target="Cholesky" | custom-call | tf_op jit(solution)/shard_map/cholesky/custom-call.1 | solution.py:118
  156.4 0.9 fusion.23
  157.3 0.9 convolution_add_fusion.5
  (56 shorter events, 15.0 us)
Async XLA Ops:
  6.5 24.6 %copy-start = (bf16[1024,256]{1,0:T(8,128)(2,1)S(1)}, bf16[1024,256]{1,0:T(8,128)(2,1)}, u32[]{:S(2)}) copy-start(bf16[1024,256]{1,0:T(8,128)(2,1)} %param.14) | copy-start | bytes 1572868
  6.5 99.3 %all-gather.2.cloned.1.call-start = ((), (), s32[]{:S(2)}) async-start(), calls=%async_computation.2 | async-start | bytes 4227072 | tf_op jit(solution)/shard_map/all_gather | solution.py:19
  58.0 6.3 %copy-start.1 = (s32[3]{0:T(128)S(1)}, s32[3]{0:T(128)}, u32[]{:S(2)}) copy-start(s32[3]{0:T(128)} %param.11) | copy-start | bytes 40
  134.6 8.5 %all-to-all-start.1 = ((f32[4,16,256]{2,1,0:T(8,128)}), f32[4,16,256]{2,1,0:T(8,128)S(1)}, u32[]{:S(2)}, u32[]{:S(2)}) async-start(f32[4,16,256]{2,1,0:T(8,128)} %bitcast.18), calls=%async_computation.1 | async-start | bytes 131072 | tf_op jit(solution)/shard_map/all_to_all | solution.py:34
Sparse Core Ops, SparseCore 0:
  16.5 89.3 all-gather.1

commit v10 on v9

--- a/solution.py
+++ b/solution.py
@@ -56,7 +56,9 @@
     total = jnp.zeros(out_ref.shape, jnp.float32)
     for slot, inner_ref in enumerate(inner_refs):
         second = b_ref[slot].astype(jnp.float32)
-        partial_value = jnp.sum(inner_ref[...] * second[None], axis=1)
+        weighed = inner_ref[...] * second[None]
+        rows, width, rank_cols = weighed.shape
+        partial_value = weighed.reshape(rows, width // 8, 8, rank_cols).sum(axis=1).sum(axis=1)
         rounded = (partial_value * scale_ref[slot]).astype(jnp.bfloat16)
         total = total + rounded.astype(jnp.float32)
     out_ref[...] = total
@@ -111,11 +113,11 @@
     top = matrix[:half, :half]
     side = matrix[half:, :half]
     bottom = matrix[half:, half:]
-    top_inverse = lower_inverse(lax.linalg.cholesky(top))
+    top_inverse = lower_inverse(lax.linalg.cholesky(top, symmetrize_input=False))
     side_factor = mm(side, top_inverse.T)
     schur = bottom - mm(side_factor, side_factor.T)
     schur, carried = lax.optimization_barrier((schur, carried))
-    bottom_inverse = lower_inverse(lax.linalg.cholesky(schur))
+    bottom_inverse = lower_inverse(lax.linalg.cholesky(schur, symmetrize_input=False))
     corner = -mm(bottom_inverse, mm(side_factor, top_inverse))
     zeros = jnp.zeros((half, matrix.shape[0] - half), matrix.dtype)
     inverse = jnp.concatenate(

time: 170 us -> 169 us (level)
  no operation moved by 1% of the time
where the time goes in v10:
time: 169 us; the launch traced here: 168 us
  waiting for transfers between devices  45.3 us (27%)
  local copies, waits for them, and re-layouts  31.5 us (19%)
  other arithmetic  29.2 us (17%)
  matrix products  23 us (14%)
  between operations  18.2 us (11%)
  blocking collectives  9.04 us (5%)
  Pallas kernels  8 us (5%)
  starting transfers between devices  3.98 us (2%)
    all_gather x1, waiting for transfers between devices, per_device(): whole_b = lax.all_gather(owned, 'tiles', axis=0, tiled=True)  41 us
    dot_general x3, local copies, waits for them, and re-layouts, per_device(): inner_sum = jnp.dot(flat_tile, c_block, precision=lax.Precision.HIGHEST)  16.8 us
    another operation x3, other arithmetic, spd_inverse(): lax.linalg.cholesky(top, symmetrize_input=False)  12.4 us
    another operation x3, other arithmetic, spd_inverse(): lax.linalg.cholesky(schur, symmetrize_input=False)  12.4 us
    dot_general x3, matrix products, per_device(): inner_sum = jnp.dot(flat_tile, c_block, precision=lax.Precision.HIGHEST)  11.7 us
    dot_general x29, matrix products, mm(): return jnp.dot(left, right, precision=lax.Precision.HIGHEST)  9.2 us
    all_to_all x1, blocking collectives, per_device(): owned = lax.all_to_all(copies, 'rep', 0, 0).reshape(-1, rank_cols)  9.04 us
    pallas_call x1, Pallas kernels, weighted_sum(): pl.pallas_call(weigh_kernel, grid=(steps,), in_specs=[pl.BlockSpec(memory...  8 us
  transfers between devices with their start and end apart: 2, of which 2 were waited for; matrix products, arithmetic and copies ran while one was open for 26% of the time, Pallas kernels for 0%

profile of v10, /device:TPU:1, one launch (start us, length us, event | category | flops | bytes accessed | tf_op | source)
XLA Modules:
  0.0 168.3 jit_solution(12474671867241576551)
XLA Ops:
  7.3 9.0 %all_to_all.10 = bf16[4,16,256]{2,1,0:T(8,128)(2,1)} all-to-all(bf16[4,16,256]{2,1,0:T(8,128)(2,1)S(1)} %broadcast_in_dim.4), channel_id=1, replica_groups=mesh['tiles'=128,'rep'=4] {'rep'}, dimensions={0} | all-to-all | bytes 65536 | tf_op jit(solution)/shard_map/all_to_all | solution.py:18
  17.2 1.3 gather_fusion
  21.9 1.5 fusion.24
  25.3 3.7 %fusion.23 = (f32[1,64,4096]{2,1,0:T(8,128)}, f32[1,64,4096]{2,1,0:T(8,128)}, f32[1,64,4096]{2,1,0:T(8,128)}) fusion(f32[3,64,4096]{2,1,0:T(8,128)} %param.8), kind=kLoop, calls=%fused_computation.67 | loop fusion | bytes 6291456 | tf_op jit(solution)/shard_map/slice | solution.py:29
  29.1 2.0 %reshape_squeeze.9 = f32[4096,64]{1,0:T(8,128)S(1)} reshape(f32[1,64,4096]{2,1,0:T(8,128)} %get-tuple-element.18) | data formatting | bytes 2097152 | tf_op jit(solution)/shard_map/reshape;squeeze | solution.py:29
  31.1 3.9 %convolution_bitcast_fusion.2 = f32[4096,256]{0,1:T(8,128)} fusion(f32[4096,64]{1,0:T(8,128)S(1)} %reshape_squeeze.9, bf16[1024,256]{1,0:T(8,128)(2,1)S(1)} %copy-done, s32[]{:T(128)S(6)} %select_n.40), kind=kOutput, calls=%fused_computation.3 | convolution fusion | flops 805306368 | bytes 6324228 | tf_op jit(solution)/shard_map/dot_general | solution.py:30
  35.0 5.6 %copy.17 = f32[4096,256]{1,0:T(8,128)} copy(f32[4096,256]{0,1:T(8,128)} %convolution_bitcast_fusion.2) | data formatting | bytes 8388608 | tf_op jit(solution)/shard_map/dot_general | solution.py:30
  40.6 2.0 %reshape_squeeze.10 = f32[4096,64]{1,0:T(8,128)S(1)} reshape(f32[1,64,4096]{2,1,0:T(8,128)} %get-tuple-element.19) | data formatting | bytes 2097152 | tf_op jit(solution)/shard_map/reshape;squeeze | solution.py:29
  42.6 3.9 %convolution_bitcast_fusion.1 = f32[4096,256]{0,1:T(8,128)} fusion(f32[4096,64]{1,0:T(8,128)S(1)} %reshape_squeeze.10, bf16[1024,256]{1,0:T(8,128)(2,1)S(1)} %copy-done, s32[]{:T(128)S(6)} %select_n.41), kind=kOutput, calls=%fused_computation.2 | convolution fusion | flops 805306368 | bytes 6324228 | tf_op jit(solution)/shard_map/dot_general | solution.py:30
  46.5 5.6 %copy.18 = f32[4096,256]{1,0:T(8,128)} copy(f32[4096,256]{0,1:T(8,128)} %convolution_bitcast_fusion.1) | data formatting | bytes 8388608 | tf_op jit(solution)/shard_map/dot_general | solution.py:30
  52.1 2.0 %reshape_squeeze.11 = f32[4096,64]{1,0:T(8,128)S(1)} reshape(f32[1,64,4096]{2,1,0:T(8,128)} %get-tuple-element.17) | data formatting | bytes 2097152 | tf_op jit(solution)/shard_map/reshape;squeeze | solution.py:29
  54.1 3.9 %convolution_bitcast_fusion = f32[4096,256]{0,1:T(8,128)} fusion(f32[4096,64]{1,0:T(8,128)S(1)} %reshape_squeeze.11, bf16[1024,256]{1,0:T(8,128)(2,1)S(1)} %copy-done, s32[]{:T(128)S(6)} %select_n.42), kind=kOutput, calls=%fused_computation.1 | convolution fusion | flops 805306368 | bytes 6324228 | tf_op jit(solution)/shard_map/dot_general | solution.py:30
  58.0 5.6 %copy.19 = f32[4096,256]{1,0:T(8,128)} copy(f32[4096,256]{0,1:T(8,128)} %convolution_bitcast_fusion) | data formatting | bytes 8388608 | tf_op jit(solution)/shard_map/dot_general | solution.py:30
  64.8 41.0 %all-gather.2.cloned.1.call-done.whole_ref = bf16[8192,256]{1,0:T(8,128)(2,1)} async-done(((bf16[64,256]{1,0:T(8,128)(2,1)}), bf16[8192,256]{1,0:T(8,128)(2,1)}) %all-gather.2.cloned.1.call-update) | async-done | bytes 4194320 | tf_op jit(solution)/shard_map/all_gather | solution.py:19
  107.3 8.0 %shard_map.73 = (f32[64,256]{1,0:T(8,128)}, f32[256,256]{1,0:T(8,128)}) custom-call(f32[3]{0:T(128)} %compare_select_fusion.1.scale_ref, bf16[3,64,256]{2,1,0:T(8,128)(2,1)} %pad_maximum_fusion.b_ref, bf16[8192,256]{1,0:T(8,128)(2,1)} %all-gather.2.cloned.1.call-done.whole_ref, f32[64,64,256]{2,1,0:T(8,128)} %bitcast.81, f32[64,64,256]{2,1,0:T(8,128)} %bitcast.82, ...), custom_call_target="tpu_custom_call" | custom-call | tf_op jit(solution)/shard_map/pallas_call | solution.py:72
  115.3 1.3 convolution_multiply_fusion
  116.6 11.7 %custom-call.4 = f32[128,128]{1,0:T(8,128)S(1)} custom-call(f32[128,128]{1,0:T(8,128)S(1)} %slice.58), custom_call_target="Cholesky" | custom-call | tf_op jit(solution)/shard_map/cholesky/custom-call.1 | solution.py:116
  129.8 0.9 fusion.21
  130.7 0.9 convolution_add_fusion.11
  134.3 4.0 %all-to-all-start.1 = ((f32[4,16,256]{2,1,0:T(8,128)}), f32[4,16,256]{2,1,0:T(8,128)S(1)}, u32[]{:S(2)}, u32[]{:S(2)}) async-start(f32[4,16,256]{2,1,0:T(8,128)} %bitcast.17), calls=%async_computation.1 | async-start | bytes 131072 | tf_op jit(solution)/shard_map/all_to_all | solution.py:34
  138.5 4.3 %all-to-all-done.1 = f32[4,16,256]{2,1,0:T(8,128)S(1)} async-done(((f32[4,16,256]{2,1,0:T(8,128)}), f32[4,16,256]{2,1,0:T(8,128)S(1)}, u32[]{:S(2)}, u32[]{:S(2)}) %all-to-all-start.1) | async-done | bytes 65568 | tf_op jit(solution)/shard_map/all_to_all | solution.py:34
  142.7 11.7 %custom-call.5 = f32[128,128]{1,0:T(8,128)S(1)} custom-call(f32[128,128]{1,0:T(8,128)S(1)} %convolution_subtract_fusion), custom_call_target="Cholesky" | custom-call | tf_op jit(solution)/shard_map/cholesky/custom-call.1 | solution.py:120
  155.9 0.9 fusion.22
  156.8 0.9 convolution_add_fusion.5
  (49 shorter events, 14.3 us)
Async XLA Ops:
  6.5 24.6 %copy-start = (bf16[1024,256]{1,0:T(8,128)(2,1)S(1)}, bf16[1024,256]{1,0:T(8,128)(2,1)}, u32[]{:S(2)}) copy-start(bf16[1024,256]{1,0:T(8,128)(2,1)} %param.14) | copy-start | bytes 1572868
  6.5 99.3 %all-gather.2.cloned.1.call-start = ((), (), s32[]{:S(2)}) async-start(), calls=%async_computation.2 | async-start | bytes 4227072 | tf_op jit(solution)/shard_map/all_gather | solution.py:19
  58.0 6.3 %copy-start.1 = (s32[3]{0:T(128)S(1)}, s32[3]{0:T(128)}, u32[]{:S(2)}) copy-start(s32[3]{0:T(128)} %param.11) | copy-start | bytes 40
  134.3 8.5 %all-to-all-start.1 = ((f32[4,16,256]{2,1,0:T(8,128)}), f32[4,16,256]{2,1,0:T(8,128)S(1)}, u32[]{:S(2)}, u32[]{:S(2)}) async-start(f32[4,16,256]{2,1,0:T(8,128)} %bitcast.17), calls=%async_computation.1 | async-start | bytes 131072 | tf_op jit(solution)/shard_map/all_to_all | solution.py:34
Sparse Core Ops, SparseCore 0:
  16.5 89.3 all-gather.1

commit v11 on v10

--- a/solution.py
+++ b/solution.py
@@ -18,18 +18,14 @@
     owned = lax.all_to_all(copies, "rep", 0, 0).reshape(-1, rank_cols)
     whole_b = lax.all_gather(owned, "tiles", axis=0, tiled=True)
     inners = []
-    b_blocks = []
     for position in range(slot_total):
         c_block = lax.dynamic_slice_in_dim(
             factor_c, tile_coords[position, 2] * tile_edge, tile_edge, 0
         ).astype(jnp.float32)
-        b_blocks.append(
-            lax.dynamic_slice_in_dim(whole_b, stored_second[position] * tile_edge, tile_edge, 0)
-        )
         flat_tile = tile_data[position].reshape(tile_edge * tile_edge, tile_edge)
         inner_sum = jnp.dot(flat_tile, c_block, precision=lax.Precision.HIGHEST)
         inners.append(inner_sum.reshape(tile_edge, tile_edge, rank_cols))
-    summed, gram_b = weighted_sum(slot_scale, jnp.stack(b_blocks), whole_b, inners)
+    summed, gram_b = weighted_sum(stored_second, slot_scale, whole_b, inners)
     pieces = summed.reshape(replicas, tile_edge // replicas, rank_cols)
     my_rows = lax.all_to_all(pieces, "rep", 0, 0).sum(0)
     gram_c = jnp.dot(factor_c.T, factor_c, preferred_element_type=jnp.float32)
@@ -38,8 +34,11 @@
     return jnp.dot(my_rows, normal_inverse, precision=lax.Precision.HIGHEST)
 
 
-def weigh_kernel(scale_ref, b_ref, whole_ref, *refs):
-    inner_refs, out_ref, gram_ref = refs[:-2], refs[-2], refs[-1]
+def weigh_kernel(place_ref, scale_ref, whole_ref, *refs):
+    del place_ref
+    slots = (len(refs) - 2) // 2
+    b_refs, inner_refs = refs[:slots], refs[slots:-2]
+    out_ref, gram_ref = refs[-2], refs[-1]
     chunk = whole_ref[...]
     gram_part = lax.dot_general(
         chunk, chunk, (((0,), (0,)), ((), ())), preferred_element_type=jnp.float32
@@ -55,7 +54,7 @@
 
     total = jnp.zeros(out_ref.shape, jnp.float32)
     for slot, inner_ref in enumerate(inner_refs):
-        second = b_ref[slot].astype(jnp.float32)
+        second = b_refs[slot][...].astype(jnp.float32)
         weighed = inner_ref[...] * second[None]
         rows, width, rank_cols = weighed.shape
         partial_value = weighed.reshape(rows, width // 8, 8, rank_cols).sum(axis=1).sum(axis=1)
@@ -64,29 +63,36 @@
     out_ref[...] = total
 
 
-def weighted_sum(slot_scale, b_blocks, whole_b, inners, rows=32):
+def weighted_sum(place, slot_scale, whole_b, inners, rows=32):
     edge, second, rank_cols = inners[0].shape
     steps = edge // rows
-    inner_spec = pl.BlockSpec((rows, second, rank_cols), lambda i: (i, 0, 0))
     whole_rows = whole_b.shape[0] // steps
-    return pl.pallas_call(
-        weigh_kernel,
+    b_specs = [
+        pl.BlockSpec((second, rank_cols), lambda i, place_ref, slot=slot: (place_ref[slot], 0))
+        for slot in range(len(inners))
+    ]
+    grid_spec = pltpu.PrefetchScalarGridSpec(
+        num_scalar_prefetch=1,
         grid=(steps,),
         in_specs=[
             pl.BlockSpec(memory_space=pltpu.SMEM),
-            pl.BlockSpec(b_blocks.shape, lambda i: (0, 0, 0)),
-            pl.BlockSpec((whole_rows, rank_cols), lambda i: (i, 0)),
+            pl.BlockSpec((whole_rows, rank_cols), lambda i, place_ref: (i, 0)),
         ]
-        + [inner_spec] * len(inners),
+        + b_specs
+        + [pl.BlockSpec((rows, second, rank_cols), lambda i, place_ref: (i, 0, 0))] * len(inners),
         out_specs=[
-            pl.BlockSpec((rows, rank_cols), lambda i: (i, 0)),
-            pl.BlockSpec((rank_cols, rank_cols), lambda i: (0, 0)),
+            pl.BlockSpec((rows, rank_cols), lambda i, place_ref: (i, 0)),
+            pl.BlockSpec((rank_cols, rank_cols), lambda i, place_ref: (0, 0)),
         ],
+    )
+    return pl.pallas_call(
+        weigh_kernel,
+        grid_spec=grid_spec,
         out_shape=[
             jax.ShapeDtypeStruct((edge, rank_cols), jnp.float32),
             jax.ShapeDtypeStruct((rank_cols, rank_cols), jnp.float32),
         ],
-    )(slot_scale, b_blocks, whole_b, *inners)
+    )(place, slot_scale, whole_b, *([whole_b] * len(inners)), *inners)
 
 
 def mm(left, right):

time: 169 us -> 168 us (level)
  waiting for transfers between devices: 45.3 us -> 49.3 us
  local copies, waits for them, and re-layouts: 31.5 us -> 29.5 us
  between operations: 18.2 us -> 16.3 us
    all_gather x1, waiting for transfers between devices: 41 us -> 45 us  [per_device(): whole_b = lax.all_gather(owned, 'tiles', axis=0, tiled=True)]
  transfers between devices with their start and end apart: 2 -> 2, of which waited for: 2 -> 2; matrix products, arithmetic and copies ran while one was open for 26% -> 25% of each run, Pallas kernels for 0% -> 0%
where the time goes in v11:
time: 168 us
  waiting for transfers between devices  49.3 us (29%)
  local copies, waits for them, and re-layouts  29.5 us (18%)
  other arithmetic  27.7 us (16%)
  matrix products  23 us (14%)
  between operations  16.3 us (10%)
  blocking collectives  9.04 us (5%)
  Pallas kernels  8.71 us (5%)
  starting transfers between devices  3.98 us (2%)
    all_gather x1, waiting for transfers between devices, per_device(): whole_b = lax.all_gather(owned, 'tiles', axis=0, tiled=True)  45 us
    dot_general x3, local copies, waits for them, and re-layouts, per_device(): inner_sum = jnp.dot(flat_tile, c_block, precision=lax.Precision.HIGHEST)  16.9 us
    another operation x3, other arithmetic, spd_inverse(): lax.linalg.cholesky(schur, symmetrize_input=False)  12.4 us
    another operation x3, other arithmetic, spd_inverse(): lax.linalg.cholesky(top, symmetrize_input=False)  12.4 us
    dot_general x3, matrix products, per_device(): inner_sum = jnp.dot(flat_tile, c_block, precision=lax.Precision.HIGHEST)  11.7 us
    dot_general x29, matrix products, mm(): return jnp.dot(left, right, precision=lax.Precision.HIGHEST)  9.2 us
    all_to_all x1, blocking collectives, per_device(): owned = lax.all_to_all(copies, 'rep', 0, 0).reshape(-1, rank_cols)  9.04 us
    pallas_call x1, Pallas kernels, weighted_sum(): pl.pallas_call(weigh_kernel, grid_spec=grid_spec, out_shape=[jax.ShapeDty...  8.71 us
  transfers between devices with their start and end apart: 2, of which 2 were waited for; matrix products, arithmetic and copies ran while one was open for 25% of the time, Pallas kernels for 0%

profile of v11, /device:TPU:1, one launch (start us, length us, event | category | flops | bytes accessed | tf_op | source)
XLA Modules:
  0.0 167.5 jit_solution(17742791742047486372)
XLA Ops:
  7.3 9.0 %all_to_all.10 = bf16[4,16,256]{2,1,0:T(8,128)(2,1)} all-to-all(bf16[4,16,256]{2,1,0:T(8,128)(2,1)S(1)} %broadcast_in_dim.4), channel_id=1, replica_groups=mesh['tiles'=128,'rep'=4] {'rep'}, dimensions={0} | all-to-all | bytes 65536 | tf_op jit(solution)/shard_map/all_to_all | solution.py:18
  16.4 1.5 fusion.24
  19.8 3.7 %fusion.23 = (f32[1,64,4096]{2,1,0:T(8,128)}, f32[1,64,4096]{2,1,0:T(8,128)}, f32[1,64,4096]{2,1,0:T(8,128)}) fusion(f32[3,64,4096]{2,1,0:T(8,128)} %param.8), kind=kLoop, calls=%fused_computation.63 | loop fusion | bytes 6291456 | tf_op jit(solution)/shard_map/slice | solution.py:25
  23.5 2.0 %reshape_squeeze.11 = f32[4096,64]{1,0:T(8,128)S(1)} reshape(f32[1,64,4096]{2,1,0:T(8,128)} %get-tuple-element.14) | data formatting | bytes 2097152 | tf_op jit(solution)/shard_map/reshape;squeeze | solution.py:25
  25.5 3.9 %convolution_bitcast_fusion = f32[4096,256]{0,1:T(8,128)} fusion(f32[4096,64]{1,0:T(8,128)S(1)} %reshape_squeeze.11, bf16[1024,256]{1,0:T(8,128)(2,1)S(1)} %copy-done, s32[]{:T(128)S(6)} %select_n.30), kind=kOutput, calls=%fused_computation.1 | convolution fusion | flops 805306368 | bytes 6324228 | tf_op jit(solution)/shard_map/dot_general | solution.py:26
  29.4 5.6 %copy.19 = f32[4096,256]{1,0:T(8,128)} copy(f32[4096,256]{0,1:T(8,128)} %convolution_bitcast_fusion) | data formatting | bytes 8388608 | tf_op jit(solution)/shard_map/dot_general | solution.py:26
  35.0 2.0 %reshape_squeeze.9 = f32[4096,64]{1,0:T(8,128)S(1)} reshape(f32[1,64,4096]{2,1,0:T(8,128)} %get-tuple-element.15) | data formatting | bytes 2097152 | tf_op jit(solution)/shard_map/reshape;squeeze | solution.py:25
  37.1 3.9 %convolution_bitcast_fusion.2 = f32[4096,256]{0,1:T(8,128)} fusion(f32[4096,64]{1,0:T(8,128)S(1)} %reshape_squeeze.9, bf16[1024,256]{1,0:T(8,128)(2,1)S(1)} %copy-done, s32[]{:T(128)S(6)} %select_n.28), kind=kOutput, calls=%fused_computation.3 | convolution fusion | flops 805306368 | bytes 6324228 | tf_op jit(solution)/shard_map/dot_general | solution.py:26
  41.0 5.6 %copy.17 = f32[4096,256]{1,0:T(8,128)} copy(f32[4096,256]{0,1:T(8,128)} %convolution_bitcast_fusion.2) | data formatting | bytes 8388608 | tf_op jit(solution)/shard_map/dot_general | solution.py:26
  46.6 2.0 %reshape_squeeze.10 = f32[4096,64]{1,0:T(8,128)S(1)} reshape(f32[1,64,4096]{2,1,0:T(8,128)} %get-tuple-element.16) | data formatting | bytes 2097152 | tf_op jit(solution)/shard_map/reshape;squeeze | solution.py:25
  48.6 3.9 %convolution_bitcast_fusion.1 = f32[4096,256]{0,1:T(8,128)} fusion(f32[4096,64]{1,0:T(8,128)S(1)} %reshape_squeeze.10, bf16[1024,256]{1,0:T(8,128)(2,1)S(1)} %copy-done, s32[]{:T(128)S(6)} %select_n.29), kind=kOutput, calls=%fused_computation.2 | convolution fusion | flops 805306368 | bytes 6324228 | tf_op jit(solution)/shard_map/dot_general | solution.py:26
  52.4 5.7 %copy.18 = f32[4096,256]{1,0:T(8,128)} copy(f32[4096,256]{0,1:T(8,128)} %convolution_bitcast_fusion.1) | data formatting | bytes 8388608 | tf_op jit(solution)/shard_map/dot_general | solution.py:26
  60.8 45.0 %all-gather.2.cloned.1.call-done.whole_ref.refs_0_.refs_1_.refs_2_ = bf16[8192,256]{1,0:T(8,128)(2,1)} async-done(((bf16[64,256]{1,0:T(8,128)(2,1)}), bf16[8192,256]{1,0:T(8,128)(2,1)}) %all-gather.2.cloned.1.call-update) | async-done | bytes 4194320 | tf_op jit(solution)/shard_map/all_gather | solution.py:19
  105.9 8.7 %shard_map.73 = (f32[64,256]{1,0:T(8,128)}, f32[256,256]{1,0:T(8,128)}) custom-call(s32[3]{0:T(128)} %broadcast_select_fusion.place_ref, f32[3]{0:T(128)} %compare_select_fusion.1.scale_ref, bf16[8192,256]{1,0:T(8,128)(2,1)} %all-gather.2.cloned.1.call-done.whole_ref.refs_0_.refs_1_.refs_2_, ...), custom_call_target="tpu_custom_call" | custom-call | tf_op jit(solution)/shard_map/pallas_call | solution.py:88
  114.6 1.3 convolution_multiply_fusion
  115.9 11.7 %custom-call.4 = f32[128,128]{1,0:T(8,128)S(1)} custom-call(f32[128,128]{1,0:T(8,128)S(1)} %slice.46), custom_call_target="Cholesky" | custom-call | tf_op jit(solution)/shard_map/cholesky/custom-call.1 | solution.py:122
  129.0 0.9 fusion.21
  130.0 0.9 convolution_add_fusion.11
  133.5 4.0 %all-to-all-start.1 = ((f32[4,16,256]{2,1,0:T(8,128)}), f32[4,16,256]{2,1,0:T(8,128)S(1)}, u32[]{:S(2)}, u32[]{:S(2)}) async-start(f32[4,16,256]{2,1,0:T(8,128)} %bitcast.11), calls=%async_computation.1 | async-start | bytes 131072 | tf_op jit(solution)/shard_map/all_to_all | solution.py:30
  137.7 4.3 %all-to-all-done.1 = f32[4,16,256]{2,1,0:T(8,128)S(1)} async-done(((f32[4,16,256]{2,1,0:T(8,128)}), f32[4,16,256]{2,1,0:T(8,128)S(1)}, u32[]{:S(2)}, u32[]{:S(2)}) %all-to-all-start.1) | async-done | bytes 65568 | tf_op jit(solution)/shard_map/all_to_all | solution.py:30
  142.0 11.7 %custom-call.5 = f32[128,128]{1,0:T(8,128)S(1)} custom-call(f32[128,128]{1,0:T(8,128)S(1)} %convolution_subtract_fusion), custom_call_target="Cholesky" | custom-call | tf_op jit(solution)/shard_map/cholesky/custom-call.1 | solution.py:126
  155.1 0.9 fusion.22
  156.1 0.9 convolution_add_fusion.5
  159.8 0.8 fusion.36
  (50 shorter events, 11.2 us)
Async XLA Ops:
  6.5 19.0 %copy-start = (bf16[1024,256]{1,0:T(8,128)(2,1)S(1)}, bf16[1024,256]{1,0:T(8,128)(2,1)}, u32[]{:S(2)}) copy-start(bf16[1024,256]{1,0:T(8,128)(2,1)} %param.14) | copy-start | bytes 1572868
  6.5 99.3 %all-gather.2.cloned.1.call-start = ((), (), s32[]{:S(2)}) async-start(), calls=%async_computation.2 | async-start | bytes 4227072 | tf_op jit(solution)/shard_map/all_gather | solution.py:19
  52.4 6.3 %copy-start.2 = (s32[3,3]{1,0:T(4,128)S(1)}, s32[3,3]{1,0:T(4,128)}, u32[]{:S(2)}) copy-start(s32[3,3]{1,0:T(4,128)} %param.9) | copy-start | bytes 112
  52.4 6.5 %copy-start.1 = (s32[128]{0:T(128)S(1)}, s32[128]{0:T(128)}, u32[]{:S(2)}) copy-start(s32[128]{0:T(128)} %param.12) | copy-start | bytes 1540
  52.4 7.4 %copy-start.3 = (s32[3]{0:T(128)S(1)}, s32[3]{0:T(128)}, u32[]{:S(2)}) copy-start(s32[3]{0:T(128)} %param.11) | copy-start | bytes 40
  133.5 8.5 %all-to-all-start.1 = ((f32[4,16,256]{2,1,0:T(8,128)}), f32[4,16,256]{2,1,0:T(8,128)S(1)}, u32[]{:S(2)}, u32[]{:S(2)}) async-start(f32[4,16,256]{2,1,0:T(8,128)} %bitcast.11), calls=%async_computation.1 | async-start | bytes 131072 | tf_op jit(solution)/shard_map/all_to_all | solution.py:30
Sparse Core Ops, SparseCore 0:
  16.5 89.3 all-gather.1

commit v12 on v11

--- a/solution.py
+++ b/solution.py
@@ -30,8 +30,8 @@
     my_rows = lax.all_to_all(pieces, "rep", 0, 0).sum(0)
     gram_c = jnp.dot(factor_c.T, factor_c, preferred_element_type=jnp.float32)
     normal_matrix = gram_b * gram_c
-    normal_inverse, my_rows = spd_inverse(normal_matrix, my_rows)
-    return jnp.dot(my_rows, normal_inverse, precision=lax.Precision.HIGHEST)
+    lower_inv, my_rows = spd_inverse(normal_matrix, my_rows)
+    return mm(mm(my_rows, lower_inv.T), lower_inv)
 
 
 def weigh_kernel(place_ref, scale_ref, whole_ref, *refs):
@@ -129,7 +129,7 @@
     inverse = jnp.concatenate(
         [jnp.concatenate([top_inverse, zeros], 1), jnp.concatenate([corner, bottom_inverse], 1)], 0
     )
-    return mm(inverse.T, inverse), carried
+    return inverse, carried
 
 
 def solution(mesh):

time: 168 us -> 168 us (level)
    dot_general x29 -> x30, matrix products: 9.2 us -> 9.86 us  [mm(): return jnp.dot(left, right, precision=lax.Precision.HIGHEST)]
where the time goes in v12:
time: 168 us
  waiting for transfers between devices  49.3 us (29%)
  local copies, waits for them, and re-layouts  29.5 us (18%)
  other arithmetic  27.7 us (16%)
  matrix products  22.8 us (14%)
  between operations  16.3 us (10%)
  blocking collectives  9.04 us (5%)
  Pallas kernels  8.71 us (5%)
  starting transfers between devices  4.81 us (3%)
    all_gather x1, waiting for transfers between devices, per_device(): whole_b = lax.all_gather(owned, 'tiles', axis=0, tiled=True)  45 us
    dot_general x3, local copies, waits for them, and re-layouts, per_device(): inner_sum = jnp.dot(flat_tile, c_block, precision=lax.Precision.HIGHEST)  16.9 us
    another operation x3, other arithmetic, spd_inverse(): lax.linalg.cholesky(top, symmetrize_input=False)  12.4 us
    another operation x3, other arithmetic, spd_inverse(): lax.linalg.cholesky(schur, symmetrize_input=False)  12.4 us
    dot_general x3, matrix products, per_device(): inner_sum = jnp.dot(flat_tile, c_block, precision=lax.Precision.HIGHEST)  11.7 us
    dot_general x30, matrix products, mm(): return jnp.dot(left, right, precision=lax.Precision.HIGHEST)  9.86 us
    all_to_all x1, blocking collectives, per_device(): owned = lax.all_to_all(copies, 'rep', 0, 0).reshape(-1, rank_cols)  9.04 us
    pallas_call x1, Pallas kernels, weighted_sum(): pl.pallas_call(weigh_kernel, grid_spec=grid_spec, out_shape=[jax.ShapeDty...  8.71 us
  transfers between devices with their start and end apart: 2, of which 2 were waited for; matrix products, arithmetic and copies ran while one was open for 25% of the time, Pallas kernels for 0%

profile of v12, /device:TPU:1, one launch (start us, length us, event | category | flops | bytes accessed | tf_op | source)
XLA Modules:
  0.0 168.2 jit_solution(17180753393982376486)
XLA Ops:
  7.3 9.0 %all_to_all.10 = bf16[4,16,256]{2,1,0:T(8,128)(2,1)} all-to-all(bf16[4,16,256]{2,1,0:T(8,128)(2,1)S(1)} %broadcast_in_dim.4), channel_id=1, replica_groups=mesh['tiles'=128,'rep'=4] {'rep'}, dimensions={0} | all-to-all | bytes 65536 | tf_op jit(solution)/shard_map/all_to_all | solution.py:18
  16.4 1.5 fusion.26
  19.8 3.7 %fusion.25 = (f32[1,64,4096]{2,1,0:T(8,128)}, f32[1,64,4096]{2,1,0:T(8,128)}, f32[1,64,4096]{2,1,0:T(8,128)}) fusion(f32[3,64,4096]{2,1,0:T(8,128)} %param.8), kind=kLoop, calls=%fused_computation.65 | loop fusion | bytes 6291456 | tf_op jit(solution)/shard_map/slice | solution.py:25
  23.5 2.0 %reshape_squeeze.11 = f32[4096,64]{1,0:T(8,128)S(1)} reshape(f32[1,64,4096]{2,1,0:T(8,128)} %get-tuple-element.14) | data formatting | bytes 2097152 | tf_op jit(solution)/shard_map/reshape;squeeze | solution.py:25
  25.5 3.9 %convolution_bitcast_fusion = f32[4096,256]{0,1:T(8,128)} fusion(f32[4096,64]{1,0:T(8,128)S(1)} %reshape_squeeze.11, bf16[1024,256]{1,0:T(8,128)(2,1)S(1)} %copy-done, s32[]{:T(128)S(6)} %select_n.30), kind=kOutput, calls=%fused_computation.1 | convolution fusion | flops 805306368 | bytes 6324228 | tf_op jit(solution)/shard_map/dot_general | solution.py:26
  29.4 5.6 %copy.20 = f32[4096,256]{1,0:T(8,128)} copy(f32[4096,256]{0,1:T(8,128)} %convolution_bitcast_fusion) | data formatting | bytes 8388608 | tf_op jit(solution)/shard_map/dot_general | solution.py:26
  35.0 2.0 %reshape_squeeze.9 = f32[4096,64]{1,0:T(8,128)S(1)} reshape(f32[1,64,4096]{2,1,0:T(8,128)} %get-tuple-element.15) | data formatting | bytes 2097152 | tf_op jit(solution)/shard_map/reshape;squeeze | solution.py:25
  37.1 3.9 %convolution_bitcast_fusion.2 = f32[4096,256]{0,1:T(8,128)} fusion(f32[4096,64]{1,0:T(8,128)S(1)} %reshape_squeeze.9, bf16[1024,256]{1,0:T(8,128)(2,1)S(1)} %copy-done, s32[]{:T(128)S(6)} %select_n.28), kind=kOutput, calls=%fused_computation.3 | convolution fusion | flops 805306368 | bytes 6324228 | tf_op jit(solution)/shard_map/dot_general | solution.py:26
  41.0 5.6 %copy.18 = f32[4096,256]{1,0:T(8,128)} copy(f32[4096,256]{0,1:T(8,128)} %convolution_bitcast_fusion.2) | data formatting | bytes 8388608 | tf_op jit(solution)/shard_map/dot_general | solution.py:26
  46.6 2.0 %reshape_squeeze.10 = f32[4096,64]{1,0:T(8,128)S(1)} reshape(f32[1,64,4096]{2,1,0:T(8,128)} %get-tuple-element.16) | data formatting | bytes 2097152 | tf_op jit(solution)/shard_map/reshape;squeeze | solution.py:25
  48.6 3.9 %convolution_bitcast_fusion.1 = f32[4096,256]{0,1:T(8,128)} fusion(f32[4096,64]{1,0:T(8,128)S(1)} %reshape_squeeze.10, bf16[1024,256]{1,0:T(8,128)(2,1)S(1)} %copy-done, s32[]{:T(128)S(6)} %select_n.29), kind=kOutput, calls=%fused_computation.2 | convolution fusion | flops 805306368 | bytes 6324228 | tf_op jit(solution)/shard_map/dot_general | solution.py:26
  52.4 5.7 %copy.19 = f32[4096,256]{1,0:T(8,128)} copy(f32[4096,256]{0,1:T(8,128)} %convolution_bitcast_fusion.1) | data formatting | bytes 8388608 | tf_op jit(solution)/shard_map/dot_general | solution.py:26
  60.8 45.0 %all-gather.2.cloned.1.call-done.whole_ref.refs_0_.refs_1_.refs_2_ = bf16[8192,256]{1,0:T(8,128)(2,1)} async-done(((bf16[64,256]{1,0:T(8,128)(2,1)}), bf16[8192,256]{1,0:T(8,128)(2,1)}) %all-gather.2.cloned.1.call-update) | async-done | bytes 4194320 | tf_op jit(solution)/shard_map/all_gather | solution.py:19
  105.9 8.7 %shard_map.73 = (f32[64,256]{1,0:T(8,128)}, f32[256,256]{1,0:T(8,128)}) custom-call(s32[3]{0:T(128)} %broadcast_select_fusion.place_ref, f32[3]{0:T(128)} %compare_select_fusion.1.scale_ref, bf16[8192,256]{1,0:T(8,128)(2,1)} %all-gather.2.cloned.1.call-done.whole_ref.refs_0_.refs_1_.refs_2_, ...), custom_call_target="tpu_custom_call" | custom-call | tf_op jit(solution)/shard_map/pallas_call | solution.py:88
  114.6 1.3 convolution_multiply_fusion
  115.9 11.7 %custom-call.4 = f32[128,128]{1,0:T(8,128)S(1)} custom-call(f32[128,128]{1,0:T(8,128)S(1)} %slice.46), custom_call_target="Cholesky" | custom-call | tf_op jit(solution)/shard_map/cholesky/custom-call.1 | solution.py:122
  129.0 0.9 fusion.23
  130.0 0.9 convolution_add_fusion.11
  133.5 4.8 %all-to-all-start.1 = ((f32[4,16,256]{2,1,0:T(8,128)}), f32[4,16,256]{2,1,0:T(8,128)S(1)}, u32[]{:S(2)}, u32[]{:S(2)}) async-start(f32[4,16,256]{2,1,0:T(8,128)} %bitcast.11), calls=%async_computation.1 | async-start | bytes 131072 | tf_op jit(solution)/shard_map/all_to_all | solution.py:30
  138.6 4.3 %all-to-all-done.1 = f32[4,16,256]{2,1,0:T(8,128)S(1)} async-done(((f32[4,16,256]{2,1,0:T(8,128)}), f32[4,16,256]{2,1,0:T(8,128)S(1)}, u32[]{:S(2)}, u32[]{:S(2)}) %all-to-all-start.1) | async-done | bytes 65568 | tf_op jit(solution)/shard_map/all_to_all | solution.py:30
  142.8 11.7 %custom-call.5 = f32[128,128]{1,0:T(8,128)S(1)} custom-call(f32[128,128]{1,0:T(8,128)S(1)} %convolution_subtract_fusion), custom_call_target="Cholesky" | custom-call | tf_op jit(solution)/shard_map/cholesky/custom-call.1 | solution.py:126
  156.0 0.9 fusion.24
  156.9 0.9 convolution_add_fusion.5
  160.4 0.9 fusion.2
  (50 shorter events, 11.0 us)
Async XLA Ops:
  6.5 19.0 %copy-start = (bf16[1024,256]{1,0:T(8,128)(2,1)S(1)}, bf16[1024,256]{1,0:T(8,128)(2,1)}, u32[]{:S(2)}) copy-start(bf16[1024,256]{1,0:T(8,128)(2,1)} %param.14) | copy-start | bytes 1572868
  6.5 99.3 %all-gather.2.cloned.1.call-start = ((), (), s32[]{:S(2)}) async-start(), calls=%async_computation.2 | async-start | bytes 4227072 | tf_op jit(solution)/shard_map/all_gather | solution.py:19
  52.4 6.3 %copy-start.2 = (s32[3,3]{1,0:T(4,128)S(1)}, s32[3,3]{1,0:T(4,128)}, u32[]{:S(2)}) copy-start(s32[3,3]{1,0:T(4,128)} %param.9) | copy-start | bytes 112
  52.4 6.5 %copy-start.1 = (s32[128]{0:T(128)S(1)}, s32[128]{0:T(128)}, u32[]{:S(2)}) copy-start(s32[128]{0:T(128)} %param.12) | copy-start | bytes 1540
  52.4 7.4 %copy-start.3 = (s32[3]{0:T(128)S(1)}, s32[3]{0:T(128)}, u32[]{:S(2)}) copy-start(s32[3]{0:T(128)} %param.11) | copy-start | bytes 40
  133.5 9.3 %all-to-all-start.1 = ((f32[4,16,256]{2,1,0:T(8,128)}), f32[4,16,256]{2,1,0:T(8,128)S(1)}, u32[]{:S(2)}, u32[]{:S(2)}) async-start(f32[4,16,256]{2,1,0:T(8,128)} %bitcast.11), calls=%async_computation.1 | async-start | bytes 131072 | tf_op jit(solution)/shard_map/all_to_all | solution.py:30
Sparse Core Ops, SparseCore 0:
  16.5 89.3 all-gather.1
